TPU v7x, 32 devices: a whole 2x2x4 slice. The times are simulated.
32 devices in a mesh: dp: 8 (over z, core), mp: 4 (over y, x).
Axes of the slice: x: 2, y: 2, z: 4, core: 2. Of those that a mesh axis runs over, the one named last changes fastest.
Arguments:
- tokens: bfloat16 [16384, 1280], P(('dp', 'mp')), may hold values from -6 to 6
- cotangent: bfloat16 [16384, 1280], P(('dp', 'mp')), may hold values from -6 to 6
- lengths: int32 [16], replicated, may hold values from 256 to 1024, as said below
- dealing: int32 [16], replicated, may hold values from 0 to 15, as said below
- gain_one: bfloat16 [1280], P('mp'), may hold values from 0.5 to 1.5
- gain_two: bfloat16 [1280], P('mp'), may hold values from 0.5 to 1.5
- attention_in: bfloat16 [1280, 3, 1280], P('mp'), may hold values from -0.15625 to 0.15625
- query_scale: float32 [80], replicated, may hold values from 0 to 1.5
- attention_out: bfloat16 [1280, 1280], P('mp'), may hold values from -1.25 to 1.25
- hidden_in: bfloat16 [1280, 1280], P('mp'), may hold values from -0.15625 to 0.15625
- hidden_out: bfloat16 [1280, 1280], P('mp'), may hold values from -0.3125 to 0.3125
Outputs:
- layer_out: bfloat16 [16384, 1280], P(('dp', 'mp'))
- tokens_grad: float32 [16384, 1280], P(('dp', 'mp'))
- series_cache: bfloat16 [2, 16384, 1280], P(None, 'dp', 'mp')
- gain_one_grad: float32 [1280], P('mp')
- gain_two_grad: float32 [1280], P('mp')
- attention_in_grad: float32 [1280, 3, 1280], P('mp')
- query_scale_grad: float32 [80], replicated
- attention_out_grad: float32 [1280, 1280], P('mp')
- hidden_in_grad: float32 [1280, 1280], P('mp')
- hidden_out_grad: float32 [1280, 1280], P('mp')
Inputs may be any that keep to these rules, and one draw needn't show every extreme that they name: `lengths`: series s belongs to group s // 2; every group has a series of exactly 1024 tokens. A permutation of the 16 places: series s goes to group dealing[s] // 2 at place dealing[s] % 2. The series of one group go to one group at most 1 at a time, and in every draw some group sends exactly 1 series to some group.
All inputs are finite; a program needn't handle non-finite values.
Results may differ from a plain program's by a relative error of at most 0.02.
Values may be sent and summed in bfloat16 or wider, within the bound.
No kernel may reach another device: no remote copies, remote signals or barrier semaphores. Data moves between devices by JAX's collectives and lax.ppermute only.
A program may use at most 256 MiB of HBM per device.

v0:
```python
import math

import jax
import jax.numpy as jnp
from jax import lax
from jax.sharding import PartitionSpec as P

D = 1280
NH = 16
HD = 80
LMAX = 1024
BLK = 128
QBLK = 512


epsilon = 1e-06
scale_base = 1.442695041
masked_score = -1e30


def lookup(values_table, positions):
    entries = jnp.arange(values_table.shape[0], dtype=jnp.int32)
    picked = jnp.where(positions[:, None] == entries[None, :], values_table[None, :], 0)
    return jnp.sum(picked, axis=1)


def packing(span_len, group_rows):
    blocks = (span_len + BLK - 1) // BLK
    block_ends = BLK * jnp.cumsum(blocks)
    starts = block_ends - BLK * blocks
    in_group = jnp.arange(group_rows, dtype=jnp.int32)
    series_at = jnp.sum((block_ends[None, :] <= in_group[:, None]).astype(jnp.int32), axis=1)
    capped = jnp.minimum(series_at, span_len.shape[0] - 1)
    offset = in_group - lookup(starts, capped)
    live_row = (series_at < span_len.shape[0]) & (offset < lookup(span_len, capped))
    return (starts, series_at, capped, offset, live_row)


def slot_table(slot_of, starts, span_len, slot_count):
    entries = jnp.arange(slot_count, dtype=jnp.int32)
    matched = slot_of[None, :] == entries[:, None]
    slot_first = jnp.sum(jnp.where(matched, starts[None, :], 0), axis=1)
    slot_length = jnp.sum(jnp.where(matched, span_len[None, :], 0), axis=1)
    return (slot_first, slot_length)


def series_maps(lengths, dealing, series_grp, group_rows, my_group):
    groups = lengths.shape[0] // series_grp
    capacity = (series_grp + groups - 1) // groups
    places = jnp.arange(series_grp, dtype=jnp.int32)
    target = dealing.reshape(groups, series_grp) // series_grp
    earlier = (target[:, :, None] == target[:, None, :]) & (
        places[None, None, :] < places[None, :, None]
    )
    rank_of = jnp.sum(earlier.astype(jnp.int32), axis=2)
    slot_of = (target * capacity + rank_of).reshape(-1)
    rank_flat = rank_of.reshape(-1)
    src_len = lax.dynamic_slice_in_dim(lengths, my_group * series_grp, series_grp)
    src_slot = lax.dynamic_slice_in_dim(slot_of, my_group * series_grp, series_grp)
    src_starts, src_at, src_capped, src_offset, src_live = packing(src_len, group_rows)
    dealt_places = jnp.arange(lengths.shape[0], dtype=jnp.int32)
    owner = jnp.sum(
        jnp.where(dealing[None, :] == dealt_places[:, None], dealt_places[None, :], 0), axis=1
    )
    my_series = lax.dynamic_slice_in_dim(owner, my_group * series_grp, series_grp)
    dst_len = lookup(lengths, my_series)
    dst_slot = my_series // series_grp * capacity + lookup(rank_flat, my_series)
    dst_starts, dst_at, dst_capped, dst_offset, dst_live = packing(dst_len, group_rows)
    slot_count = groups * capacity
    send_first, send_len = slot_table(src_slot, src_starts, src_len, slot_count)
    back_first, back_len = slot_table(dst_slot, dst_starts, dst_len, slot_count)
    src_index = lookup(src_slot, src_capped) * LMAX + src_offset
    dst_index = lookup(dst_slot, dst_capped) * LMAX + dst_offset
    key_live = jnp.where(dst_at < series_grp, dst_live, True)
    return (
        send_first,
        send_len,
        back_first,
        back_len,
        src_index,
        src_live,
        dst_index,
        dst_live,
        dst_at,
        key_live,
    )


def fill_slots(values, slot_first, slot_length):
    positions = jnp.arange(LMAX, dtype=jnp.int32)
    row_index = jnp.clip(slot_first[:, None] + positions[None, :], 0, values.shape[1] - 1).reshape(
        -1
    )
    inside = (positions[None, :] < slot_length[:, None]).reshape(-1)
    picked = jnp.take(values, row_index, axis=1)
    picked = jnp.where(inside[None, :, None], picked, jnp.zeros((), values.dtype))
    return picked.reshape(values.shape[0], slot_first.shape[0], LMAX, values.shape[2])


def place_rows(slots_in, row_index, live_row):
    flattened = slots_in.reshape(slots_in.shape[0], -1, slots_in.shape[3])
    picked = jnp.take(flattened, jnp.clip(row_index, 0, flattened.shape[1] - 1), axis=1)
    return jnp.where(live_row[None, :, None], picked, jnp.zeros((), flattened.dtype))


def unit_terms(unit_sides, other_sides):
    qkv_grad, att_rows, preact_grad, hidden = unit_sides
    normed_one, branch_grad, normed_two, feed_grad = other_sides
    qkv_part = jnp.einsum("cru,rd->ucd", qkv_grad, normed_one, preferred_element_type=jnp.float32)
    out_part = jnp.einsum("ru,rd->ud", att_rows, branch_grad, preferred_element_type=jnp.float32)
    in_part = jnp.einsum("ru,rd->ud", preact_grad, normed_two, preferred_element_type=jnp.float32)
    down_part = jnp.einsum("ru,rd->ud", hidden, feed_grad, preferred_element_type=jnp.float32)
    return jnp.concatenate(
        [qkv_part, out_part[:, None], in_part[:, None], down_part[:, None]], axis=1
    )


def per_device(
    tokens,
    cotangent,
    lengths,
    dealing,
    gain_one,
    gain_two,
    attention_in,
    query_scale,
    attention_out,
    hidden_in,
    hidden_out,
):
    gains_one, gains_two, qkv_all, out_all, in_all, down_all = (
        lax.all_gather(gain_one, "mp", axis=0, tiled=True),
        lax.all_gather(gain_two, "mp", axis=0, tiled=True),
        lax.all_gather(attention_in, "mp", axis=0, tiled=True),
        lax.all_gather(attention_out, "mp", axis=0, tiled=True),
        lax.all_gather(hidden_in, "mp", axis=0, tiled=True),
        lax.all_gather(hidden_out, "mp", axis=0, tiled=True),
    )
    row_count = tokens.shape[0]
    mp_count = lax.axis_size("mp")
    my_group = lax.axis_index("dp")
    my_part = lax.axis_index("mp")
    group_rows = row_count * mp_count
    series_grp = group_rows // LMAX
    heads_here = NH // mp_count
    width_here = heads_here * HD
    (
        send_first,
        send_len,
        back_first,
        back_len,
        src_index,
        src_live,
        dst_index,
        dst_live,
        segment,
        key_live,
    ) = series_maps(lengths, dealing, series_grp, group_rows, my_group)
    live_mine = lax.dynamic_slice_in_dim(src_live, my_part * row_count, row_count).astype(
        jnp.float32
    )[:, None]
    inputs = tokens.astype(jnp.float32)
    inv_one = lax.rsqrt(jnp.mean(inputs * inputs, axis=1, keepdims=True) + epsilon)
    gain_first = gains_one.astype(jnp.float32)
    normed_one = (inputs * inv_one * gain_first).astype(jnp.bfloat16)
    projected = jnp.einsum("rd,ucd->cru", normed_one, qkv_all, preferred_element_type=jnp.float32)
    dim_scale = scale_base / math.sqrt(HD) * jax.nn.softplus(query_scale)
    query_raw = projected[0].reshape(row_count, NH, HD)
    queries_out = (query_raw * dim_scale).reshape(row_count, D).astype(jnp.bfloat16)
    outgoing = jnp.stack(
        [queries_out, projected[1].astype(jnp.bfloat16), projected[2].astype(jnp.bfloat16)]
    )
    by_head = lax.all_to_all(outgoing, "mp", split_axis=2, concat_axis=1, tiled=True)
    incoming = lax.all_to_all(
        fill_slots(by_head, send_first, send_len), "dp", split_axis=1, concat_axis=1, tiled=True
    )
    dealt = place_rows(incoming, dst_index, dst_live)
    margin = LMAX - BLK
    window = margin + QBLK
    queries = dealt[0].reshape(group_rows, heads_here, HD)
    keys_pad = jnp.pad(dealt[1], ((margin, 0), (0, 0))).reshape(group_rows + margin, heads_here, HD)
    values_pad = jnp.pad(dealt[2], ((margin, 0), (0, 0))).reshape(
        group_rows + margin, heads_here, HD
    )
    segment_pad = jnp.concatenate([jnp.full((margin,), -1, jnp.int32), segment])
    live_pad = jnp.concatenate([jnp.zeros((margin,), jnp.bool_), key_live])
    block_starts = jnp.arange(group_rows // QBLK, dtype=jnp.int32) * QBLK
    query_pos = jnp.arange(QBLK, dtype=jnp.int32)
    key_pos = jnp.arange(window, dtype=jnp.int32) - margin

    def block_scores(block_start):
        query_block = lax.dynamic_slice_in_dim(queries, block_start, QBLK, 0)
        key_window = lax.dynamic_slice_in_dim(keys_pad, block_start, window, 0)
        value_window = lax.dynamic_slice_in_dim(values_pad, block_start, window, 0)
        seg_query = lax.dynamic_slice_in_dim(segment, block_start, QBLK, 0)
        seg_key = lax.dynamic_slice_in_dim(segment_pad, block_start, window, 0)
        live_key = lax.dynamic_slice_in_dim(live_pad, block_start, window, 0)
        allowed = (
            (seg_query[:, None] == seg_key[None, :])
            & (key_pos[None, :] <= query_pos[:, None])
            & live_key[None, :]
        )
        scores = jnp.einsum(
            "qhd,khd->hqk", query_block, key_window, preferred_element_type=jnp.float32
        )
        return (
            query_block,
            key_window,
            value_window,
            jnp.where(allowed[None], scores, masked_score),
        )

    def forward_block(carry, block_start):
        query_block, key_window, value_window, scores = block_scores(block_start)
        row_max = jnp.max(scores, axis=2, keepdims=True)
        exponent = jnp.exp(scores - row_max)
        row_total = jnp.sum(exponent, axis=2, keepdims=True)
        soft_weights = (exponent / row_total).astype(jnp.bfloat16)
        mixed = jnp.einsum(
            "hqk,khd->qhd", soft_weights, value_window, preferred_element_type=jnp.float32
        )
        log_total = (row_max + jnp.log(row_total))[:, :, 0]
        return (carry, (mixed.astype(jnp.bfloat16).reshape(QBLK, width_here), log_total))

    _, (mixed_blocks, log_totals) = lax.scan(forward_block, jnp.int32(0), block_starts)
    att_dealt = mixed_blocks.reshape(group_rows, width_here)
    returned = lax.all_to_all(
        fill_slots(att_dealt[None], back_first, back_len),
        "dp",
        split_axis=1,
        concat_axis=1,
        tiled=True,
    )
    att_group = place_rows(returned, src_index, src_live)[0]
    att_rows = lax.all_to_all(att_group, "mp", split_axis=0, concat_axis=1, tiled=True)
    branch = jnp.dot(att_rows, out_all, preferred_element_type=jnp.float32)
    first_sum = inputs + branch
    inv_two = lax.rsqrt(jnp.mean(first_sum * first_sum, axis=1, keepdims=True) + epsilon)
    gain_second = gains_two.astype(jnp.float32)
    normed_two = (first_sum * inv_two * gain_second).astype(jnp.bfloat16)
    preact = jnp.einsum("rd,fd->rf", normed_two, in_all, preferred_element_type=jnp.float32)
    hidden = jax.nn.silu(preact).astype(jnp.bfloat16)
    feed = jnp.dot(hidden, down_all, preferred_element_type=jnp.float32)
    layer_out = ((first_sum + feed) * live_mine).astype(jnp.bfloat16)
    out_grad = cotangent.astype(jnp.float32) * live_mine
    feed_grad = out_grad.astype(jnp.bfloat16)
    hidden_grad = jnp.einsum("rd,fd->rf", feed_grad, down_all, preferred_element_type=jnp.float32)
    gate_sig = jax.nn.sigmoid(preact)
    preact_grad = (hidden_grad * gate_sig * (1.0 + preact * (1.0 - gate_sig))).astype(jnp.bfloat16)
    normed_two_grad = jnp.dot(preact_grad, in_all, preferred_element_type=jnp.float32)
    scaled_two = gain_second * normed_two_grad
    first_grad = (
        out_grad
        + inv_two * scaled_two
        - first_sum * inv_two**3 * jnp.mean(scaled_two * first_sum, axis=1, keepdims=True)
    )
    branch_grad = first_grad.astype(jnp.bfloat16)
    att_rows_grad = jnp.einsum(
        "rd,ud->ru", branch_grad, out_all, preferred_element_type=jnp.float32
    ).astype(jnp.bfloat16)
    grad_group = lax.all_to_all(att_rows_grad, "mp", split_axis=1, concat_axis=0, tiled=True)
    grad_incoming = lax.all_to_all(
        fill_slots(grad_group[None], send_first, send_len),
        "dp",
        split_axis=1,
        concat_axis=1,
        tiled=True,
    )
    grad_dealt = place_rows(grad_incoming, dst_index, dst_live)[0].reshape(
        group_rows, heads_here, HD
    )

    def backward_block(carry, item):
        block_start, log_total = item
        key_grads, value_grads = carry
        query_block, key_window, value_window, scores = block_scores(block_start)
        probs_full = jnp.exp(scores - log_total[:, :, None])
        grad_block = lax.dynamic_slice_in_dim(grad_dealt, block_start, QBLK, 0)
        weight_grad = jnp.einsum(
            "qhd,khd->hqk", grad_block, value_window, preferred_element_type=jnp.float32
        )
        row_dot = jnp.sum(probs_full * weight_grad, axis=2, keepdims=True)
        score_grad = (probs_full * (weight_grad - row_dot)).astype(jnp.bfloat16)
        query_grad = jnp.einsum(
            "hqk,khd->qhd", score_grad, key_window, preferred_element_type=jnp.float32
        )
        key_part = jnp.einsum(
            "hqk,qhd->khd", score_grad, query_block, preferred_element_type=jnp.float32
        )
        value_part = jnp.einsum(
            "hqk,qhd->khd",
            probs_full.astype(jnp.bfloat16),
            grad_block,
            preferred_element_type=jnp.float32,
        )
        key_grads = lax.dynamic_update_slice_in_dim(
            key_grads,
            lax.dynamic_slice_in_dim(key_grads, block_start, window, 0) + key_part,
            block_start,
            0,
        )
        value_grads = lax.dynamic_update_slice_in_dim(
            value_grads,
            lax.dynamic_slice_in_dim(value_grads, block_start, window, 0) + value_part,
            block_start,
            0,
        )
        return ((key_grads, value_grads), query_grad.astype(jnp.bfloat16).reshape(QBLK, width_here))

    empty = jnp.zeros((group_rows + margin, heads_here, HD), jnp.float32)
    (key_grads, value_grads), query_blocks = lax.scan(
        backward_block, (empty, empty), (block_starts, log_totals)
    )
    grad_stack = jnp.stack(
        [
            query_blocks.reshape(group_rows, width_here),
            key_grads[margin:].reshape(group_rows, width_here).astype(jnp.bfloat16),
            value_grads[margin:].reshape(group_rows, width_here).astype(jnp.bfloat16),
        ]
    )
    grad_returned = lax.all_to_all(
        fill_slots(grad_stack, back_first, back_len), "dp", split_axis=1, concat_axis=1, tiled=True
    )
    grad_rows_group = place_rows(grad_returned, src_index, src_live)
    proj_grad = lax.all_to_all(grad_rows_group, "mp", split_axis=1, concat_axis=2, tiled=True)
    query_scaled_grad = proj_grad[0].astype(jnp.float32).reshape(row_count, NH, HD)
    scale_part = (
        jnp.sum(query_scaled_grad * query_raw, axis=(0, 1))
        * (scale_base / math.sqrt(HD))
        * jax.nn.sigmoid(query_scale)
    )
    query_grad_rows = (query_scaled_grad * dim_scale).reshape(row_count, D).astype(jnp.bfloat16)
    qkv_grad = jnp.stack([query_grad_rows, proj_grad[1], proj_grad[2]])
    normed_one_grad = jnp.einsum(
        "cru,ucd->rd", qkv_grad, qkv_all, preferred_element_type=jnp.float32
    )
    scaled_one = gain_first * normed_one_grad
    tokens_grad = (
        first_grad
        + inv_one * scaled_one
        - inputs * inv_one**3 * jnp.mean(scaled_one * inputs, axis=1, keepdims=True)
    )
    gain_one_part = jnp.sum(normed_one_grad * inputs * inv_one, axis=0)
    gain_two_part = jnp.sum(normed_two_grad * first_sum * inv_two, axis=0)
    gain_one_sum, gain_two_sum, query_scale_grad = lax.psum(
        (gain_one_part, gain_two_part, scale_part), ("dp", "mp")
    )
    shard_width = D // mp_count
    gain_one_grad = lax.dynamic_slice_in_dim(gain_one_sum, my_part * shard_width, shard_width)
    gain_two_grad = lax.dynamic_slice_in_dim(gain_two_sum, my_part * shard_width, shard_width)
    unit_sides = (qkv_grad, att_rows, preact_grad, hidden)
    other_sides = (normed_one, branch_grad, normed_two, feed_grad)
    shares = lax.psum_scatter(
        unit_terms(unit_sides, other_sides).astype(jnp.bfloat16),
        "mp",
        scatter_dimension=0,
        tiled=True,
    )
    totals = lax.psum(shares, "dp").astype(jnp.float32)
    return (
        layer_out,
        tokens_grad,
        dealt[1:],
        gain_one_grad,
        gain_two_grad,
        totals[:, 0:3],
        query_scale_grad,
        totals[:, 3],
        totals[:, 4],
        totals[:, 5],
    )


def solution(mesh):
    placed = (
        P(("dp", "mp"), None),
        P(("dp", "mp"), None),
        P(),
        P(),
        P("mp"),
        P("mp"),
        P("mp", None, None),
        P(),
        P("mp", None),
        P("mp", None),
        P("mp", None),
    )
    return jax.shard_map(
        per_device,
        mesh=mesh,
        in_specs=placed,
        out_specs=(
            P(("dp", "mp"), None),
            P(("dp", "mp"), None),
            P(None, "dp", "mp"),
            P("mp"),
            P("mp"),
            P("mp", None, None),
            P(),
            P("mp", None),
            P("mp", None),
            P("mp", None),
        ),
        check_vma=False,
    )
```

profile of v0, /device:TPU:0, one launch (start us, length us, event | category | flops | bytes accessed | tf_op | source)
XLA Modules:
  0.0 2723.5 jit_solution(17013730551581716672)
XLA Ops:
  25.4 86.7 %all-gather.5.cloned.1.call-done = bf16[1280,3,1280]{2,0,1:T(8,128)(2,1)} async-done(((bf16[320,3,1280]{2,0,1:T(8,128)(2,1)}), bf16[1280,3,1280]{2,0,1:T(8,128)(2,1)}) %all-gather.5.cloned.1.call-update) | async-done | bytes 9830416 | tf_op jit(solution)/shard_map/all_gather | solution.py:134
  141.5 57.1 %all-to-all-done = bf16[3,512,1280]{1,0,2:T(4,128)(2,1)} async-done(((bf16[3,512,1280]{1,0,2:T(4,128)(2,1)}), bf16[3,512,1280]{1,0,2:T(4,128)(2,1)}, u32[]{:S(2)}, u32[]{:S(2)}) %all-to-all-start) | async-done | bytes 3932192 | tf_op jit(solution)/shard_map/all_to_all | solution.py:173
  214.1 79.1 %gather_fusion = bf16[8192,3,320]{2,1,0:T(4,128)(2,1)} fusion(bf16[3,2048,320]{2,0,1:T(4,128)(2,1)} %bitcast.197, s32[8192]{0:T(1024)S(1)} %fusion.80), kind=kCustom, calls=%fused_computation.clone | custom fusion | bytes 31490048 | tf_op jit(solution)/shard_map/jit(_take)/gather | solution.py:95
  293.2 44.5 %bitcast_select_fusion.1 = bf16[3,8192,320]{2,0,1:T(4,128)(2,1)} fusion(bf16[8192,3,320]{2,1,0:T(4,128)(2,1)} %gather_fusion, pred[8192]{0:T(1024)(128)(4,1)S(1)} %compare_and_fusion.1, pred[8192]{0:T(1024)(128)(4,1)S(1)} %bitcast.224), kind=kLoop, calls=%fused_computation.66 | loop fusion | flops 15728640 | bytes 31473664 | tf_op jit(solution)/shard_map/jit(_where)/select_n | solution.py:96
  337.7 36.1 %copy.139 = bf16[3,8,1024,320]{2,3,0,1:T(8,128)(2,1)} copy(bf16[3,8,1024,320]{3,0,2,1:T(4,128)(2,1)} %bitcast.196) | data formatting | bytes 31457280 | tf_op jit(solution)/shard_map/reshape | solution.py:97
  382.8 337.8 %all-to-all-done.1 = bf16[3,8,1024,320]{2,3,0,1:T(8,128)(2,1)} async-done(((bf16[3,8,1024,320]{2,3,0,1:T(8,128)(2,1)}), bf16[3,8,1024,320]{2,3,0,1:T(8,128)(2,1)}, u32[]{:S(2)}, u32[]{:S(2)}) %all-to-all-start.1) | async-done | bytes 15728672 | tf_op jit(solution)/shard_map/all_to_all | solution.py:174
  720.7 36.9 %copy.140 = bf16[3,8,1024,320]{3,0,2,1:T(4,128)(2,1)} copy(bf16[3,8,1024,320]{2,3,0,1:T(8,128)(2,1)} %all-to-all-done.1) | data formatting | bytes 31457280 | tf_op jit(solution)/shard_map/all_to_all | solution.py:174
  757.6 27.6 %gather_fusion.1 = bf16[2048,3,320]{2,1,0:T(4,128)(2,1)} fusion(bf16[3,8192,320]{2,0,1:T(4,128)(2,1)} %bitcast.202, s32[2048]{0:T(1024)S(1)} %broadcast_clamp_fusion.1), kind=kCustom, calls=%fused_computation.1.clone | custom fusion | bytes 7872512 | tf_op jit(solution)/shard_map/jit(_take)/gather | solution.py:102
  832.7 62.7 %while.28 = (s32[]{:T(128)}, bf16[4,512,320]{1,2,0:T(8,128)(2,1)S(1)}, f32[4,4,512]{2,1,0:T(4,128)S(1)}, s32[4]{0:T(128)S(1)}, bf16[2944,4,80]{0,2,1:T(8,128)(2,...) while((s32[]{:T(128)}, ...), condition=%wide.region_20.23_spmd.clone, body=%wide.region_17.22_spmd.clone.sunk | while | flops 951745920 | bytes 40703860 | solution.py:225
  897.5 33.1 %gather_fusion.2 = bf16[8192,320]{1,0:T(8,128)(2,1)} fusion(bf16[2048,320]{1,0:T(8,128)(2,1)S(1)} %bitcast.194, s32[8192]{0:T(1024)S(1)} %fusion.81), kind=kCustom, calls=%fused_computation.2.clone | custom fusion | bytes 10518528 | tf_op jit(solution)/shard_map/jit(_take)/gather | solution.py:95
  953.1 114.8 %all-to-all-done.2 = bf16[1,8,1024,320]{2,3,0,1:T(8,128)(2,1)} async-done(((bf16[1,8,1024,320]{2,3,0,1:T(8,128)(2,1)}), bf16[1,8,1024,320]{2,3,0,1:T(8,128)(2,1)}, u32[]{:S(2)}, u32[]{:S(2)}) %all-to-all-start.2) | async-done | bytes 5242912 | tf_op jit(solution)/shard_map/all_to_all | solution.py:227
  1164.8 33.1 %gather_fusion.4 = bf16[8192,320]{1,0:T(8,128)(2,1)} fusion(bf16[2048,320]{1,0:T(8,128)(2,1)S(1)} %bitcast.193, s32[8192]{0:T(1024)S(1)} %copy-done.23), kind=kCustom, calls=%fused_computation.6.clone | custom fusion | bytes 10518528 | tf_op jit(solution)/shard_map/jit(_take)/gather | solution.py:95
  1218.6 116.4 %all-to-all-done.5 = bf16[1,8,1024,320]{2,3,0,1:T(8,128)(2,1)} async-done(((bf16[1,8,1024,320]{2,3,0,1:T(8,128)(2,1)}), bf16[1,8,1024,320]{2,3,0,1:T(8,128)(2,1)}, u32[]{:S(2)}, u32[]{:S(2)}) %all-to-all-start.5) | async-done | bytes 5242912 | tf_op jit(solution)/shard_map/all_to_all | solution.py:262
  1362.4 236.7 %while.29 = (s32[]{:T(128)}, f32[2944,4,80]{0,2,1:T(8,128)}, f32[2944,4,80]{0,2,1:T(8,128)}, bf16[4,512,320]{1,2,0:T(8,128)(2,1)}, s32[4]{0:T(128)S(1)}, /*index...) while((s32[]{:T(128)}, f32[2944,4,80]{0,2,1:T(8,128)}, ...), condition=%wide.region_27.32_spmd.clone, body=%wide.region_25.31_spmd.clone.sunk | while | flops 2345418240 | bytes 192526352 | solution.py:311
  1647.8 79.1 %gather_fusion.6 = bf16[8192,3,320]{2,1,0:T(4,128)(2,1)} fusion(bf16[3,2048,320]{2,0,1:T(4,128)(2,1)} %pad_maximum_fusion.1, s32[8192]{0:T(1024)S(1)} %copy-done.21), kind=kCustom, calls=%fused_computation.4.clone | custom fusion | bytes 31490048 | tf_op jit(solution)/shard_map/jit(_take)/gather | solution.py:95
  1727.0 44.5 %bitcast_select_fusion = bf16[3,8192,320]{2,0,1:T(4,128)(2,1)} fusion(bf16[8192,3,320]{2,1,0:T(4,128)(2,1)} %gather_fusion.6, pred[8192]{0:T(1024)(128)(4,1)S(1)} %copy-done.25, pred[8192]{0:T(1024)(128)(4,1)S(1)} %bitcast.223), kind=kLoop, calls=%fused_computation.65 | loop fusion | flops 15728640 | bytes 31473664 | tf_op jit(solution)/shard_map/jit(_where)/select_n | solution.py:96
  1771.5 36.1 %copy.157 = bf16[3,8,1024,320]{2,3,0,1:T(8,128)(2,1)} copy(bf16[3,8,1024,320]{3,0,2,1:T(4,128)(2,1)} %bitcast.195) | data formatting | bytes 31457280 | tf_op jit(solution)/shard_map/reshape | solution.py:97
  1807.6 348.5 %all_to_all.89 = bf16[3,8,1024,320]{2,3,0,1:T(8,128)(2,1)} all-to-all(bf16[3,8,1024,320]{2,3,0,1:T(8,128)(2,1)} %copy.157), channel_id=1, replica_groups=mesh['dp'=8,'mp'=4] {'dp'}, dimensions={1} | all-to-all | bytes 31457280 | tf_op jit(solution)/shard_map/all_to_all | solution.py:321
  2156.2 36.7 %copy.158 = bf16[3,8,1024,320]{3,0,2,1:T(4,128)(2,1)} copy(bf16[3,8,1024,320]{2,3,0,1:T(8,128)(2,1)} %all_to_all.89) | data formatting | bytes 31457280 | tf_op jit(solution)/shard_map/all_to_all | solution.py:321
  2192.8 27.6 %gather_fusion.7 = bf16[2048,3,320]{2,1,0:T(4,128)(2,1)} fusion(bf16[3,8192,320]{2,0,1:T(4,128)(2,1)} %bitcast.201, s32[2048]{0:T(1024)S(1)} %copy-done.37), kind=kCustom, calls=%fused_computation.5.clone | custom fusion | bytes 7872512 | tf_op jit(solution)/shard_map/jit(_take)/gather | solution.py:102
  2251.8 56.2 %all-to-all-done.7 = bf16[3,2048,320]{2,0,1:T(4,128)(2,1)} async-done(((bf16[3,2048,320]{2,0,1:T(4,128)(2,1)}), bf16[3,2048,320]{2,0,1:T(4,128)(2,1)}, u32[]{:S(2)}, u32[]{:S(2)}) %all-to-all-start.7) | async-done | bytes 3932192 | tf_op jit(solution)/shard_map/all_to_all | solution.py:325
  2398.3 155.3 %reduce-scatter.4.cloned.1.call-done = bf16[320,7680]{1,0:T(8,128)(2,1)} async-done(((bf16[1280,7680]{1,0:T(8,128)(2,1)}), bf16[320,7680]{1,0:T(8,128)(2,1)}) %reduce-scatter.4.cloned.1.call-update) | async-done | bytes 4915216
  2574.6 40.6 %all-reduce.6 = (f32[1280]{0:T(1024)S(1)}, f32[1280]{0:T(1024)S(1)}, f32[80]{0:T(128)}) all-reduce(f32[1280]{0:T(1024)S(1)} %get-tuple-element.301, f32[1280]{0:T(1024)S(1)} %copy-done.54, f32[80]{0:T(128)S(1)} %divide_multiply_fusion), channel_id=1, replica_groups=mesh['dp'=8,'mp'=4] {'dp','mp'}, use_global_device_ids=true, to_apply=%region_30.35 | all-reduce | flops 2640 | bytes 21120 | tf_op jit(solution)/shard_map/psum | solution.py:345
  2621.3 70.1 %all-reduce.10.cloned.1.call-done = bf16[320,6,1280]{0,2,1:T(8,128)(2,1)} async-done(((bf16[320,6,1280]{0,2,1:T(8,128)(2,1)}), bf16[320,6,1280]{0,2,1:T(8,128)(2,1)}) %all-reduce.10.cloned.1.call-update) | async-done | bytes 4915216 | tf_op jit(solution)/shard_map/psum | solution.py:359
  (460 shorter events, 782.6 us)
Async XLA Ops:
  7.2 104.9 %all-gather.5.cloned.1.call-start = ((), (), s32[]{:S(2)}) async-start(), calls=%async_computation.9 | async-start | bytes 12288000 | tf_op jit(solution)/shard_map/all_gather | solution.py:134
  23.7 96.1 %copy-start.40 = (f32[1280]{0:T(1024)}, f32[1280]{0:T(1024)S(1)}, u32[]{:S(2)}) copy-start(f32[1280]{0:T(1024)S(1)} %convert_element_type.139) | copy-start | bytes 15364
  24.5 95.6 %copy-start.28 = (f32[1280]{0:T(1024)}, f32[1280]{0:T(1024)S(1)}, u32[]{:S(2)}) copy-start(f32[1280]{0:T(1024)S(1)} %mul.263) | copy-start | bytes 15364
  134.6 63.9 %all-to-all-start = ((bf16[3,512,1280]{1,0,2:T(4,128)(2,1)}), bf16[3,512,1280]{1,0,2:T(4,128)(2,1)}, u32[]{:S(2)}, u32[]{:S(2)}) async-start(bf16[3,512,1280]{1,0,2:T(4,128)(2,1)} %copy.135), calls=%async_computation | async-start | bytes 10485760 | tf_op jit(solution)/shard_map/all_to_all | solution.py:173
  141.3 151.9 %copy-start.32 = (pred[1,8,8,128]{3,1,2,0:T(8,128)(4,1)}, pred[1,8,8,128]{3,1,2,0:T(8,128)(4,1)S(1)}, u32[]{:S(2)}) copy-start(pred[1,8,8,128]{3,1,2,0:T(8,128)(4,1)S(1)} %copy.202) | copy-start | bytes 24580
  141.5 151.7 %copy-start.26 = (pred[8192]{0:T(1024)(128)(4,1)}, pred[8192]{0:T(1024)(128)(4,1)S(1)}, u32[]{:S(2)}) copy-start(pred[8192]{0:T(1024)(128)(4,1)S(1)} %compare_and_fusion.1) | copy-start | bytes 24580
  373.8 346.8 %all-to-all-start.1 = ((bf16[3,8,1024,320]{2,3,0,1:T(8,128)(2,1)}), bf16[3,8,1024,320]{2,3,0,1:T(8,128)(2,1)}, u32[]{:S(2)}, u32[]{:S(2)}) async-start(bf16[3,8,1024,320]{2,3,0,1:T(8,128)(2,1)} %copy.139), calls=%async_computation.1 | async-start | bytes 31457280 | tf_op jit(solution)/shard_map/all_to_all | solution.py:174
  379.5 724.1 %all-gather.7.cloned.1.call-start = ((), (), s32[]{:S(2)}) async-start(), calls=%async_computation.10 | async-start | bytes 4096000 | tf_op jit(solution)/shard_map/all_gather | solution.py:135
  382.0 403.2 %copy-start.44 = (pred[2048]{0:T(1024)(128)(4,1)}, pred[2048]{0:T(1024)(128)(4,1)S(1)}, u32[]{:S(2)}) copy-start(pred[2048]{0:T(1024)(128)(4,1)S(1)} %get-tuple-element.367) | copy-start | bytes 6148
  382.1 403.2 %copy-start.46 = (pred[2048]{0:T(1024)(128)(4,1)}, pred[2048]{0:T(1024)(128)(4,1)S(1)}, u32[]{:S(2)}) copy-start(pred[2048]{0:T(1024)(128)(4,1)S(1)} %get-tuple-element.387) | copy-start | bytes 6148
  382.1 375.5 %copy-start.34 = (s32[2048]{0:T(1024)}, s32[2048]{0:T(1024)S(1)}, u32[]{:S(2)}) copy-start(s32[2048]{0:T(1024)S(1)} %broadcast_clamp_fusion.1) | copy-start | bytes 24580
  382.8 514.7 %copy-start.20 = (s32[8192]{0:T(1024)}, s32[8192]{0:T(1024)S(1)}, u32[]{:S(2)}) copy-start(s32[8192]{0:T(1024)S(1)} %fusion.81) | copy-start | bytes 98308
  946.6 121.3 %all-to-all-start.2 = ((bf16[1,8,1024,320]{2,3,0,1:T(8,128)(2,1)}), bf16[1,8,1024,320]{2,3,0,1:T(8,128)(2,1)}, u32[]{:S(2)}, u32[]{:S(2)}) async-start(bf16[1,8,1024,320]{2,3,0,1:T(8,128)(2,1)} %copy.145), calls=%async_computation.2 | async-start | bytes 10485760 | tf_op jit(solution)/shard_map/all_to_all | solution.py:227
  951.4 174.1 %all-gather.9.cloned.1.call-start = ((), (), s32[]{:S(2)}) async-start(), calls=%async_computation.11 | async-start | bytes 4096000 | tf_op jit(solution)/shard_map/all_gather | solution.py:136
  952.2 179.6 %all-gather.11.cloned.1.call-start = ((), (), s32[]{:S(2)}) async-start(), calls=%async_computation.12 | async-start | bytes 4096000 | tf_op jit(solution)/shard_map/all_gather | solution.py:137
  953.0 122.9 %copy-start.36 = (s32[2048]{0:T(1024)}, s32[2048]{0:T(1024)S(1)}, u32[]{:S(2)}) copy-start(s32[2048]{0:T(1024)S(1)} %broadcast_clamp_fusion) | copy-start | bytes 24580
  953.1 133.7 %copy-start.48 = (pred[2048]{0:T(1024)(128)(4,1)}, pred[2048]{0:T(1024)(128)(4,1)S(1)}, u32[]{:S(2)}) copy-start(pred[2048]{0:T(1024)(128)(4,1)S(1)} %get-tuple-element.386) | copy-start | bytes 6148
  953.1 150.5 %copy-start.42 = (pred[2048]{0:T(1024)(128)(4,1)}, pred[2048]{0:T(1024)(128)(4,1)S(1)}, u32[]{:S(2)}) copy-start(pred[2048]{0:T(1024)(128)(4,1)S(1)} %get-tuple-element.385) | copy-start | bytes 6148
  1089.9 29.7 %all-to-all-start.3 = ((bf16[4,512,320]{1,2,0:T(8,128)(2,1)}), bf16[4,512,320]{1,2,0:T(8,128)(2,1)S(1)}, u32[]{:S(2)}, u32[]{:S(2)}) async-start(bf16[4,512,320]{1,2,0:T(8,128)(2,1)} %copy.147), calls=%async_computation.3 | async-start | bytes 2621440 | tf_op jit(solution)/shard_map/all_to_all | solution.py:235
  1213.9 121.1 %all-to-all-start.5 = ((bf16[1,8,1024,320]{2,3,0,1:T(8,128)(2,1)}), bf16[1,8,1024,320]{2,3,0,1:T(8,128)(2,1)}, u32[]{:S(2)}, u32[]{:S(2)}) async-start(bf16[1,8,1024,320]{2,3,0,1:T(8,128)(2,1)} %copy.150), calls=%async_computation.5 | async-start | bytes 10485760 | tf_op jit(solution)/shard_map/all_to_all | solution.py:262
  1218.5 124.6 %copy-start.35 = (s32[2048]{0:T(1024)S(1)}, s32[2048]{0:T(1024)}, u32[]{:S(2)}) copy-start(s32[2048]{0:T(1024)} %copy-done.34) | copy-start | bytes 24580
  2232.9 75.1 %all-to-all-start.7 = ((bf16[3,2048,320]{2,0,1:T(4,128)(2,1)}), bf16[3,2048,320]{2,0,1:T(4,128)(2,1)}, u32[]{:S(2)}, u32[]{:S(2)}) async-start(bf16[3,2048,320]{2,0,1:T(4,128)(2,1)} %bitcast_select_fusion.2), calls=%async_computation.7 | async-start | bytes 12582912 | tf_op jit(solution)/shard_map/all_to_all | solution.py:325
  2238.2 315.3 %reduce-scatter.4.cloned.1.call-start = ((), (), s32[]{:S(2)}) async-start(), calls=%async_computation.14 | async-start | bytes 24576000
  2377.8 313.6 %all-reduce.10.cloned.1.call-start = ((), (), s32[]{:S(2)}) async-start(), calls=%async_computation.13 | async-start | bytes 11796480 | tf_op jit(solution)/shard_map/psum | solution.py:359
  (80 other events, 1147.0 us)
Sparse Core Ops, SparseCore 0:
  9.8 102.1 all-gather.4
  382.2 45.3 all-gather.6
  954.1 45.3 all-gather.8
  1001.1 44.9 all-gather.10
  2377.9 175.6 reduce-scatter.3
  2561.7 129.6 all-reduce.9
where the time goes:
time: 2740 us; the launch traced here: 2720 us
  waiting for transfers between devices  1010 us (37%)
  local copies, waits for them, and re-layouts  791 us (29%)
  blocking collectives  420 us (15%)
  other arithmetic  217 us (8%)
  matrix products  199 us (7%)
  starting transfers between devices  39.6 us (1%)
    all_to_all x1, blocking collectives, per_device(): lax.all_to_all(fill_slots(grad_stack, back_first, back_len), 'dp', split_...  349 us
    all_to_all x1, waiting for transfers between devices, per_device(): lax.all_to_all(fill_slots(by_head, send_first, send_len), 'dp', split_axi...  338 us
    gather x4, local copies, waits for them, and re-layouts, fill_slots(): picked = jnp.take(values, row_index, axis=1)  225 us
    unnamed x7, waiting for transfers between devices  158 us
    all_to_all x1, waiting for transfers between devices, per_device(): lax.all_to_all(fill_slots(grad_group[None], send_first, send_len), 'dp',...  116 us
    all_to_all x1, waiting for transfers between devices, per_device(): lax.all_to_all(fill_slots(att_dealt[None], back_first, back_len), 'dp', s...  115 us
    select_n x4, other arithmetic, fill_slots(): jnp.where(inside[None, :, None], picked, jnp.zeros((), values.dtype))  105 us
    reshape x4, local copies, waits for them, and re-layouts, fill_slots(): picked.reshape(values.shape[0], slot_first.shape[0], LMAX, values.shape[2])  88.5 us
  transfers between devices with their start and end apart: 12, of which 9 were waited for; matrix products, arithmetic and copies ran while one was open for 11% of the time, Pallas kernels for 0%

commit v1 on v0

--- a/solution.py
+++ b/solution.py
@@ -128,10 +128,9 @@
     hidden_in,
     hidden_out,
 ):
-    gains_one, gains_two, qkv_all, out_all, in_all, down_all = (
+    gains_one, gains_two, out_all, in_all, down_all = (
         lax.all_gather(gain_one, "mp", axis=0, tiled=True),
         lax.all_gather(gain_two, "mp", axis=0, tiled=True),
-        lax.all_gather(attention_in, "mp", axis=0, tiled=True),
         lax.all_gather(attention_out, "mp", axis=0, tiled=True),
         lax.all_gather(hidden_in, "mp", axis=0, tiled=True),
         lax.all_gather(hidden_out, "mp", axis=0, tiled=True),
@@ -153,9 +152,13 @@
         src_live,
         dst_index,
         dst_live,
-        segment,
-        key_live,
+        dst_at,
+        dst_key_live,
     ) = series_maps(lengths, dealing, series_grp, group_rows, my_group)
+    src_len = lax.dynamic_slice_in_dim(lengths, my_group * series_grp, series_grp)
+    _, segment, _, _, _ = packing(src_len, group_rows)
+    key_live = jnp.where(segment < series_grp, src_live, True)
+    group_live = src_live.astype(jnp.float32)[:, None]
     live_mine = lax.dynamic_slice_in_dim(src_live, my_part * row_count, row_count).astype(
         jnp.float32
     )[:, None]
@@ -163,23 +166,26 @@
     inv_one = lax.rsqrt(jnp.mean(inputs * inputs, axis=1, keepdims=True) + epsilon)
     gain_first = gains_one.astype(jnp.float32)
     normed_one = (inputs * inv_one * gain_first).astype(jnp.bfloat16)
-    projected = jnp.einsum("rd,ucd->cru", normed_one, qkv_all, preferred_element_type=jnp.float32)
+    normed_group = lax.all_gather(normed_one, "mp", axis=0, tiled=True)
+    projected = jnp.einsum(
+        "rd,ucd->cru", normed_group, attention_in, preferred_element_type=jnp.float32
+    )
     dim_scale = scale_base / math.sqrt(HD) * jax.nn.softplus(query_scale)
-    query_raw = projected[0].reshape(row_count, NH, HD)
-    queries_out = (query_raw * dim_scale).reshape(row_count, D).astype(jnp.bfloat16)
-    outgoing = jnp.stack(
-        [queries_out, projected[1].astype(jnp.bfloat16), projected[2].astype(jnp.bfloat16)]
-    )
-    by_head = lax.all_to_all(outgoing, "mp", split_axis=2, concat_axis=1, tiled=True)
+    query_raw = projected[0].reshape(group_rows, heads_here, HD)
+    queries = (query_raw * dim_scale).astype(jnp.bfloat16)
+    keys_group = projected[1].astype(jnp.bfloat16)
+    values_group = projected[2].astype(jnp.bfloat16)
+    kv_group = jnp.stack([keys_group, values_group])
     incoming = lax.all_to_all(
-        fill_slots(by_head, send_first, send_len), "dp", split_axis=1, concat_axis=1, tiled=True
-    )
-    dealt = place_rows(incoming, dst_index, dst_live)
+        fill_slots(kv_group, send_first, send_len), "dp", split_axis=1, concat_axis=1, tiled=True
+    )
+    cache = place_rows(incoming, dst_index, dst_live)
     margin = LMAX - BLK
     window = margin + QBLK
-    queries = dealt[0].reshape(group_rows, heads_here, HD)
-    keys_pad = jnp.pad(dealt[1], ((margin, 0), (0, 0))).reshape(group_rows + margin, heads_here, HD)
-    values_pad = jnp.pad(dealt[2], ((margin, 0), (0, 0))).reshape(
+    keys_pad = jnp.pad(keys_group, ((margin, 0), (0, 0))).reshape(
+        group_rows + margin, heads_here, HD
+    )
+    values_pad = jnp.pad(values_group, ((margin, 0), (0, 0))).reshape(
         group_rows + margin, heads_here, HD
     )
     segment_pad = jnp.concatenate([jnp.full((margin,), -1, jnp.int32), segment])
@@ -223,15 +229,9 @@
         return (carry, (mixed.astype(jnp.bfloat16).reshape(QBLK, width_here), log_total))
 
     _, (mixed_blocks, log_totals) = lax.scan(forward_block, jnp.int32(0), block_starts)
-    att_dealt = mixed_blocks.reshape(group_rows, width_here)
-    returned = lax.all_to_all(
-        fill_slots(att_dealt[None], back_first, back_len),
-        "dp",
-        split_axis=1,
-        concat_axis=1,
-        tiled=True,
-    )
-    att_group = place_rows(returned, src_index, src_live)[0]
+    att_group = jnp.where(
+        src_live[:, None], mixed_blocks.reshape(group_rows, width_here), jnp.zeros((), jnp.bfloat16)
+    )
     att_rows = lax.all_to_all(att_group, "mp", split_axis=0, concat_axis=1, tiled=True)
     branch = jnp.dot(att_rows, out_all, preferred_element_type=jnp.float32)
     first_sum = inputs + branch
@@ -259,14 +259,7 @@
         "rd,ud->ru", branch_grad, out_all, preferred_element_type=jnp.float32
     ).astype(jnp.bfloat16)
     grad_group = lax.all_to_all(att_rows_grad, "mp", split_axis=1, concat_axis=0, tiled=True)
-    grad_incoming = lax.all_to_all(
-        fill_slots(grad_group[None], send_first, send_len),
-        "dp",
-        split_axis=1,
-        concat_axis=1,
-        tiled=True,
-    )
-    grad_dealt = place_rows(grad_incoming, dst_index, dst_live)[0].reshape(
+    grad_dealt = jnp.where(src_live[:, None], grad_group, jnp.zeros((), jnp.bfloat16)).reshape(
         group_rows, heads_here, HD
     )
 
@@ -305,35 +298,40 @@
             block_start,
             0,
         )
-        return ((key_grads, value_grads), query_grad.astype(jnp.bfloat16).reshape(QBLK, width_here))
+        return ((key_grads, value_grads), query_grad.reshape(QBLK, heads_here, HD))
 
     empty = jnp.zeros((group_rows + margin, heads_here, HD), jnp.float32)
     (key_grads, value_grads), query_blocks = lax.scan(
         backward_block, (empty, empty), (block_starts, log_totals)
     )
-    grad_stack = jnp.stack(
-        [
-            query_blocks.reshape(group_rows, width_here),
-            key_grads[margin:].reshape(group_rows, width_here).astype(jnp.bfloat16),
-            value_grads[margin:].reshape(group_rows, width_here).astype(jnp.bfloat16),
-        ]
-    )
-    grad_returned = lax.all_to_all(
-        fill_slots(grad_stack, back_first, back_len), "dp", split_axis=1, concat_axis=1, tiled=True
-    )
-    grad_rows_group = place_rows(grad_returned, src_index, src_live)
-    proj_grad = lax.all_to_all(grad_rows_group, "mp", split_axis=1, concat_axis=2, tiled=True)
-    query_scaled_grad = proj_grad[0].astype(jnp.float32).reshape(row_count, NH, HD)
+    query_scaled_grad = query_blocks.reshape(group_rows, heads_here, HD).astype(jnp.bfloat16)
+    query_scaled_grad = jnp.where(
+        src_live[:, None, None], query_scaled_grad, jnp.zeros((), jnp.bfloat16)
+    ).astype(jnp.float32)
     scale_part = (
         jnp.sum(query_scaled_grad * query_raw, axis=(0, 1))
         * (scale_base / math.sqrt(HD))
         * jax.nn.sigmoid(query_scale)
     )
-    query_grad_rows = (query_scaled_grad * dim_scale).reshape(row_count, D).astype(jnp.bfloat16)
-    qkv_grad = jnp.stack([query_grad_rows, proj_grad[1], proj_grad[2]])
-    normed_one_grad = jnp.einsum(
-        "cru,ucd->rd", qkv_grad, qkv_all, preferred_element_type=jnp.float32
-    )
+    query_grad_group = (query_scaled_grad * dim_scale).reshape(group_rows, width_here)
+    key_grad_group = key_grads[margin:].reshape(group_rows, width_here).astype(jnp.bfloat16)
+    value_grad_group = value_grads[margin:].reshape(group_rows, width_here).astype(jnp.bfloat16)
+    proj_grad = jnp.stack(
+        [
+            query_grad_group.astype(jnp.bfloat16),
+            jnp.where(src_live[:, None], key_grad_group, jnp.zeros((), jnp.bfloat16)),
+            jnp.where(src_live[:, None], value_grad_group, jnp.zeros((), jnp.bfloat16)),
+        ]
+    )
+    qkv_part = jnp.einsum(
+        "cru,rd->ucd", proj_grad, normed_group, preferred_element_type=jnp.float32
+    )
+    normed_one_part = jnp.einsum(
+        "cru,ucd->rd", proj_grad, attention_in, preferred_element_type=jnp.float32
+    )
+    normed_one_grad = lax.psum_scatter(
+        normed_one_part.astype(jnp.bfloat16), "mp", scatter_dimension=0, tiled=True
+    ).astype(jnp.float32)
     scaled_one = gain_first * normed_one_grad
     tokens_grad = (
         first_grad
@@ -348,19 +346,20 @@
     shard_width = D // mp_count
     gain_one_grad = lax.dynamic_slice_in_dim(gain_one_sum, my_part * shard_width, shard_width)
     gain_two_grad = lax.dynamic_slice_in_dim(gain_two_sum, my_part * shard_width, shard_width)
-    unit_sides = (qkv_grad, att_rows, preact_grad, hidden)
-    other_sides = (normed_one, branch_grad, normed_two, feed_grad)
+    out_part = jnp.einsum("ru,rd->ud", att_rows, branch_grad, preferred_element_type=jnp.float32)
+    in_part = jnp.einsum("ru,rd->ud", preact_grad, normed_two, preferred_element_type=jnp.float32)
+    down_part = jnp.einsum("ru,rd->ud", hidden, feed_grad, preferred_element_type=jnp.float32)
+    row_terms = jnp.stack([out_part, in_part, down_part], axis=1)
     shares = lax.psum_scatter(
-        unit_terms(unit_sides, other_sides).astype(jnp.bfloat16),
-        "mp",
-        scatter_dimension=0,
-        tiled=True,
-    )
-    totals = lax.psum(shares, "dp").astype(jnp.float32)
+        row_terms.astype(jnp.bfloat16), "mp", scatter_dimension=0, tiled=True
+    )
+    totals = lax.psum(
+        jnp.concatenate([qkv_part.astype(jnp.bfloat16), shares], axis=1), "dp"
+    ).astype(jnp.float32)
     return (
         layer_out,
         tokens_grad,
-        dealt[1:],
+        cache,
         gain_one_grad,
         gain_two_grad,
         totals[:, 0:3],

time: 2740 us -> 914 us (0.33)
  waiting for transfers between devices: 1010 us -> 102 us
  local copies, waits for them, and re-layouts: 791 us -> 337 us
  blocking collectives: 420 us -> 52.5 us
  other arithmetic: 217 us -> 115 us
  matrix products: 199 us -> 236 us
    all_to_all x5 -> x2, waiting for transfers between devices: 682 us -> 7.18 us  [the longest x1 7.18 us: per_device(): lax.all_to_all(att_rows_grad, 'mp', split_axis=1, concat_axis=0, tiled=True)]
    all_to_all x2 -> x0, blocking collectives: 367 us -> none  [the longest x1 349 us: per_device(): lax.all_to_all(fill_slots(grad_stack, back_first, back_len), 'dp', split_...]
    unnamed x7, waiting for transfers between devices: 158 us -> 1.97 us
    gather x4 -> x2, local copies, waits for them, and re-layouts: 225 us -> 107 us  [fill_slots(): picked = jnp.take(values, row_index, axis=1)]
    select_n x4 -> x1, other arithmetic: 105 us -> 10.4 us  [fill_slots(): jnp.where(inside[None, :, None], picked, jnp.zeros((), values.dtype))]
    reshape x4 -> x0, local copies, waits for them, and re-layouts: 88.5 us -> none  [fill_slots(): picked.reshape(values.shape[0], slot_first.shape[0], LMAX, values.shape[2])]
    all_to_all x8 -> x1, local copies, waits for them, and re-layouts: 117 us -> 31.3 us  [per_device(): lax.all_to_all(fill_slots(kv_group, send_first, send_len), 'dp', split_ax...]
    psum x1, waiting for transfers between devices: 70.1 us -> 0.01 us  [per_device(): lax.psum(jnp.concatenate([qkv_part.astype(jnp.bfloat16), shares], axis=1)...]
  transfers between devices with their start and end apart: 12 -> 10, of which waited for: 9 -> 3; matrix products, arithmetic and copies ran while one was open for 11% -> 67% of each run, Pallas kernels for 0% -> 0%
where the time goes in v1:
time: 914 us; the launch traced here: 898 us
  local copies, waits for them, and re-layouts  337 us (37%)
  matrix products  236 us (26%)
  other arithmetic  115 us (13%)
  waiting for transfers between devices  102 us (11%)
  blocking collectives  52.5 us (6%)
  loops' own time  26.3 us (3%)
  between operations  15.6 us (2%)
  starting transfers between devices  14.1 us (2%)
    gather x2, local copies, waits for them, and re-layouts, fill_slots(): picked = jnp.take(values, row_index, axis=1)  107 us
    all_gather x1, waiting for transfers between devices, per_device(): normed_group = lax.all_gather(normed_one, 'mp', axis=0, tiled=True)  55.1 us
    dot_general x4, matrix products, backward_block(): jnp.einsum('qhd,khd->hqk', grad_block, value_window, preferred_element_ty...  50.7 us
    dynamic_update_slice x4, local copies, waits for them, and re-layouts, backward_block(): lax.dynamic_update_slice_in_dim(value_grads, lax.dynamic_slice_in_dim(val...  41.7 us
    dynamic_update_slice x4, local copies, waits for them, and re-layouts, backward_block(): lax.dynamic_update_slice_in_dim(key_grads, lax.dynamic_slice_in_dim(key_g...  41.6 us
    psum x1, blocking collectives, per_device(): lax.psum((gain_one_part, gain_two_part, scale_part), ('dp', 'mp'))  41 us
    reduce_scatter x1, waiting for transfers between devices, per_device(): lax.psum_scatter(normed_one_part.astype(jnp.bfloat16), 'mp', scatter_dime...  37.3 us
    all_to_all x1, local copies, waits for them, and re-layouts, per_device(): lax.all_to_all(fill_slots(kv_group, send_first, send_len), 'dp', split_ax...  31.3 us
  transfers between devices with their start and end apart: 10, of which 3 were waited for; matrix products, arithmetic and copies ran while one was open for 67% of the time, Pallas kernels for 0%

profile of v1, /device:TPU:0, one launch (start us, length us, event | category | flops | bytes accessed | tf_op | source)
XLA Modules:
  0.0 897.5 jit_solution(4901830106620692918)
XLA Ops:
  13.3 11.5 %all-reduce.7 = (bf16[1280]{0:T(1024)(128)(2,1)S(1)}, bf16[1280]{0:T(1024)(128)(2,1)S(1)}) all-reduce(bf16[1280]{0:T(1024)(128)(2,1)S(1)} %dynamic-update-slice, bf16[1280]{0:T(1024)(128)(2,1)S(1)} %dynamic-update-slice.1), channel_id=1, replica_groups=mesh['dp'=8,'mp'=4] {'mp'}, use_global_device_ids=true, to_apply=%add.4 | all-reduce | flops 2560 | bytes 10240
  33.9 55.1 %all-gather.5.cloned.1.call-done = bf16[2048,1280]{1,0:T(8,128)(2,1)} async-done(((bf16[512,1280]{1,0:T(8,128)(2,1)}), bf16[2048,1280]{1,0:T(8,128)(2,1)}) %all-gather.5.cloned.1.call-update) | async-done | bytes 5242896 | tf_op jit(solution)/shard_map/all_gather | solution.py:169
  102.9 70.1 %while.30 = (s32[]{:T(128)}, bf16[4,512,320]{1,2,0:T(8,128)(2,1)}, f32[4,4,512]{2,1,0:T(4,128)S(1)}, s32[4]{0:T(128)S(1)}, bf16[2944,4,80]{0,2,1:T(8,128)(2,1)},...) while((s32[]{:T(128)}, bf16[4,512,320]{1,2,0:T(8,128)(2,1)}, ...), condition=%wide.region_8.9_spmd.clone.clone, body=%wide.region_5.8_spmd.clone.sunk.clone | while | flops 951745920 | bytes 40703828 | solution.py:231
  191.9 76.3 %gather_fusion = bf16[8192,2,320]{2,1,0:T(2,128)(2,1)} fusion(bf16[2,2048,320]{2,0,1:T(2,128)(2,1)} %copy.45, s32[8192]{0:T(1024)S(1)} %broadcast_clamp_fusion), kind=kCustom, calls=%fused_computation | custom fusion | bytes 21004288 | tf_op jit(solution)/shard_map/jit(_take)/gather | solution.py:95
  268.2 30.8 %copy.46 = bf16[2,8,1024,320]{2,3,0,1:T(8,128)(2,1)} copy(bf16[2,8,1024,320]{3,0,2,1:T(2,128)(2,1)} %bitcast.148) | data formatting | bytes 20971520 | tf_op jit(solution)/shard_map/jit(_take)/gather | solution.py:95
  299.0 10.4 %select_select_fusion = bf16[2,8,1024,320]{2,3,0,1:T(8,128)(2,1)} fusion(bf16[2,8,1024,320]{2,3,0,1:T(8,128)(2,1)} %copy.46, pred[8,1024]{1,0:T(8,128)(4,1)S(1)} %get-tuple-element.341, pred[8,1024]{1,0:T(8,128)(4,1)S(1)} %get-tuple-element.340), kind=kLoop, calls=%fused_computation.60 | loop fusion | flops 10485760 | bytes 20987904 | tf_op jit(solution)/shard_map/jit(_where)/select_n | solution.py:96
  338.5 18.9 %fusion.51 = bf16[1280,1,1280]{2,0,1:T(8,128)(2,1)} fusion(bf16[512,1280]{0,1:T(8,128)(2,1)} %bitcast.11, f32[512,1280]{1,0:T(8,128)S(1)} %multiply_subtract_fusion), kind=kOutput, calls=%fused_computation.65 | convolution fusion | flops 1680015360 | bytes 7208960 | tf_op jit(solution)/shard_map/ru,rd->ud/dot_general | solution.py:349
  403.0 266.3 %while.31 = (s32[]{:T(128)}, f32[2944,4,80]{0,2,1:T(8,128)}, f32[2944,4,80]{0,2,1:T(8,128)}, bf16[4,512,4,80]{1,3,2,0:T(8,128)(2,1)}, s32[4]{0:T(128)S(1)}, /*in...) while((s32[]{:T(128)}, f32[2944,4,80]{0,2,1:T(8,128)}, ...), condition=%wide.region_13.14_spmd.clone.clone, body=%wide.region_11.13_spmd.clone.sunk.clone | while | flops 2345254400 | bytes 200849328 | solution.py:304
  421.7 10.8 %dynamic_update_slice.40 = f32[2944,4,80]{0,2,1:T(8,128)} dynamic-update-slice(f32[2944,4,80]{0,2,1:T(8,128)} %get-tuple-element.597, f32[1408,4,80]{0,2,1:T(8,128)} %fusion.171, s32[]{:T(128)S(6)} %select_n.374, s32[]{:T(128)} %constant.159.clone.1..sunk.3, s32[]{:T(128)} %constant.159.clone.1..sunk.3) | dynamic-update-slice | bytes 3604484 | tf_op jit(solution)/shard_map/while/body/eval_jaxpr/dynamic_update_slice | solution.py:295
  432.5 12.8 %multiply_reduce_fusion.6 = (f32[4,512]{1,0:T(4,128)S(1)}, f32[4,512,1408]{2,1,0:T(8,128)}) fusion(f32[4,512,1408]{2,1,0:T(8,128)} %copy-done.1, f32[4,512]{1,0:T(4,128)S(1)} %dynamic-slice_bitcast_fusion.3, pred[512,1408]{1,0:T(8,128)(4,1)S(1)} %fusion.169, bf16[2944,4,80]{0,2,1:T(8,128)(2,1)} %get-tuple-element.620, s32[]{:T(128)S(6)} %select_n.374, ...), kind=kOutput, calls=%fused_computation.26.clone.1.clone | convolution fusion | flops 472905728 | bytes 25034760 | tf_op jit(solution)/shard_map/while/body/eval_jaxpr/qhd,khd->hqk/dot_general | solution.py:272
  460.6 10.7 %dynamic_update_slice.39 = f32[2944,4,80]{0,2,1:T(8,128)} dynamic-update-slice(f32[2944,4,80]{0,2,1:T(8,128)} %get-tuple-element.596, f32[1408,4,80]{0,2,1:T(8,128)} %fusion.170, s32[]{:T(128)S(6)} %select_n.374, s32[]{:T(128)} %constant.159.clone.1..sunk.3, s32[]{:T(128)} %constant.159.clone.1..sunk.3) | dynamic-update-slice | bytes 3604484 | tf_op jit(solution)/shard_map/while/body/eval_jaxpr/dynamic_update_slice | solution.py:289
  489.8 10.6 %dynamic_update_slice.40 = f32[2944,4,80]{0,2,1:T(8,128)} dynamic-update-slice(f32[2944,4,80]{0,2,1:T(8,128)} %get-tuple-element.597, f32[1408,4,80]{0,2,1:T(8,128)} %fusion.171, s32[]{:T(128)S(6)} %select_n.374, s32[]{:T(128)} %constant.159.clone.1..sunk.3, s32[]{:T(128)} %constant.159.clone.1..sunk.3) | dynamic-update-slice | bytes 3604484 | tf_op jit(solution)/shard_map/while/body/eval_jaxpr/dynamic_update_slice | solution.py:295
  500.4 12.7 %multiply_reduce_fusion.6 = (f32[4,512]{1,0:T(4,128)S(1)}, f32[4,512,1408]{2,1,0:T(8,128)}) fusion(f32[4,512,1408]{2,1,0:T(8,128)} %copy-done.1, f32[4,512]{1,0:T(4,128)S(1)} %dynamic-slice_bitcast_fusion.3, pred[512,1408]{1,0:T(8,128)(4,1)S(1)} %fusion.169, bf16[2944,4,80]{0,2,1:T(8,128)(2,1)} %get-tuple-element.620, s32[]{:T(128)S(6)} %select_n.374, ...), kind=kOutput, calls=%fused_computation.26.clone.1.clone | convolution fusion | flops 472905728 | bytes 25034760 | tf_op jit(solution)/shard_map/while/body/eval_jaxpr/qhd,khd->hqk/dot_general | solution.py:272
  527.3 10.6 %dynamic_update_slice.39 = f32[2944,4,80]{0,2,1:T(8,128)} dynamic-update-slice(f32[2944,4,80]{0,2,1:T(8,128)} %get-tuple-element.596, f32[1408,4,80]{0,2,1:T(8,128)} %fusion.170, s32[]{:T(128)S(6)} %select_n.374, s32[]{:T(128)} %constant.159.clone.1..sunk.3, s32[]{:T(128)} %constant.159.clone.1..sunk.3) | dynamic-update-slice | bytes 3604484 | tf_op jit(solution)/shard_map/while/body/eval_jaxpr/dynamic_update_slice | solution.py:289
  556.3 10.4 %dynamic_update_slice.40 = f32[2944,4,80]{0,2,1:T(8,128)} dynamic-update-slice(f32[2944,4,80]{0,2,1:T(8,128)} %get-tuple-element.597, f32[1408,4,80]{0,2,1:T(8,128)} %fusion.171, s32[]{:T(128)S(6)} %select_n.374, s32[]{:T(128)} %constant.159.clone.1..sunk.3, s32[]{:T(128)} %constant.159.clone.1..sunk.3) | dynamic-update-slice | bytes 3604484 | tf_op jit(solution)/shard_map/while/body/eval_jaxpr/dynamic_update_slice | solution.py:295
  566.8 12.7 %multiply_reduce_fusion.6 = (f32[4,512]{1,0:T(4,128)S(1)}, f32[4,512,1408]{2,1,0:T(8,128)}) fusion(f32[4,512,1408]{2,1,0:T(8,128)} %copy-done.1, f32[4,512]{1,0:T(4,128)S(1)} %dynamic-slice_bitcast_fusion.3, pred[512,1408]{1,0:T(8,128)(4,1)S(1)} %fusion.169, bf16[2944,4,80]{0,2,1:T(8,128)(2,1)} %get-tuple-element.620, s32[]{:T(128)S(6)} %select_n.374, ...), kind=kOutput, calls=%fused_computation.26.clone.1.clone | convolution fusion | flops 472905728 | bytes 25034760 | tf_op jit(solution)/shard_map/while/body/eval_jaxpr/qhd,khd->hqk/dot_general | solution.py:272
  593.7 10.4 %dynamic_update_slice.39 = f32[2944,4,80]{0,2,1:T(8,128)} dynamic-update-slice(f32[2944,4,80]{0,2,1:T(8,128)} %get-tuple-element.596, f32[1408,4,80]{0,2,1:T(8,128)} %fusion.170, s32[]{:T(128)S(6)} %select_n.374, s32[]{:T(128)} %constant.159.clone.1..sunk.3, s32[]{:T(128)} %constant.159.clone.1..sunk.3) | dynamic-update-slice | bytes 3604484 | tf_op jit(solution)/shard_map/while/body/eval_jaxpr/dynamic_update_slice | solution.py:289
  632.3 12.6 %multiply_reduce_fusion.6 = (f32[4,512]{1,0:T(4,128)S(1)}, f32[4,512,1408]{2,1,0:T(8,128)}) fusion(f32[4,512,1408]{2,1,0:T(8,128)} %copy-done.1, f32[4,512]{1,0:T(4,128)S(1)} %dynamic-slice_bitcast_fusion.3, pred[512,1408]{1,0:T(8,128)(4,1)S(1)} %fusion.169, bf16[2944,4,80]{0,2,1:T(8,128)(2,1)} %get-tuple-element.620, s32[]{:T(128)S(6)} %select_n.374, ...), kind=kOutput, calls=%fused_computation.26.clone.1.clone | convolution fusion | flops 472905728 | bytes 25034760 | tf_op jit(solution)/shard_map/while/body/eval_jaxpr/qhd,khd->hqk/dot_general | solution.py:272
  700.8 10.2 %fusion.66 = bf16[320,3,1280]{2,0,1:T(8,128)(2,1)} fusion(bf16[2048,1280]{1,0:T(8,128)(2,1)} %all-gather.5.cloned.1.call-done, bf16[1,2048,320]{1,2,0:T(8,128)(2,1)} %copy-done.15, bf16[1,2048,320]{1,2,0:T(8,128)(2,1)} %copy-done.14, bf16[1,2048,320]{1,2,0:T(8,128)(2,1)} %copy-done.13), kind=kOutput, calls=%fused_computation.91 | convolution fusion | flops 5046190080 | bytes 11632640 | tf_op jit(solution)/shard_map/cru,rd->ucd/dot_general | solution.py:326
  716.8 37.3 %reduce-scatter.3.cloned.1.call-done = bf16[512,1280]{1,0:T(8,128)(2,1)} async-done(((bf16[2048,1280]{1,0:T(8,128)(2,1)}), bf16[512,1280]{1,0:T(8,128)(2,1)}) %reduce-scatter.3.cloned.1.call-update) | async-done | bytes 1310736 | tf_op jit(solution)/shard_map/reduce_scatter | solution.py:332
  756.7 41.0 %all-reduce.6 = (f32[1280]{0:T(1024)S(1)}, f32[1280]{0:T(1024)S(1)}, f32[80]{0:T(128)}) all-reduce(f32[1280]{0:T(1024)S(1)} %get-tuple-element.251, f32[1280]{0:T(1024)S(1)} %copy-done.28, f32[80]{0:T(128)S(1)} %divide_multiply_fusion), channel_id=1, replica_groups=mesh['dp'=8,'mp'=4] {'dp','mp'}, use_global_device_ids=true, to_apply=%region_28.29 | all-reduce | flops 2640 | bytes 21120 | tf_op jit(solution)/shard_map/psum | solution.py:343
  803.8 31.3 %copy.47 = bf16[2,8,1024,320]{3,0,2,1:T(2,128)(2,1)} copy(bf16[2,8,1024,320]{2,3,0,1:T(8,128)(2,1)} %all-to-all-done.2) | data formatting | bytes 20971520 | tf_op jit(solution)/shard_map/all_to_all | solution.py:179
  835.2 23.6 %gather_fusion.1 = bf16[2048,2,320]{2,1,0:T(2,128)(2,1)} fusion(bf16[2,8192,320]{2,0,1:T(2,128)(2,1)} %bitcast.150, s32[2048]{0:T(1024)S(1)} %broadcast_clamp_fusion.1), kind=kCustom, calls=%fused_computation.1 | custom fusion | bytes 5251072 | tf_op jit(solution)/shard_map/jit(_take)/gather | solution.py:102
  858.8 13.1 %fusion.69 = bf16[2,2048,320]{2,0,1:T(2,128)(2,1)} fusion(bf16[2048,2,320]{2,1,0:T(2,128)(2,1)} %gather_fusion.1, pred[2048]{0:T(1024)(128)(4,1)S(1)} %get-tuple-element.330, pred[2048]{0:T(1024)(128)(4,1)S(1)} %get-tuple-element.329), kind=kLoop, calls=%fused_computation.92 | loop fusion | flops 2621440 | bytes 5246976 | tf_op jit(solution)/shard_map/jit(_where)/select_n | solution.py:103
  (317 shorter events, 381.6 us)
Async XLA Ops:
  7.2 81.9 %copy-start = (bf16[320,3,1280]{2,0,1:T(8,128)(2,1)S(1)}, bf16[320,3,1280]{2,0,1:T(8,128)(2,1)}, u32[]{:S(2)}) copy-start(bf16[320,3,1280]{2,0,1:T(8,128)(2,1)} %param.21) | copy-start | bytes 7372804
  7.2 81.9 %all-gather.5.cloned.1.call-start = ((), (), s32[]{:S(2)}) async-start(), calls=%async_computation.5 | async-start | bytes 6553600 | tf_op jit(solution)/shard_map/all_gather | solution.py:169
  9.6 20.1 %copy-start.22 = (f32[512]{0:T(512)}, f32[512]{0:T(512)S(1)}, u32[]{:S(2)}) copy-start(f32[512]{0:T(512)S(1)} %get-tuple-element.332) | copy-start | bytes 6148
  28.2 281.3 %all-gather.7.cloned.1.call-start = ((), (), s32[]{:S(2)}) async-start(), calls=%async_computation.6 | async-start | bytes 4096000 | tf_op jit(solution)/shard_map/all_gather | solution.py:134
  29.0 286.7 %all-gather.9.cloned.1.call-start = ((), (), s32[]{:S(2)}) async-start(), calls=%async_computation.7 | async-start | bytes 4096000 | tf_op jit(solution)/shard_map/all_gather | solution.py:135
  29.7 296.1 %all-gather.11.cloned.1.call-start = ((), (), s32[]{:S(2)}) async-start(), calls=%async_computation.8 | async-start | bytes 4096000 | tf_op jit(solution)/shard_map/all_gather | solution.py:136
  30.9 65.4 %copy-start.18 = (pred[2048]{0:T(1024)(128)(4,1)}, pred[2048]{0:T(1024)(128)(4,1)S(1)}, u32[]{:S(2)}) copy-start(pred[2048]{0:T(1024)(128)(4,1)S(1)} %get-tuple-element.314) | copy-start | bytes 6148
  175.5 134.0 %all-to-all-start = ((bf16[4,512,320]{1,2,0:T(8,128)(2,1)}), bf16[4,512,320]{1,2,0:T(8,128)(2,1)}, u32[]{:S(2)}, u32[]{:S(2)}) async-start(bf16[4,512,320]{1,2,0:T(8,128)(2,1)} %broadcast_select_fusion.4), calls=%async_computation | async-start | bytes 2621440 | tf_op jit(solution)/shard_map/all_to_all | solution.py:235
  338.5 19.0 %copy-start.7 = (f32[512,1280]{1,0:T(8,128)}, f32[512,1280]{1,0:T(8,128)S(1)}, u32[]{:S(2)}) copy-start(f32[512,1280]{1,0:T(8,128)S(1)} %multiply_subtract_fusion) | copy-start | bytes 7864324
  338.5 19.0 %copy-start.6 = (bf16[1280,1280]{1,0:T(8,128)(2,1)S(1)}, bf16[1280,1280]{1,0:T(8,128)(2,1)}, u32[]{:S(2)}) copy-start(bf16[1280,1280]{1,0:T(8,128)(2,1)} %all-gather.7.cloned.1.call-done) | copy-start | bytes 9830404
  362.8 21.0 %all-to-all-start.1 = ((bf16[512,4,320]{0,2,1:T(8,128)(2,1)}), bf16[512,4,320]{0,2,1:T(8,128)(2,1)}, u32[]{:S(2)}, u32[]{:S(2)}) async-start(bf16[512,4,320]{0,2,1:T(8,128)(2,1)} %bitcast.155), calls=%async_computation.1 | async-start | bytes 2621440 | tf_op jit(solution)/shard_map/all_to_all | solution.py:261
  367.1 343.9 %reduce-scatter.5.cloned.1.call-start = ((), (), s32[]{:S(2)}) async-start(), calls=%async_computation.10 | async-start | bytes 12288000 | tf_op jit(solution)/shard_map/reduce_scatter | solution.py:353
  383.8 420.1 %all-to-all-start.2 = ((bf16[2,8,1024,320]{2,3,0,1:T(8,128)(2,1)}), bf16[2,8,1024,320]{2,3,0,1:T(8,128)(2,1)}, u32[]{:S(2)}, u32[]{:S(2)}) async-start(bf16[2,8,1024,320]{2,3,0,1:T(8,128)(2,1)} %select_select_fusion), calls=%async_computation.3 | async-start | bytes 20971520 | tf_op jit(solution)/shard_map/all_to_all | solution.py:179
  388.9 365.1 %reduce-scatter.3.cloned.1.call-start = ((), (), s32[]{:S(2)}) async-start(), calls=%async_computation.9 | async-start | bytes 6553600 | tf_op jit(solution)/shard_map/reduce_scatter | solution.py:332
  389.0 7.4 copy-start.19
  432.5 12.8 %copy-start.2 = (f32[4,512,1408]{2,1,0:T(8,128)S(1)}, f32[4,512,1408]{2,1,0:T(8,128)}, u32[]{:S(2)}) copy-start(f32[4,512,1408]{2,1,0:T(8,128)} %copy-done.1) | copy-start | bytes 34603012 | tf_op jit(solution)/shard_map/while
  500.4 12.7 %copy-start.2 = (f32[4,512,1408]{2,1,0:T(8,128)S(1)}, f32[4,512,1408]{2,1,0:T(8,128)}, u32[]{:S(2)}) copy-start(f32[4,512,1408]{2,1,0:T(8,128)} %copy-done.1) | copy-start | bytes 34603012 | tf_op jit(solution)/shard_map/while
  566.8 12.7 %copy-start.2 = (f32[4,512,1408]{2,1,0:T(8,128)S(1)}, f32[4,512,1408]{2,1,0:T(8,128)}, u32[]{:S(2)}) copy-start(f32[4,512,1408]{2,1,0:T(8,128)} %copy-done.1) | copy-start | bytes 34603012 | tf_op jit(solution)/shard_map/while
  632.3 12.6 %copy-start.2 = (f32[4,512,1408]{2,1,0:T(8,128)S(1)}, f32[4,512,1408]{2,1,0:T(8,128)}, u32[]{:S(2)}) copy-start(f32[4,512,1408]{2,1,0:T(8,128)} %copy-done.1) | copy-start | bytes 34603012 | tf_op jit(solution)/shard_map/while
  692.3 188.2 %all-reduce.10.cloned.1.call-start = ((), (), s32[]{:S(2)}) async-start(), calls=%async_computation.11 | async-start | bytes 9830400 | tf_op jit(solution)/shard_map/psum | solution.py:356
  716.1 37.9 %copy-start.17 = (f32[1280]{0:T(1024)S(1)}, f32[1280]{0:T(1024)}, u32[]{:S(2)}) copy-start(f32[1280]{0:T(1024)} %copy-done.16) | copy-start | bytes 15364
  716.1 37.9 %copy-start.23 = (f32[512]{0:T(512)S(1)}, f32[512]{0:T(512)}, u32[]{:S(2)}) copy-start(f32[512]{0:T(512)} %copy-done.22) | copy-start | bytes 6148
  716.1 40.6 %copy-start.28 = (f32[1280]{0:T(1024)S(1)}, f32[1280]{0:T(1024)}, u32[]{:S(2)}) copy-start(f32[1280]{0:T(1024)} %get-tuple-element.249) | copy-start | bytes 15364
  716.1 82.9 %copy-start.24 = (f32[512]{0:T(512)S(1)}, f32[512]{0:T(512)}, u32[]{:S(2)}) copy-start(f32[512]{0:T(512)} %get-tuple-element.331) | copy-start | bytes 6148
  (31 other events, 100.2 us)
Sparse Core Ops, SparseCore 0:
  28.4 60.6 all-gather.4
  90.9 44.9 all-gather.6
  137.7 45.0 all-gather.8
  184.5 46.2 all-gather.10
  376.7 99.4 reduce-scatter.4
  692.4 61.5 reduce-scatter.2
  757.0 111.1 all-reduce.9

commit v2 on v1

v2 whole, which is shorter than its diff:
```python
import math

import jax
import jax.numpy as jnp
from jax import lax
from jax.experimental import pallas as pl
from jax.experimental.pallas import tpu as pltpu
from jax.sharding import PartitionSpec as P

D = 1280
NH = 16
HD = 80
LMAX = 1024
BLK = 128
TQ = 128


epsilon = 1e-06
scale_base = 1.442695041
masked_score = -1e30


def lookup(values_table, positions):
    entries = jnp.arange(values_table.shape[0], dtype=jnp.int32)
    picked = jnp.where(positions[:, None] == entries[None, :], values_table[None, :], 0)
    return jnp.sum(picked, axis=1)


def packing(span_len, group_rows):
    blocks = (span_len + BLK - 1) // BLK
    block_ends = BLK * jnp.cumsum(blocks)
    starts = block_ends - BLK * blocks
    in_group = jnp.arange(group_rows, dtype=jnp.int32)
    series_at = jnp.sum((block_ends[None, :] <= in_group[:, None]).astype(jnp.int32), axis=1)
    capped = jnp.minimum(series_at, span_len.shape[0] - 1)
    offset = in_group - lookup(starts, capped)
    live_row = (series_at < span_len.shape[0]) & (offset < lookup(span_len, capped))
    return (starts, series_at, capped, offset, live_row)


def slot_table(slot_of, starts, span_len, slot_count):
    entries = jnp.arange(slot_count, dtype=jnp.int32)
    matched = slot_of[None, :] == entries[:, None]
    slot_first = jnp.sum(jnp.where(matched, starts[None, :], 0), axis=1)
    slot_length = jnp.sum(jnp.where(matched, span_len[None, :], 0), axis=1)
    return (slot_first, slot_length)


def series_maps(lengths, dealing, series_grp, group_rows, my_group):
    groups = lengths.shape[0] // series_grp
    capacity = (series_grp + groups - 1) // groups
    places = jnp.arange(series_grp, dtype=jnp.int32)
    target = dealing.reshape(groups, series_grp) // series_grp
    earlier = (target[:, :, None] == target[:, None, :]) & (
        places[None, None, :] < places[None, :, None]
    )
    rank_of = jnp.sum(earlier.astype(jnp.int32), axis=2)
    slot_of = (target * capacity + rank_of).reshape(-1)
    rank_flat = rank_of.reshape(-1)
    src_len = lax.dynamic_slice_in_dim(lengths, my_group * series_grp, series_grp)
    src_slot = lax.dynamic_slice_in_dim(slot_of, my_group * series_grp, series_grp)
    src_starts, src_at, src_capped, src_offset, src_live = packing(src_len, group_rows)
    dealt_places = jnp.arange(lengths.shape[0], dtype=jnp.int32)
    owner = jnp.sum(
        jnp.where(dealing[None, :] == dealt_places[:, None], dealt_places[None, :], 0), axis=1
    )
    my_series = lax.dynamic_slice_in_dim(owner, my_group * series_grp, series_grp)
    dst_len = lookup(lengths, my_series)
    dst_slot = my_series // series_grp * capacity + lookup(rank_flat, my_series)
    dst_starts, dst_at, dst_capped, dst_offset, dst_live = packing(dst_len, group_rows)
    slot_count = groups * capacity
    send_first, send_len = slot_table(src_slot, src_starts, src_len, slot_count)
    back_first, back_len = slot_table(dst_slot, dst_starts, dst_len, slot_count)
    src_index = lookup(src_slot, src_capped) * LMAX + src_offset
    dst_index = lookup(dst_slot, dst_capped) * LMAX + dst_offset
    key_live = jnp.where(dst_at < series_grp, dst_live, True)
    return (
        send_first,
        send_len,
        back_first,
        back_len,
        src_index,
        src_live,
        dst_index,
        dst_live,
        dst_at,
        key_live,
    )


def fill_slots(values, slot_first, slot_length):
    padded = jnp.pad(values, ((0, 0), (0, LMAX), (0, 0)))
    positions = jnp.arange(LMAX, dtype=jnp.int32)[None, :, None]
    slots = []
    for g in range(slot_first.shape[0]):
        window = lax.dynamic_slice_in_dim(padded, slot_first[g], LMAX, axis=1)
        slots.append(jnp.where(positions < slot_length[g], window, jnp.zeros((), values.dtype)))
    return jnp.stack(slots, axis=1)


def place_slots(incoming, place_slot, place_start, place_len, out_rows):
    positions = jnp.arange(LMAX, dtype=jnp.int32)[None, :, None]
    placed = jnp.zeros((incoming.shape[0], out_rows + LMAX, incoming.shape[3]), incoming.dtype)
    for q in range(place_slot.shape[0]):
        window = lax.dynamic_index_in_dim(incoming, place_slot[q], axis=1, keepdims=False)
        window = jnp.where(positions < place_len[q], window, jnp.zeros((), incoming.dtype))
        placed = lax.dynamic_update_slice_in_dim(placed, window, place_start[q], axis=1)
    return placed[:, :out_rows]


def dealt_places(lengths, dealing, series_grp, my_group):
    groups = lengths.shape[0] // series_grp
    dealt_places = jnp.arange(lengths.shape[0], dtype=jnp.int32)
    owner = jnp.sum(
        jnp.where(dealing[None, :] == dealt_places[:, None], dealt_places[None, :], 0), axis=1
    )
    my_series = lax.dynamic_slice_in_dim(owner, my_group * series_grp, series_grp)
    place_len = lookup(lengths, my_series)
    blocks = (place_len + BLK - 1) // BLK
    place_start = BLK * jnp.cumsum(blocks) - BLK * blocks
    return my_series // series_grp, place_start, place_len


def block_bounds(src_len, group_rows):
    starts, series_at, capped, offset, live_row = packing(src_len, group_rows)
    first_rows = jnp.arange(group_rows // TQ, dtype=jnp.int32) * TQ
    seg = series_at[first_rows]
    inside = seg < src_len.shape[0]
    seg_c = jnp.minimum(seg, src_len.shape[0] - 1)
    block_start = jnp.where(inside, lookup(starts, seg_c), 0)
    block_end = jnp.where(inside, block_start + lookup(src_len, seg_c), 0)
    return block_start.astype(jnp.int32), block_end.astype(jnp.int32), live_row


def _window(i, rows):
    qs = i * TQ
    ws = jnp.minimum(jnp.maximum(qs - (LMAX - TQ), 0), rows - LMAX)
    return qs, pl.multiple_of(ws, TQ)


def _allowed(qs, ws, s0, e0):
    a = qs + lax.broadcasted_iota(jnp.int32, (TQ, LMAX), 0)
    b = ws + lax.broadcasted_iota(jnp.int32, (TQ, LMAX), 1)
    return (b >= s0) & (b <= a) & (b < e0)


def attn_fwd_kernel(starts_ref, ends_ref, q_ref, k_ref, v_ref, o_ref, lse_ref):
    i = pl.program_id(0)
    heads, rows = k_ref.shape[0], k_ref.shape[1]
    qs, ws = _window(i, rows)
    s0 = starts_ref[i]
    e0 = ends_ref[i]

    @pl.when(s0 < e0)
    def _():
        allowed = _allowed(qs, ws, s0, e0)
        for h in range(heads):
            q = q_ref[h]
            k = k_ref[h, pl.ds(ws, LMAX), :]
            v = v_ref[h, pl.ds(ws, LMAX), :]
            s = lax.dot_general(q, k, (((1,), (1,)), ((), ())), preferred_element_type=jnp.float32)
            s = jnp.where(allowed, s, masked_score)
            m = jnp.max(s, axis=1, keepdims=True)
            p = jnp.exp(s - m)
            l = jnp.sum(p, axis=1, keepdims=True)
            probs = (p / l).astype(jnp.bfloat16)
            o = jnp.dot(probs, v, preferred_element_type=jnp.float32)
            o_ref[h] = o.astype(o_ref.dtype)
            lse_ref[h] = m + jnp.log(l)

    @pl.when(s0 >= e0)
    def _():
        o_ref[...] = jnp.zeros(o_ref.shape, o_ref.dtype)
        lse_ref[...] = jnp.zeros(lse_ref.shape, lse_ref.dtype)


def attn_bwd_kernel(starts_ref, ends_ref, q_ref, k_ref, v_ref, do_ref, lse_ref,
                    dq_ref, dk_ref, dv_ref, dk_acc, dv_acc):
    i = pl.program_id(0)
    heads, rows = k_ref.shape[0], k_ref.shape[1]
    qs, ws = _window(i, rows)
    s0 = starts_ref[i]
    e0 = ends_ref[i]

    @pl.when(i == 0)
    def _():
        dk_acc[...] = jnp.zeros(dk_acc.shape, dk_acc.dtype)
        dv_acc[...] = jnp.zeros(dv_acc.shape, dv_acc.dtype)

    @pl.when(s0 < e0)
    def _():
        allowed = _allowed(qs, ws, s0, e0)
        for h in range(heads):
            q = q_ref[h]
            k = k_ref[h, pl.ds(ws, LMAX), :]
            v = v_ref[h, pl.ds(ws, LMAX), :]
            do = do_ref[h]
            s = lax.dot_general(q, k, (((1,), (1,)), ((), ())), preferred_element_type=jnp.float32)
            s = jnp.where(allowed, s, masked_score)
            probs = jnp.exp(s - lse_ref[h])
            dp = lax.dot_general(do, v, (((1,), (1,)), ((), ())), preferred_element_type=jnp.float32)
            row_dot = jnp.sum(probs * dp, axis=1, keepdims=True)
            ds = (probs * (dp - row_dot)).astype(jnp.bfloat16)
            dq = jnp.dot(ds, k, preferred_element_type=jnp.float32)
            dq_ref[h] = dq.astype(dq_ref.dtype)
            dk_acc[h, pl.ds(ws, LMAX), :] += jnp.dot(ds.T, q, preferred_element_type=jnp.float32)
            dv_acc[h, pl.ds(ws, LMAX), :] += jnp.dot(
                probs.astype(jnp.bfloat16).T, do, preferred_element_type=jnp.float32
            )

    @pl.when(s0 >= e0)
    def _():
        dq_ref[...] = jnp.zeros(dq_ref.shape, dq_ref.dtype)

    @pl.when(i == pl.num_programs(0) - 1)
    def _():
        dk_ref[...] = dk_acc[...].astype(dk_ref.dtype)
        dv_ref[...] = dv_acc[...].astype(dv_ref.dtype)


def attention_forward(q, k, v, starts, ends):
    heads, rows, width = q.shape
    blocks = rows // TQ
    whole = pl.BlockSpec((heads, rows, width), lambda i, s, e: (0, 0, 0))
    part = pl.BlockSpec((heads, TQ, width), lambda i, s, e: (0, i, 0))
    flops = 4 * heads * rows * LMAX * width
    return pl.pallas_call(
        attn_fwd_kernel,
        grid_spec=pltpu.PrefetchScalarGridSpec(
            num_scalar_prefetch=2,
            grid=(blocks,),
            in_specs=[part, whole, whole],
            out_specs=[part, pl.BlockSpec((heads, TQ, 1), lambda i, s, e: (0, i, 0))],
        ),
        out_shape=[
            jax.ShapeDtypeStruct((heads, rows, width), jnp.bfloat16),
            jax.ShapeDtypeStruct((heads, rows, 1), jnp.float32),
        ],
        compiler_params=pltpu.CompilerParams(
            dimension_semantics=("arbitrary",), vmem_limit_bytes=48 * 1024 * 1024
        ),
        cost_estimate=pl.CostEstimate(
            flops=flops, transcendentals=heads * rows * LMAX, bytes_accessed=4 * q.size * 2
        ),
    )(starts, ends, q, k, v)


def attention_backward(q, k, v, do, lse, starts, ends):
    heads, rows, width = q.shape
    blocks = rows // TQ
    whole = pl.BlockSpec((heads, rows, width), lambda i, s, e: (0, 0, 0))
    part = pl.BlockSpec((heads, TQ, width), lambda i, s, e: (0, i, 0))
    flops = 10 * heads * rows * LMAX * width
    return pl.pallas_call(
        attn_bwd_kernel,
        grid_spec=pltpu.PrefetchScalarGridSpec(
            num_scalar_prefetch=2,
            grid=(blocks,),
            in_specs=[part, whole, whole, part, pl.BlockSpec((heads, TQ, 1), lambda i, s, e: (0, i, 0))],
            out_specs=[part, whole, whole],
            scratch_shapes=[
                pltpu.VMEM((heads, rows, width), jnp.float32),
                pltpu.VMEM((heads, rows, width), jnp.float32),
            ],
        ),
        out_shape=[jax.ShapeDtypeStruct((heads, rows, width), jnp.bfloat16)] * 3,
        compiler_params=pltpu.CompilerParams(
            dimension_semantics=("arbitrary",), vmem_limit_bytes=48 * 1024 * 1024
        ),
        cost_estimate=pl.CostEstimate(
            flops=flops, transcendentals=heads * rows * LMAX, bytes_accessed=7 * q.size * 2
        ),
    )(starts, ends, q, k, v, do, lse)


def per_device(
    tokens,
    cotangent,
    lengths,
    dealing,
    gain_one,
    gain_two,
    attention_in,
    query_scale,
    attention_out,
    hidden_in,
    hidden_out,
):
    out_all, in_all, down_all = (
        lax.all_gather(attention_out, "mp", axis=0, tiled=True),
        lax.all_gather(hidden_in, "mp", axis=0, tiled=True),
        lax.all_gather(hidden_out, "mp", axis=0, tiled=True),
    )
    row_count = tokens.shape[0]
    mp_count = lax.axis_size("mp")
    my_group = lax.axis_index("dp")
    my_part = lax.axis_index("mp")
    group_rows = row_count * mp_count
    series_grp = group_rows // LMAX
    heads_here = NH // mp_count
    width_here = heads_here * HD
    shard_width = D // mp_count
    maps = series_maps(lengths, dealing, series_grp, group_rows, my_group)
    send_first, send_len = maps[0], maps[1]
    place_slot, place_start, place_len = dealt_places(lengths, dealing, series_grp, my_group)
    src_len = lax.dynamic_slice_in_dim(lengths, my_group * series_grp, series_grp)
    block_start, block_end, src_live = block_bounds(src_len, group_rows)
    live_mine = lax.dynamic_slice_in_dim(src_live, my_part * row_count, row_count).astype(
        jnp.float32
    )[:, None]
    gain_rows = jnp.zeros((8, D), jnp.bfloat16)
    gain_rows = gain_rows.at[0, :shard_width].set(gain_one).at[0, shard_width : 2 * shard_width].set(gain_two)
    packed = lax.all_gather(jnp.concatenate([tokens, gain_rows]), "mp", axis=0, tiled=False)
    gain_first = packed[:, row_count, :shard_width].reshape(D).astype(jnp.float32)
    gain_second = packed[:, row_count, shard_width : 2 * shard_width].reshape(D).astype(jnp.float32)
    inputs_group = packed[:, :row_count].reshape(group_rows, D).astype(jnp.float32)
    inv_group = lax.rsqrt(jnp.mean(inputs_group * inputs_group, axis=1, keepdims=True) + epsilon)
    normed_group = (inputs_group * inv_group * gain_first).astype(jnp.bfloat16)
    inputs = tokens.astype(jnp.float32)
    inv_one = lax.rsqrt(jnp.mean(inputs * inputs, axis=1, keepdims=True) + epsilon)
    projected = jnp.einsum(
        "rd,ucd->cru", normed_group, attention_in, preferred_element_type=jnp.float32
    )
    dim_scale = scale_base / math.sqrt(HD) * jax.nn.softplus(query_scale)
    query_raw = projected[0].reshape(group_rows, heads_here, HD).transpose(1, 0, 2)
    queries = (query_raw * dim_scale).astype(jnp.bfloat16)
    keys_group = projected[1].astype(jnp.bfloat16)
    values_group = projected[2].astype(jnp.bfloat16)
    kv_group = jnp.stack([keys_group, values_group])
    incoming = lax.all_to_all(
        fill_slots(kv_group, send_first, send_len), "dp", split_axis=1, concat_axis=1, tiled=True
    )
    cache = place_slots(incoming, place_slot, place_start, place_len, group_rows)
    keys = keys_group.reshape(group_rows, heads_here, HD).transpose(1, 0, 2)
    values = values_group.reshape(group_rows, heads_here, HD).transpose(1, 0, 2)
    mixed, log_total = attention_forward(queries, keys, values, block_start, block_end)
    att_group = jnp.where(
        src_live[:, None],
        mixed.transpose(1, 0, 2).reshape(group_rows, width_here),
        jnp.zeros((), jnp.bfloat16),
    )
    att_rows = lax.all_to_all(att_group, "mp", split_axis=0, concat_axis=1, tiled=True)
    branch = jnp.dot(att_rows, out_all, preferred_element_type=jnp.float32)
    first_sum = inputs + branch
    inv_two = lax.rsqrt(jnp.mean(first_sum * first_sum, axis=1, keepdims=True) + epsilon)
    normed_two = (first_sum * inv_two * gain_second).astype(jnp.bfloat16)
    preact = jnp.einsum("rd,fd->rf", normed_two, in_all, preferred_element_type=jnp.float32)
    hidden = jax.nn.silu(preact).astype(jnp.bfloat16)
    feed = jnp.dot(hidden, down_all, preferred_element_type=jnp.float32)
    layer_out = ((first_sum + feed) * live_mine).astype(jnp.bfloat16)
    out_grad = cotangent.astype(jnp.float32) * live_mine
    feed_grad = out_grad.astype(jnp.bfloat16)
    hidden_grad = jnp.einsum("rd,fd->rf", feed_grad, down_all, preferred_element_type=jnp.float32)
    gate_sig = jax.nn.sigmoid(preact)
    preact_grad = (hidden_grad * gate_sig * (1.0 + preact * (1.0 - gate_sig))).astype(jnp.bfloat16)
    normed_two_grad = jnp.dot(preact_grad, in_all, preferred_element_type=jnp.float32)
    scaled_two = gain_second * normed_two_grad
    first_grad = (
        out_grad
        + inv_two * scaled_two
        - first_sum * inv_two**3 * jnp.mean(scaled_two * first_sum, axis=1, keepdims=True)
    )
    branch_grad = first_grad.astype(jnp.bfloat16)
    att_rows_grad = jnp.einsum(
        "rd,ud->ru", branch_grad, out_all, preferred_element_type=jnp.float32
    ).astype(jnp.bfloat16)
    grad_group = lax.all_to_all(att_rows_grad, "mp", split_axis=1, concat_axis=0, tiled=True)
    grad_heads = (
        jnp.where(src_live[:, None], grad_group, jnp.zeros((), jnp.bfloat16))
        .reshape(group_rows, heads_here, HD)
        .transpose(1, 0, 2)
    )
    query_scaled_grad, key_grad, value_grad = attention_backward(
        queries, keys, values, grad_heads, log_total, block_start, block_end
    )
    live_heads = src_live[None, :, None]
    query_scaled_grad = jnp.where(live_heads, query_scaled_grad, jnp.zeros((), jnp.bfloat16)).astype(
        jnp.float32
    )
    scale_part = (
        jnp.sum(query_scaled_grad * query_raw, axis=(0, 1))
        * (scale_base / math.sqrt(HD))
        * jax.nn.sigmoid(query_scale)
    )
    query_grad = (query_scaled_grad * dim_scale).astype(jnp.bfloat16)
    proj_grad = jnp.stack(
        [
            query_grad,
            jnp.where(live_heads, key_grad, jnp.zeros((), jnp.bfloat16)),
            jnp.where(live_heads, value_grad, jnp.zeros((), jnp.bfloat16)),
        ]
    )
    weight_heads = attention_in.reshape(heads_here, HD, 3, D)
    qkv_part = jnp.einsum(
        "chre,rd->hecd", proj_grad, normed_group, preferred_element_type=jnp.float32
    ).reshape(width_here, 3, D)
    normed_one_part = jnp.einsum(
        "chre,hecd->rd", proj_grad, weight_heads, preferred_element_type=jnp.float32
    )
    normed_one_grad = lax.psum_scatter(
        normed_one_part.astype(jnp.bfloat16), "mp", scatter_dimension=0, tiled=True
    ).astype(jnp.float32)
    scaled_one = gain_first * normed_one_grad
    tokens_grad = (
        first_grad
        + inv_one * scaled_one
        - inputs * inv_one**3 * jnp.mean(scaled_one * inputs, axis=1, keepdims=True)
    )
    gain_one_part = jnp.sum(normed_one_grad * inputs * inv_one, axis=0)
    gain_two_part = jnp.sum(normed_two_grad * first_sum * inv_two, axis=0)
    small = jnp.concatenate(
        [
            gain_one_part.reshape(mp_count, shard_width),
            gain_two_part.reshape(mp_count, shard_width),
            jnp.broadcast_to(scale_part, (mp_count, HD)),
        ],
        axis=1,
    )
    small = lax.psum(lax.psum_scatter(small, "mp", scatter_dimension=0, tiled=True), "dp")
    gain_one_grad = small[0, :shard_width]
    gain_two_grad = small[0, shard_width : 2 * shard_width]
    query_scale_grad = small[0, 2 * shard_width :]
    out_part = jnp.einsum("ru,rd->ud", att_rows, branch_grad, preferred_element_type=jnp.float32)
    in_part = jnp.einsum("ru,rd->ud", preact_grad, normed_two, preferred_element_type=jnp.float32)
    down_part = jnp.einsum("ru,rd->ud", hidden, feed_grad, preferred_element_type=jnp.float32)
    row_terms = jnp.stack([out_part, in_part, down_part], axis=1)
    shares = lax.psum_scatter(
        row_terms.astype(jnp.bfloat16), "mp", scatter_dimension=0, tiled=True
    )
    totals = lax.psum(
        jnp.concatenate([qkv_part.astype(jnp.bfloat16), shares], axis=1), "dp"
    ).astype(jnp.float32)
    return (
        layer_out,
        tokens_grad,
        cache,
        gain_one_grad,
        gain_two_grad,
        totals[:, 0:3],
        query_scale_grad,
        totals[:, 3],
        totals[:, 4],
        totals[:, 5],
    )


def solution(mesh):
    placed = (
        P(("dp", "mp"), None),
        P(("dp", "mp"), None),
        P(),
        P(),
        P("mp"),
        P("mp"),
        P("mp", None, None),
        P(),
        P("mp", None),
        P("mp", None),
        P("mp", None),
    )
    return jax.shard_map(
        per_device,
        mesh=mesh,
        in_specs=placed,
        out_specs=(
            P(("dp", "mp"), None),
            P(("dp", "mp"), None),
            P(None, "dp", "mp"),
            P("mp"),
            P("mp"),
            P("mp", None, None),
            P(),
            P("mp", None),
            P("mp", None),
            P("mp", None),
        ),
        check_vma=False,
    )
```

time: 914 us -> 677 us (0.74)
  the two profiles are of different devices: /device:TPU:0 before, /device:TPU:16 now
where the time goes in v2:
time: 677 us; the launch traced here: 664 us
  blocking collectives  141 us (21%)
  waiting for transfers between devices  134 us (20%)
  local copies, waits for them, and re-layouts  97 us (14%)
  Pallas kernels  85.2 us (13%)
  other arithmetic  85 us (13%)
  matrix products  59.8 us (9%)
  between operations  38.3 us (6%)
  starting transfers between devices  23.8 us (4%)
    psum x1, blocking collectives, per_device(): lax.psum(lax.psum_scatter(small, 'mp', scatter_dimension=0, tiled=True),...  126 us
    all_gather x1, waiting for transfers between devices, per_device(): lax.all_gather(jnp.concatenate([tokens, gain_rows]), 'mp', axis=0, tiled=...  59.6 us
    pallas_call x1, Pallas kernels, attention_backward(): pl.pallas_call(attn_bwd_kernel, grid_spec=pltpu.PrefetchScalarGridSpec(nu...  48.8 us
    pallas_call x1, Pallas kernels, attention_forward(): pl.pallas_call(attn_fwd_kernel, grid_spec=pltpu.PrefetchScalarGridSpec(nu...  36.3 us
    reduce_scatter x1, waiting for transfers between devices, per_device(): lax.psum_scatter(normed_one_part.astype(jnp.bfloat16), 'mp', scatter_dime...  27.8 us
    dynamic_update_slice x2, local copies, waits for them, and re-layouts, place_slots(): lax.dynamic_update_slice_in_dim(placed, window, place_start[q], axis=1)  25.5 us
    all_to_all x1, waiting for transfers between devices, per_device(): lax.all_to_all(att_rows_grad, 'mp', split_axis=1, concat_axis=0, tiled=True)  20.9 us
    all_gather x1, waiting for transfers between devices, per_device(): lax.all_gather(hidden_out, 'mp', axis=0, tiled=True)  17.3 us
  transfers between devices with their start and end apart: 10, of which 5 were waited for; matrix products, arithmetic and copies ran while one was open for 29% of the time, Pallas kernels for 13%

profile of v2, /device:TPU:16, one launch (start us, length us, event | category | flops | bytes accessed | tf_op | source)
XLA Modules:
  0.0 663.9 jit_solution(12716393631373551227)
XLA Ops:
  20.4 59.6 %all-gather.12.cloned.1.call-done = bf16[2080,1280]{1,0:T(8,128)(2,1)} async-done(((bf16[520,1280]{1,0:T(8,128)(2,1)}), bf16[2080,1280]{1,0:T(8,128)(2,1)}) %all-gather.12.cloned.1.call-update) | async-done | bytes 5324816 | tf_op jit(solution)/shard_map/all_gather | solution.py:313
  81.0 7.5 %slice_convert_fusion = f32[4,512,1280]{2,1,0:T(8,128)} fusion(bf16[4,520,1280]{2,1,0:T(8,128)(2,1)} %bitcast.151), kind=kLoop, calls=%fused_computation.19 | loop fusion | flops 2621440 | bytes 15728640 | tf_op jit(solution)/shard_map/convert_element_type | solution.py:316
  89.7 5.3 fusion.1
  95.0 5.3 fusion.14
  123.0 36.3 %shard_map.186 = (bf16[4,2048,80]{2,1,0:T(8,128)(2,1)S(1)}, f32[4,2048,1]{2,1,0:T(8,128)}) custom-call(s32[16]{0:T(128)S(1)} %get-tuple-element.80.starts_ref, s32[16]{0:T(128)S(1)} %get-tuple-element.79.ends_ref, bf16[4,2048,80]{2,1,0:T(8,128)(2,1)S(1)} %fusion.13.q_ref, bf16[4,2048,80]{2,1,0:T(8,128)(2,1)} %bitcast.160, bf16[4,2048,80]{2,1,0:T(8,128)(2,1)} %bitcast.162), custom_call_target="tpu_custom_call" | custom-call | flops 2684354560 | bytes 5242880 | tf_op jit(solution)/shard_map/pallas_call | solution.py:227
  175.9 8.8 %reduce-scatter.5.cloned.1.call-start = ((), (), s32[]{:S(2)}) async-start(), calls=%async_computation.9 | async-start | bytes 12288000 | tf_op jit(solution)/shard_map/reduce_scatter | solution.py:427
  184.9 6.3 all-to-all-done
  191.2 6.2 multiply_reduce_fusion.3
  197.4 4.7 fusion.53
  207.4 17.3 %all-gather.10.cloned.1.call-done = bf16[1280,1280]{1,0:T(8,128)(2,1)} async-done(((bf16[320,1280]{1,0:T(8,128)(2,1)}), bf16[1280,1280]{1,0:T(8,128)(2,1)}) %all-gather.10.cloned.1.call-update) | async-done | bytes 3276816 | tf_op jit(solution)/shard_map/all_gather | solution.py:292
  224.7 5.5 fusion.25
  297.4 20.9 %all-to-all-done.1 = bf16[512,4,320]{0,2,1:T(8,128)(2,1)} async-done(((bf16[512,4,320]{0,2,1:T(8,128)(2,1)}), bf16[512,4,320]{0,2,1:T(8,128)(2,1)}, u32[]{:S(2)}, u32[]{:S(2)}) %all-to-all-start.1) | async-done | bytes 1310752 | tf_op jit(solution)/shard_map/all_to_all | solution.py:367
  318.3 5.6 all-to-all-start.2
  338.1 48.8 %shard_map.187 = (bf16[4,2048,80]{2,1,0:T(8,128)(2,1)S(1)}, bf16[4,2048,80]{2,1,0:T(8,128)(2,1)S(1)}, bf16[4,2048,80]{2,1,0:T(8,128)(2,1)}) custom-call(s32[16]{0:T(128)S(1)} %get-tuple-element.80.starts_ref, s32[16]{0:T(128)S(1)} %get-tuple-element.79.ends_ref, bf16[4,2048,80]{2,1,0:T(8,128)(2,1)} %copy-done.1, bf16[4,2048,80]{2,1,0:T(8,128)(2,1)} %bitcast.161, ...), custom_call_target="tpu_custom_call" | custom-call | flops 6710886400 | bytes 9175040 | tf_op jit(solution)/shard_map/pallas_call | solution.py:254
  391.0 8.8 %bitcast_convert_fusion = bf16[2048,1280]{1,0:T(8,128)(2,1)} fusion(bf16[4,80,3,1280]{3,1,0,2:T(8,128)(2,1)S(1)} %bitcast.148, bf16[1,4,2048,80]{3,2,1,0:T(8,128)(2,1)S(1)} %get-tuple-element.76, bf16[1,4,2048,80]{3,2,1,0:T(8,128)(2,1)S(1)} %get-tuple-element.75, bf16[1,4,2048,80]{3,2,1,0:T(8,128)(2,1)S(1)} %get-tuple-element.72), kind=kOutput, calls=%fused_computation.1 | convolution fusion | flops 5039718400 | bytes 11632640 | tf_op jit(solution)/shard_map/chre,hecd->rd/dot_general | solution.py:397
  413.7 6.9 %fusion.24 = bf16[512,1280]{1,0:T(8,128)(2,1)} fusion(f32[512,1280]{1,0:T(8,128)} %get-tuple-element.106, bf16[1280,1280]{1,0:T(8,128)(2,1)} %all-gather.10.cloned.1.call-done, f32[512]{0:T(512)S(1)} %dynamic-slice_convert_fusion, f32[512,1280]{1,0:T(8,128)} %copy-done.32), kind=kOutput, calls=%fused_computation.43 | convolution fusion | flops 1682964480 | bytes 9832448 | tf_op jit(solution)/shard_map/dot_general | solution.py:349
  420.9 6.9 %fusion.18 = bf16[1280,3,4,80]{0,3,2,1:T(8,128)(2,1)} fusion(bf16[2048,1280]{1,0:T(8,128)(2,1)S(1)} %bitcast.157, bf16[1,4,2048,80]{3,2,1,0:T(8,128)(2,1)S(1)} %copy-done.20, bf16[1,4,2048,80]{3,2,1,0:T(8,128)(2,1)S(1)} %copy-done.18, bf16[1,4,2048,80]{3,2,1,0:T(8,128)(2,1)S(1)} %copy-done.16), kind=kOutput, calls=%fused_computation.36 | convolution fusion | flops 5046190080 | bytes 11632640 | tf_op jit(solution)/shard_map/chre,rd->hecd/dot_general | solution.py:394
  427.8 5.1 pad_maximum_fusion.2
  433.6 27.8 %reduce-scatter.3.cloned.1.call-done = bf16[512,1280]{1,0:T(8,128)(2,1)} async-done(((bf16[2048,1280]{1,0:T(8,128)(2,1)}), bf16[512,1280]{1,0:T(8,128)(2,1)}) %reduce-scatter.3.cloned.1.call-update) | async-done | bytes 1310736 | tf_op jit(solution)/shard_map/reduce_scatter | solution.py:400
  464.2 15.0 %all-reduce.2 = f32[4,720]{1,0:T(4,128)S(1)} all-reduce(f32[4,720]{1,0:T(4,128)S(1)} %maximum_maximum_fusion), channel_id=4, replica_groups=mesh['dp'=8,'mp'=4] {'mp'}, use_global_device_ids=true, to_apply=%region_22.23.clone | all-reduce | flops 2880 | bytes 23040
  479.8 126.1 %psum.14 = f32[1,720]{1,0:T(1,128)S(1)} all-reduce(f32[1,720]{1,0:T(1,128)S(1)} %constant_dynamic-slice_fusion), channel_id=1, replica_groups=mesh['dp'=8,'mp'=4] {'dp'}, use_global_device_ids=true, to_apply=%region_23.24 | all-reduce | flops 720 | bytes 5760 | tf_op jit(solution)/shard_map/psum | solution.py:419
  607.2 4.8 fusion.27
  617.8 12.7 %dynamic_update_slice.6 = bf16[2,3072,320]{1,2,0:T(8,128)(2,1)} dynamic-update-slice(bf16[2,3072,320]{1,2,0:T(8,128)(2,1)} %broadcast_in_dim.250, bf16[2,1024,320]{1,2,0:T(8,128)(2,1)} %get-tuple-element.65, s32[]{:T(128)} %constant.144.clone.1, s32[]{:T(128)S(6)} %select_n.226, s32[]{:T(128)} %constant.144.clone.1) | dynamic-update-slice | bytes 2621444 | tf_op jit(solution)/shard_map/dynamic_update_slice | solution.py:107
  630.5 12.7 %dynamic_update_slice.7 = bf16[2,3072,320]{1,2,0:T(8,128)(2,1)} dynamic-update-slice(bf16[2,3072,320]{1,2,0:T(8,128)(2,1)} %dynamic_update_slice.6, bf16[2,1024,320]{1,2,0:T(8,128)(2,1)} %get-tuple-element.64, s32[]{:T(128)} %constant.144.clone.1, s32[]{:T(128)S(6)} %select_n.229, s32[]{:T(128)} %constant.144.clone.1) | dynamic-update-slice | bytes 2621444 | tf_op jit(solution)/shard_map/dynamic_update_slice | solution.py:107
  (209 shorter events, 160.6 us)
Async XLA Ops:
  7.2 87.8 %copy-start = (bf16[320,3,1280]{2,0,1:T(8,128)(2,1)S(1)}, bf16[320,3,1280]{2,0,1:T(8,128)(2,1)}, u32[]{:S(2)}) copy-start(bf16[320,3,1280]{2,0,1:T(8,128)(2,1)} %param.21) | copy-start | bytes 7372804
  7.2 72.9 %all-gather.12.cloned.1.call-start = ((), (), s32[]{:S(2)}) async-start(), calls=%async_computation.11 | async-start | bytes 6656000 | tf_op jit(solution)/shard_map/all_gather | solution.py:313
  16.8 168.1 %all-gather.6.cloned.1.call-start = ((), (), s32[]{:S(2)}) async-start(), calls=%async_computation.5 | async-start | bytes 4096000 | tf_op jit(solution)/shard_map/all_gather | solution.py:290
  17.6 179.7 %all-gather.8.cloned.1.call-start = ((), (), s32[]{:S(2)}) async-start(), calls=%async_computation.6 | async-start | bytes 4096000 | tf_op jit(solution)/shard_map/all_gather | solution.py:291
  18.3 206.4 %all-gather.10.cloned.1.call-start = ((), (), s32[]{:S(2)}) async-start(), calls=%async_computation.7 | async-start | bytes 4096000 | tf_op jit(solution)/shard_map/all_gather | solution.py:292
  81.0 7.5 %copy-start.6 = (bf16[2080,1280]{1,0:T(8,128)(2,1)S(1)}, bf16[2080,1280]{1,0:T(8,128)(2,1)}, u32[]{:S(2)}) copy-start(bf16[2080,1280]{1,0:T(8,128)(2,1)} %all-gather.12.cloned.1.call-done) | copy-start | bytes 15974404
  123.0 36.3 %copy-start.1 = (bf16[4,2048,80]{2,1,0:T(8,128)(2,1)}, bf16[4,2048,80]{2,1,0:T(8,128)(2,1)S(1)}, u32[]{:S(2)}) copy-start(bf16[4,2048,80]{2,1,0:T(8,128)(2,1)S(1)} %fusion.13.q_ref) | copy-start | bytes 3932164
  171.6 19.5 %all-to-all-start = ((bf16[4,512,320]{1,2,0:T(8,128)(2,1)}), bf16[4,512,320]{1,2,0:T(8,128)(2,1)}, u32[]{:S(2)}, u32[]{:S(2)}) async-start(bf16[4,512,320]{1,2,0:T(8,128)(2,1)} %copy.47), calls=%async_computation | async-start | bytes 2621440 | tf_op jit(solution)/shard_map/all_to_all | solution.py:342
  175.9 251.9 %reduce-scatter.5.cloned.1.call-start = ((), (), s32[]{:S(2)}) async-start(), calls=%async_computation.9 | async-start | bytes 12288000 | tf_op jit(solution)/shard_map/reduce_scatter | solution.py:427
  197.3 6.2 copy-start.22
  269.3 5.8 copy-start.3
  282.4 35.8 %all-to-all-start.1 = ((bf16[512,4,320]{0,2,1:T(8,128)(2,1)}), bf16[512,4,320]{0,2,1:T(8,128)(2,1)}, u32[]{:S(2)}, u32[]{:S(2)}) async-start(bf16[512,4,320]{0,2,1:T(8,128)(2,1)} %bitcast.158), calls=%async_computation.1 | async-start | bytes 2621440 | tf_op jit(solution)/shard_map/all_to_all | solution.py:367
  286.8 6.9 %copy-start.4 = (bf16[2,3072,320]{1,2,0:T(8,128)(2,1)S(1)}, bf16[2,3072,320]{1,2,0:T(8,128)(2,1)}, u32[]{:S(2)}) copy-start(bf16[2,3072,320]{1,2,0:T(8,128)(2,1)} %copy-done.3) | copy-start | bytes 11796484
  318.3 293.7 %all-to-all-start.2 = ((bf16[2,8,1024,320]{2,3,0,1:T(8,128)(2,1)}), bf16[2,8,1024,320]{2,3,0,1:T(8,128)(2,1)}, u32[]{:S(2)}, u32[]{:S(2)}) async-start(bf16[2,8,1024,320]{2,3,0,1:T(8,128)(2,1)} %bitcast_dynamic-update-slice_fusion), calls=%async_computation.3 | async-start | bytes 20971520 | tf_op jit(solution)/shard_map/all_to_all | solution.py:330
  323.8 137.5 %reduce-scatter.3.cloned.1.call-start = ((), (), s32[]{:S(2)}) async-start(), calls=%async_computation.8 | async-start | bytes 6553600 | tf_op jit(solution)/shard_map/reduce_scatter | solution.py:400
  338.1 48.8 %copy-start.5 = (f32[2048,4,80]{2,0,1:T(8,128)S(1)}, f32[2048,4,80]{2,0,1:T(8,128)}, u32[]{:S(2)}) copy-start(f32[2048,4,80]{2,0,1:T(8,128)} %copy.43) | copy-start | bytes 7864324
  399.9 7.0 %copy-start.31 = (u32[32]{0:T(128)S(1)}, u32[32]{0:T(128)}, u32[]{:S(2)}) copy-start(u32[32]{0:T(128)} %constant.171) | copy-start | bytes 388
  399.9 20.8 %slice-start = ((s8[5242880]{0:T(1024)(128)(4,1)}), s8[1048576]{0:T(1024)(128)(4,1)S(1)}, s32[]{:S(2)}) async-start(s8[5242880]{0:T(1024)(128)(4,1)} %bitcast.156), calls=%async_computation.12 | async-start | bytes 2097152
  399.9 246.9 %all-reduce.5.cloned.1.call-start = ((), (), s32[]{:S(2)}) async-start(), calls=%async_computation.10 | async-start | bytes 9830400 | tf_op jit(solution)/shard_map/psum | solution.py:430
  413.7 7.0 %slice-start.1 = ((s8[5242880]{0:T(1024)(128)(4,1)}), s8[4194304]{0:T(1024)(128)(4,1)S(1)}, s32[]{:S(2)}) async-start(s8[5242880]{0:T(1024)(128)(4,1)} %bitcast.156), calls=%async_computation.13 | async-start | bytes 8388608
  413.7 7.0 %copy-start.16 = (bf16[1,4,2048,80]{3,2,1,0:T(8,128)(2,1)S(1)}, bf16[1,4,2048,80]{3,2,1,0:T(8,128)(2,1)}, u32[]{:S(2)}) copy-start(bf16[1,4,2048,80]{3,2,1,0:T(8,128)(2,1)} %copy-done.15) | copy-start | bytes 3932164
  413.7 7.0 %copy-start.18 = (bf16[1,4,2048,80]{3,2,1,0:T(8,128)(2,1)S(1)}, bf16[1,4,2048,80]{3,2,1,0:T(8,128)(2,1)}, u32[]{:S(2)}) copy-start(bf16[1,4,2048,80]{3,2,1,0:T(8,128)(2,1)} %copy-done.17) | copy-start | bytes 3932164
  413.7 7.1 %copy-start.20 = (bf16[1,4,2048,80]{3,2,1,0:T(8,128)(2,1)S(1)}, bf16[1,4,2048,80]{3,2,1,0:T(8,128)(2,1)}, u32[]{:S(2)}) copy-start(bf16[1,4,2048,80]{3,2,1,0:T(8,128)(2,1)} %copy-done.19) | copy-start | bytes 3932164
  432.9 28.4 %copy-start.25 = (f32[1280]{0:T(1024)S(1)}, f32[1280]{0:T(1024)}, u32[]{:S(2)}) copy-start(f32[1280]{0:T(1024)} %copy-done.24) | copy-start | bytes 15364
  (21 other events, 69.3 us)
Sparse Core Ops, SparseCore 0:
  17.0 63.0 all-gather.11
  81.9 44.9 all-gather.5
  128.7 45.0 all-gather.7
  175.5 49.1 all-gather.9
  244.4 112.1 reduce-scatter.4
  400.0 61.2 reduce-scatter.2
  464.3 178.8 all-reduce.4

commit v3 on v2

--- a/solution.py
+++ b/solution.py
@@ -6,6 +6,7 @@
 from jax.experimental import pallas as pl
 from jax.experimental.pallas import tpu as pltpu
 from jax.sharding import PartitionSpec as P
+
 
 D = 1280
 NH = 16
@@ -59,7 +60,7 @@
     rank_flat = rank_of.reshape(-1)
     src_len = lax.dynamic_slice_in_dim(lengths, my_group * series_grp, series_grp)
     src_slot = lax.dynamic_slice_in_dim(slot_of, my_group * series_grp, series_grp)
-    src_starts, src_at, src_capped, src_offset, src_live = packing(src_len, group_rows)
+    src_starts, _, src_capped, src_offset, src_live = packing(src_len, group_rows)
     dealt_places = jnp.arange(lengths.shape[0], dtype=jnp.int32)
     owner = jnp.sum(
         jnp.where(dealing[None, :] == dealt_places[:, None], dealt_places[None, :], 0), axis=1
@@ -88,28 +89,33 @@
     )
 
 
-def fill_slots(values, slot_first, slot_length):
+def send_windows(values, slot_first, slot_length, my_group, groups):
     padded = jnp.pad(values, ((0, 0), (0, LMAX), (0, 0)))
     positions = jnp.arange(LMAX, dtype=jnp.int32)[None, :, None]
-    slots = []
-    for g in range(slot_first.shape[0]):
-        window = lax.dynamic_slice_in_dim(padded, slot_first[g], LMAX, axis=1)
-        slots.append(jnp.where(positions < slot_length[g], window, jnp.zeros((), values.dtype)))
-    return jnp.stack(slots, axis=1)
-
-
-def place_slots(incoming, place_slot, place_start, place_len, out_rows):
-    positions = jnp.arange(LMAX, dtype=jnp.int32)[None, :, None]
-    placed = jnp.zeros((incoming.shape[0], out_rows + LMAX, incoming.shape[3]), incoming.dtype)
-    for q in range(place_slot.shape[0]):
-        window = lax.dynamic_index_in_dim(incoming, place_slot[q], axis=1, keepdims=False)
-        window = jnp.where(positions < place_len[q], window, jnp.zeros((), incoming.dtype))
-        placed = lax.dynamic_update_slice_in_dim(placed, window, place_start[q], axis=1)
-    return placed[:, :out_rows]
+    windows = []
+    for shift in range(groups):
+        target = (my_group + shift) % groups
+        window = lax.dynamic_slice_in_dim(padded, slot_first[target], LMAX, axis=1)
+        windows.append(
+            jnp.where(positions < slot_length[target], window, jnp.zeros((), values.dtype))
+        )
+    return windows
+
+
+def place_slots(received, place_shift, place_start, place_len, out_rows):
+    stacked = jnp.stack(received)
+    rows = jnp.arange(out_rows, dtype=jnp.int32)[None, :, None]
+    placed = jnp.zeros((stacked.shape[1], out_rows, stacked.shape[3]), stacked.dtype)
+    for q in range(place_shift.shape[0]):
+        window = lax.dynamic_index_in_dim(stacked, place_shift[q], axis=0, keepdims=False)
+        padded = jnp.pad(window, ((0, 0), (out_rows, out_rows - LMAX), (0, 0)))
+        shifted = lax.dynamic_slice_in_dim(padded, out_rows - place_start[q], out_rows, axis=1)
+        inside = (rows >= place_start[q]) & (rows < place_start[q] + place_len[q])
+        placed = jnp.where(inside, shifted, placed)
+    return placed
 
 
 def dealt_places(lengths, dealing, series_grp, my_group):
-    groups = lengths.shape[0] // series_grp
     dealt_places = jnp.arange(lengths.shape[0], dtype=jnp.int32)
     owner = jnp.sum(
         jnp.where(dealing[None, :] == dealt_places[:, None], dealt_places[None, :], 0), axis=1
@@ -122,7 +128,7 @@
 
 
 def block_bounds(src_len, group_rows):
-    starts, series_at, capped, offset, live_row = packing(src_len, group_rows)
+    starts, series_at, _, _, live_row = packing(src_len, group_rows)
     first_rows = jnp.arange(group_rows // TQ, dtype=jnp.int32) * TQ
     seg = series_at[first_rows]
     inside = seg < src_len.shape[0]
@@ -327,10 +333,16 @@
     keys_group = projected[1].astype(jnp.bfloat16)
     values_group = projected[2].astype(jnp.bfloat16)
     kv_group = jnp.stack([keys_group, values_group])
-    incoming = lax.all_to_all(
-        fill_slots(kv_group, send_first, send_len), "dp", split_axis=1, concat_axis=1, tiled=True
-    )
-    cache = place_slots(incoming, place_slot, place_start, place_len, group_rows)
+    groups = lax.axis_size("dp")
+    windows = send_windows(kv_group, send_first, send_len, my_group, groups)
+    received = [windows[0]] + [
+        lax.ppermute(
+            windows[shift], "dp", [(r, (r + shift) % groups) for r in range(groups)]
+        )
+        for shift in range(1, groups)
+    ]
+    place_shift = (my_group - place_slot) % groups
+    cache = place_slots(received, place_shift, place_start, place_len, group_rows)
     keys = keys_group.reshape(group_rows, heads_here, HD).transpose(1, 0, 2)
     values = values_group.reshape(group_rows, heads_here, HD).transpose(1, 0, 2)
     mixed, log_total = attention_forward(queries, keys, values, block_start, block_end)
@@ -406,7 +418,7 @@
         + inv_one * scaled_one
         - inputs * inv_one**3 * jnp.mean(scaled_one * inputs, axis=1, keepdims=True)
     )
-    gain_one_part = jnp.sum(normed_one_grad * inputs * inv_one, axis=0)
+    gain_one_part = jnp.sum(normed_one_part * inputs_group * inv_group, axis=0)
     gain_two_part = jnp.sum(normed_two_grad * first_sum * inv_two, axis=0)
     small = jnp.concatenate(
         [

time: 677 us -> 826 us (1.22)
  the two profiles are of different devices: /device:TPU:16 before, /device:TPU:0 now
where the time goes in v3:
time: 826 us; the launch traced here: 815 us
  waiting for transfers between devices  355 us (43%)
  local copies, waits for them, and re-layouts  79.9 us (10%)
  other arithmetic  74.9 us (9%)
  Pallas kernels  73 us (9%)
  matrix products  69.7 us (8%)
  blocking collectives  65.8 us (8%)
  starting transfers between devices  57.5 us (7%)
  between operations  39.3 us (5%)
    ppermute x7, waiting for transfers between devices, per_device(): lax.ppermute(windows[shift], 'dp', [(r, (r + shift) % groups) for r in ra...  142 us
    psum x1, waiting for transfers between devices, per_device(): lax.psum(jnp.concatenate([qkv_part.astype(jnp.bfloat16), shares], axis=1)...  67.1 us
    all_gather x1, waiting for transfers between devices, per_device(): lax.all_gather(jnp.concatenate([tokens, gain_rows]), 'mp', axis=0, tiled=...  61.3 us
    psum x1, blocking collectives, per_device(): lax.psum(lax.psum_scatter(small, 'mp', scatter_dimension=0, tiled=True),...  50.9 us
    ppermute x7, starting transfers between devices, per_device(): lax.ppermute(windows[shift], 'dp', [(r, (r + shift) % groups) for r in ra...  48.2 us
    pallas_call x1, Pallas kernels, attention_backward(): pl.pallas_call(attn_bwd_kernel, grid_spec=pltpu.PrefetchScalarGridSpec(nu...  41.9 us
    pallas_call x1, Pallas kernels, attention_forward(): pl.pallas_call(attn_fwd_kernel, grid_spec=pltpu.PrefetchScalarGridSpec(nu...  31 us
    all_to_all x1, waiting for transfers between devices, per_device(): lax.all_to_all(att_rows_grad, 'mp', split_axis=1, concat_axis=0, tiled=True)  30.9 us
  transfers between devices with their start and end apart: 16, of which 8 were waited for; matrix products, arithmetic and copies ran while one was open for 20% of the time, Pallas kernels for 9%

profile of v3, /device:TPU:0, one launch (start us, length us, event | category | flops | bytes accessed | tf_op | source)
XLA Modules:
  0.0 815.0 jit_solution(14190332843078930266)
XLA Ops:
  20.5 61.3 %all-gather.12.cloned.1.call-done = bf16[2080,1280]{1,0:T(8,128)(2,1)} async-done(((bf16[520,1280]{1,0:T(8,128)(2,1)}), bf16[2080,1280]{1,0:T(8,128)(2,1)}) %all-gather.12.cloned.1.call-update) | async-done | bytes 5324816 | tf_op jit(solution)/shard_map/all_gather | solution.py:319
  90.2 5.3 fusion.17
  118.3 31.0 %shard_map.186 = (bf16[4,2048,80]{2,1,0:T(8,128)(2,1)S(1)}, f32[4,2048,1]{2,1,0:T(8,128)}) custom-call(s32[16]{0:T(128)S(1)} %get-tuple-element.87.starts_ref, s32[16]{0:T(128)S(1)} %get-tuple-element.86.ends_ref, bf16[4,2048,80]{2,1,0:T(8,128)(2,1)S(1)} %fusion.16.q_ref, bf16[4,2048,80]{2,1,0:T(8,128)(2,1)} %bitcast.167, bf16[4,2048,80]{2,1,0:T(8,128)(2,1)} %bitcast.169), custom_call_target="tpu_custom_call" | custom-call | flops 2684354560 | bytes 5242880 | tf_op jit(solution)/shard_map/pallas_call | solution.py:233
  166.4 22.9 %all-to-all-done = bf16[4,512,320]{1,2,0:T(8,128)(2,1)} async-done(((bf16[4,512,320]{1,2,0:T(8,128)(2,1)}), bf16[4,512,320]{1,2,0:T(8,128)(2,1)}, u32[]{:S(2)}, u32[]{:S(2)}) %all-to-all-start) | async-done | bytes 1310752 | tf_op jit(solution)/shard_map/all_to_all | solution.py:354
  189.3 6.2 multiply_reduce_fusion.2
  206.0 28.6 %all-gather.10.cloned.1.call-done = bf16[1280,1280]{1,0:T(8,128)(2,1)} async-done(((bf16[320,1280]{1,0:T(8,128)(2,1)}), bf16[1280,1280]{1,0:T(8,128)(2,1)}) %all-gather.10.cloned.1.call-update) | async-done | bytes 3276816 | tf_op jit(solution)/shard_map/all_gather | solution.py:298
  234.7 5.5 fusion.27
  245.2 13.7 %fusion.7 = bf16[1280,1,1280]{2,0,1:T(8,128)(2,1)S(1)} fusion(bf16[512,1280]{0,1:T(8,128)(2,1)} %bitcast.17, f32[512,1280]{1,0:T(8,128)S(1)} %multiply_subtract_fusion), kind=kOutput, calls=%fused_computation.17 | convolution fusion | flops 1680015360 | bytes 7208960 | tf_op jit(solution)/shard_map/ru,rd->ud/dot_general | solution.py:435
  263.6 5.7 convolution_convert_fusion.3
  276.7 30.9 %all-to-all-done.1 = bf16[512,4,320]{0,2,1:T(8,128)(2,1)} async-done(((bf16[512,4,320]{0,2,1:T(8,128)(2,1)}), bf16[512,4,320]{0,2,1:T(8,128)(2,1)}, u32[]{:S(2)}, u32[]{:S(2)}) %all-to-all-start.1) | async-done | bytes 1310752 | tf_op jit(solution)/shard_map/all_to_all | solution.py:379
  321.5 41.9 %shard_map.187 = (bf16[4,2048,80]{2,1,0:T(8,128)(2,1)S(1)}, bf16[4,2048,80]{2,1,0:T(8,128)(2,1)S(1)}, bf16[4,2048,80]{2,1,0:T(8,128)(2,1)}) custom-call(s32[16]{0:T(128)S(1)} %get-tuple-element.87.starts_ref, s32[16]{0:T(128)S(1)} %get-tuple-element.86.ends_ref, bf16[4,2048,80]{2,1,0:T(8,128)(2,1)} %copy-done.2, bf16[4,2048,80]{2,1,0:T(8,128)(2,1)} %bitcast.168, ...), custom_call_target="tpu_custom_call" | custom-call | flops 6710886400 | bytes 9175040 | tf_op jit(solution)/shard_map/pallas_call | solution.py:260
  366.0 10.6 %bitcast_convert_fusion = (bf16[2048,1280]{1,0:T(8,128)(2,1)}, f32[2048,1280,1,1]{1,0,3,2:T(8,128)}) fusion(bf16[4,80,3,1280]{3,1,0,2:T(8,128)(2,1)S(1)} %bitcast.154, bf16[1,4,2048,80]{3,2,1,0:T(8,128)(2,1)S(1)} %get-tuple-element.83, bf16[1,4,2048,80]{3,2,1,0:T(8,128)(2,1)S(1)} %get-tuple-element.82, bf16[1,4,2048,80]{3,2,1,0:T(8,128)(2,1)S(1)} %get-tuple-element.79), kind=kOutput, calls=%fused_computation.2 | convolution fusion | flops 5039718400 | bytes 22118400 | tf_op jit(solution)/shard_map/chre,hecd->rd/dot_general | solution.py:409
  412.0 9.6 %dynamic-slice_select_fusion = (bf16[2,1024,320]{1,2,0:T(8,128)(2,1)}, bf16[2,1024,320]{1,2,0:T(8,128)(2,1)}, bf16[2,1024,320]{1,2,0:T(8,128)(2,1)}, bf16[2,1024...) fusion(bf16[2,3072,320]{1,2,0:T(8,128)(2,1)S(1)} %fusion.20, ...), kind=kLoop, calls=%fused_computation.86 | loop fusion | flops 4587520 | bytes 18357276 | tf_op jit(solution)/shard_map/jit(_where)/select_n | solution.py:100
  423.0 7.6 collective-permute-start.4
  438.6 9.3 %collective-permute-done = bf16[2,1024,320]{1,2,0:T(8,128)(2,1)} collective-permute-done((bf16[2,1024,320]{1,2,0:T(8,128)(2,1)}, bf16[2,1024,320]{1,2,0:T(8,128)(2,1)}, u32[]{:S(2)}, u32[]{:S(2)}) %collective-permute-start) | collective-permute-done | bytes 1310752 | tf_op jit(solution)/shard_map/ppermute | solution.py:339
  447.9 24.3 %collective-permute-start.5 = (bf16[2,1024,320]{1,2,0:T(8,128)(2,1)}, bf16[2,1024,320]{1,2,0:T(8,128)(2,1)S(1)}, u32[]{:S(2)}, u32[]{:S(2)}) collective-permute-start(bf16[2,1024,320]{1,2,0:T(8,128)(2,1)} %get-tuple-element.72), channel_id=1, source_target_pairs={{0,24},{4,28},{8,0},{12,4},{16,8},{20,12},{24,16},{28,20},{1,25},{... | collective-permute-start | bytes 3932168 | tf_op jit(solution)/shard_map/ppermute | solution.py:339
  474.8 71.5 %collective-permute-done.1 = bf16[2,1024,320]{1,2,0:T(8,128)(2,1)} collective-permute-done((bf16[2,1024,320]{1,2,0:T(8,128)(2,1)}, bf16[2,1024,320]{1,2,0:T(8,128)(2,1)}, u32[]{:S(2)}, u32[]{:S(2)}) %collective-permute-start.1) | collective-permute-done | bytes 1310752 | tf_op jit(solution)/shard_map/ppermute | solution.py:339
  546.3 13.4 %collective-permute-start.6 = (bf16[2,1024,320]{1,2,0:T(8,128)(2,1)}, bf16[2,1024,320]{1,2,0:T(8,128)(2,1)S(1)}, u32[]{:S(2)}, u32[]{:S(2)}) collective-permute-start(bf16[2,1024,320]{1,2,0:T(8,128)(2,1)} %get-tuple-element.71), channel_id=1, source_target_pairs={{0,28},{4,0},{8,4},{12,8},{16,12},{20,16},{24,20},{28,24},{1,29},{... | collective-permute-start | bytes 3932168 | tf_op jit(solution)/shard_map/ppermute | solution.py:339
  562.2 61.2 %collective-permute-done.2 = bf16[2,1024,320]{1,2,0:T(8,128)(2,1)} collective-permute-done((bf16[2,1024,320]{1,2,0:T(8,128)(2,1)}, bf16[2,1024,320]{1,2,0:T(8,128)(2,1)}, u32[]{:S(2)}, u32[]{:S(2)}) %collective-permute-start.2) | collective-permute-done | bytes 1310752 | tf_op jit(solution)/shard_map/ppermute | solution.py:339
  638.5 6.2 fusion.21
  649.8 7.0 fusion.1
  657.0 14.9 %all-reduce.4 = f32[4,720]{1,0:T(4,128)S(1)} all-reduce(f32[4,720]{1,0:T(4,128)S(1)} %maximum_maximum_fusion), channel_id=4, replica_groups=mesh['dp'=8,'mp'=4] {'mp'}, use_global_device_ids=true, to_apply=%region_22.23.clone | all-reduce | flops 2880 | bytes 23040
  672.6 50.9 %psum.14 = f32[1,720]{1,0:T(1,128)S(1)} all-reduce(f32[1,720]{1,0:T(1,128)S(1)} %constant_dynamic-slice_fusion), channel_id=1, replica_groups=mesh['dp'=8,'mp'=4] {'dp'}, use_global_device_ids=true, to_apply=%region_23.24 | all-reduce | flops 720 | bytes 5760 | tf_op jit(solution)/shard_map/psum | solution.py:431
  730.4 67.1 %all-reduce.7.cloned.1.call-done = bf16[320,6,1280]{2,0,1:T(8,128)(2,1)} async-done(((bf16[320,6,1280]{2,0,1:T(8,128)(2,1)}), bf16[320,6,1280]{2,0,1:T(8,128)(2,1)}) %all-reduce.7.cloned.1.call-update) | async-done | bytes 4915216 | tf_op jit(solution)/shard_map/psum | solution.py:442
  (226 shorter events, 169.0 us)
Async XLA Ops:
  7.2 83.0 %copy-start = (bf16[320,3,1280]{2,0,1:T(8,128)(2,1)S(1)}, bf16[320,3,1280]{2,0,1:T(8,128)(2,1)}, u32[]{:S(2)}) copy-start(bf16[320,3,1280]{2,0,1:T(8,128)(2,1)} %param.21) | copy-start | bytes 7372804
  7.2 74.6 %all-gather.12.cloned.1.call-start = ((), (), s32[]{:S(2)}) async-start(), calls=%async_computation.10 | async-start | bytes 6656000 | tf_op jit(solution)/shard_map/all_gather | solution.py:319
  16.9 149.5 %all-gather.6.cloned.1.call-start = ((), (), s32[]{:S(2)}) async-start(), calls=%async_computation.4 | async-start | bytes 4096000 | tf_op jit(solution)/shard_map/all_gather | solution.py:296
  17.7 177.8 %all-gather.8.cloned.1.call-start = ((), (), s32[]{:S(2)}) async-start(), calls=%async_computation.5 | async-start | bytes 4096000 | tf_op jit(solution)/shard_map/all_gather | solution.py:297
  18.4 216.3 %all-gather.10.cloned.1.call-start = ((), (), s32[]{:S(2)}) async-start(), calls=%async_computation.6 | async-start | bytes 4096000 | tf_op jit(solution)/shard_map/all_gather | solution.py:298
  118.3 31.1 %copy-start.2 = (bf16[4,2048,80]{2,1,0:T(8,128)(2,1)}, bf16[4,2048,80]{2,1,0:T(8,128)(2,1)S(1)}, u32[]{:S(2)}) copy-start(bf16[4,2048,80]{2,1,0:T(8,128)(2,1)S(1)} %fusion.16.q_ref) | copy-start | bytes 3932164
  161.7 27.7 %all-to-all-start = ((bf16[4,512,320]{1,2,0:T(8,128)(2,1)}), bf16[4,512,320]{1,2,0:T(8,128)(2,1)}, u32[]{:S(2)}, u32[]{:S(2)}) async-start(bf16[4,512,320]{1,2,0:T(8,128)(2,1)} %copy.47), calls=%async_computation | async-start | bytes 2621440 | tf_op jit(solution)/shard_map/all_to_all | solution.py:354
  166.0 478.8 %reduce-scatter.5.cloned.1.call-start = ((), (), s32[]{:S(2)}) async-start(), calls=%async_computation.8 | async-start | bytes 12288000 | tf_op jit(solution)/shard_map/reduce_scatter | solution.py:439
  271.9 35.7 %all-to-all-start.1 = ((bf16[512,4,320]{0,2,1:T(8,128)(2,1)}), bf16[512,4,320]{0,2,1:T(8,128)(2,1)}, u32[]{:S(2)}, u32[]{:S(2)}) async-start(bf16[512,4,320]{0,2,1:T(8,128)(2,1)} %bitcast.165), calls=%async_computation.1 | async-start | bytes 2621440 | tf_op jit(solution)/shard_map/all_to_all | solution.py:379
  276.2 448.4 %reduce-scatter.3.cloned.1.call-start = ((), (), s32[]{:S(2)}) async-start(), calls=%async_computation.7 | async-start | bytes 6553600 | tf_op jit(solution)/shard_map/reduce_scatter | solution.py:412
  321.5 41.9 %copy-start.4 = (f32[2048,4,80]{2,0,1:T(8,128)S(1)}, f32[2048,4,80]{2,0,1:T(8,128)}, u32[]{:S(2)}) copy-start(f32[2048,4,80]{2,0,1:T(8,128)} %copy.43) | copy-start | bytes 7864324
  376.6 33.9 %copy-start.7 = (bf16[1,2048,320]{1,2,0:T(8,128)(2,1)S(1)}, bf16[1,2048,320]{1,2,0:T(8,128)(2,1)}, u32[]{:S(2)}) copy-start(bf16[1,2048,320]{1,2,0:T(8,128)(2,1)} %get-tuple-element.69) | copy-start | bytes 3932164
  376.6 420.9 %all-reduce.7.cloned.1.call-start = ((), (), s32[]{:S(2)}) async-start(), calls=%async_computation.9 | async-start | bytes 9830400 | tf_op jit(solution)/shard_map/psum | solution.py:442
  412.0 23.2 %copy-start.30 = (bf16[1280,1280]{1,0:T(8,128)(2,1)S(1)}, bf16[1280,1280]{1,0:T(8,128)(2,1)}, u32[]{:S(2)}) copy-start(bf16[1280,1280]{1,0:T(8,128)(2,1)} %all-gather.10.cloned.1.call-done) | copy-start | bytes 9830404
  412.0 23.2 %copy-start.36 = (f32[512,1280]{1,0:T(8,128)S(1)}, f32[512,1280]{1,0:T(8,128)}, u32[]{:S(2)}) copy-start(f32[512,1280]{1,0:T(8,128)} %copy-done.35) | copy-start | bytes 7864324
  421.6 26.3 %collective-permute-start = (bf16[2,1024,320]{1,2,0:T(8,128)(2,1)}, bf16[2,1024,320]{1,2,0:T(8,128)(2,1)}, u32[]{:S(2)}, u32[]{:S(2)}) collective-permute-start(bf16[2,1024,320]{1,2,0:T(8,128)(2,1)} %get-tuple-element.77), channel_id=1, source_target_pairs={{0,4},{4,8},{8,12},{12,16},{16,20},{20,24},{24,28},{28,0},{1,5},{5... | collective-permute-start | bytes 3932168 | tf_op jit(solution)/shard_map/ppermute | solution.py:339
  423.0 205.3 %collective-permute-start.4 = (bf16[2,1024,320]{1,2,0:T(8,128)(2,1)}, bf16[2,1024,320]{1,2,0:T(8,128)(2,1)S(1)}, u32[]{:S(2)}, u32[]{:S(2)}) collective-permute-start(bf16[2,1024,320]{1,2,0:T(8,128)(2,1)} %get-tuple-element.73), channel_id=1, source_target_pairs={{0,20},{4,24},{8,28},{12,0},{16,4},{20,8},{24,12},{28,16},{1,21},{... | collective-permute-start | bytes 3932168 | tf_op jit(solution)/shard_map/ppermute | solution.py:339
  430.6 195.2 %collective-permute-start.3 = (bf16[2,1024,320]{1,2,0:T(8,128)(2,1)}, bf16[2,1024,320]{1,2,0:T(8,128)(2,1)}, u32[]{:S(2)}, u32[]{:S(2)}) collective-permute-start(bf16[2,1024,320]{1,2,0:T(8,128)(2,1)} %get-tuple-element.74), channel_id=1, source_target_pairs={{0,16},{4,20},{8,24},{12,28},{16,0},{20,4},{24,8},{28,12},{1,17},{... | collective-permute-start | bytes 3932168 | tf_op jit(solution)/shard_map/ppermute | solution.py:339
  430.6 192.8 %collective-permute-start.2 = (bf16[2,1024,320]{1,2,0:T(8,128)(2,1)}, bf16[2,1024,320]{1,2,0:T(8,128)(2,1)}, u32[]{:S(2)}, u32[]{:S(2)}) collective-permute-start(bf16[2,1024,320]{1,2,0:T(8,128)(2,1)} %get-tuple-element.75), channel_id=1, source_target_pairs={{0,12},{4,16},{8,20},{12,24},{16,28},{20,0},{24,4},{28,8},{1,13},{... | collective-permute-start | bytes 3932168 | tf_op jit(solution)/shard_map/ppermute | solution.py:339
  430.6 115.6 %collective-permute-start.1 = (bf16[2,1024,320]{1,2,0:T(8,128)(2,1)}, bf16[2,1024,320]{1,2,0:T(8,128)(2,1)}, u32[]{:S(2)}, u32[]{:S(2)}) collective-permute-start(bf16[2,1024,320]{1,2,0:T(8,128)(2,1)} %get-tuple-element.76), channel_id=1, source_target_pairs={{0,8},{4,12},{8,16},{12,20},{16,24},{20,28},{24,0},{28,4},{1,9},{5... | collective-permute-start | bytes 3932168 | tf_op jit(solution)/shard_map/ppermute | solution.py:339
  447.9 181.6 %collective-permute-start.5 = (bf16[2,1024,320]{1,2,0:T(8,128)(2,1)}, bf16[2,1024,320]{1,2,0:T(8,128)(2,1)S(1)}, u32[]{:S(2)}, u32[]{:S(2)}) collective-permute-start(bf16[2,1024,320]{1,2,0:T(8,128)(2,1)} %get-tuple-element.72), channel_id=1, source_target_pairs={{0,24},{4,28},{8,0},{12,4},{16,8},{20,12},{24,16},{28,20},{1,25},{... | collective-permute-start | bytes 3932168 | tf_op jit(solution)/shard_map/ppermute | solution.py:339
  546.3 84.4 %collective-permute-start.6 = (bf16[2,1024,320]{1,2,0:T(8,128)(2,1)}, bf16[2,1024,320]{1,2,0:T(8,128)(2,1)S(1)}, u32[]{:S(2)}, u32[]{:S(2)}) collective-permute-start(bf16[2,1024,320]{1,2,0:T(8,128)(2,1)} %get-tuple-element.71), channel_id=1, source_target_pairs={{0,28},{4,0},{8,4},{12,8},{16,12},{20,16},{24,20},{28,24},{1,29},{... | collective-permute-start | bytes 3932168 | tf_op jit(solution)/shard_map/ppermute | solution.py:339
  649.8 74.8 %copy-start.5 = (bf16[512,1280]{1,0:T(8,128)(2,1)S(1)}, bf16[512,1280]{1,0:T(8,128)(2,1)}, u32[]{:S(2)}) copy-start(bf16[512,1280]{1,0:T(8,128)(2,1)} %param.15) | copy-start | bytes 3932164
  649.8 74.8 %copy-start.25 = (f32[1280]{0:T(1024)S(1)}, f32[1280]{0:T(1024)}, u32[]{:S(2)}) copy-start(f32[1280]{0:T(1024)} %copy-done.24) | copy-start | bytes 15364
  (31 other events, 187.3 us)
Sparse Core Ops, SparseCore 0:
  17.0 64.6 all-gather.11
  83.6 44.9 all-gather.5
  130.5 58.9 all-gather.7
  191.2 43.4 all-gather.9
  263.7 112.1 reduce-scatter.4
  378.7 63.0 reduce-scatter.2
  649.3 148.1 all-reduce.6

commit v4 on v3

--- a/solution.py
+++ b/solution.py
@@ -324,17 +324,18 @@
     normed_group = (inputs_group * inv_group * gain_first).astype(jnp.bfloat16)
     inputs = tokens.astype(jnp.float32)
     inv_one = lax.rsqrt(jnp.mean(inputs * inputs, axis=1, keepdims=True) + epsilon)
+    weight_heads = attention_in.reshape(heads_here, HD, 3, D)
     projected = jnp.einsum(
-        "rd,ucd->cru", normed_group, attention_in, preferred_element_type=jnp.float32
+        "rd,hecd->chre", normed_group, weight_heads, preferred_element_type=jnp.float32
     )
     dim_scale = scale_base / math.sqrt(HD) * jax.nn.softplus(query_scale)
-    query_raw = projected[0].reshape(group_rows, heads_here, HD).transpose(1, 0, 2)
+    query_raw = projected[0]
     queries = (query_raw * dim_scale).astype(jnp.bfloat16)
-    keys_group = projected[1].astype(jnp.bfloat16)
-    values_group = projected[2].astype(jnp.bfloat16)
-    kv_group = jnp.stack([keys_group, values_group])
+    keys = projected[1].astype(jnp.bfloat16)
+    values = projected[2].astype(jnp.bfloat16)
+    kv_rows = jnp.stack([keys, values]).transpose(0, 2, 1, 3).reshape(2, group_rows, width_here)
     groups = lax.axis_size("dp")
-    windows = send_windows(kv_group, send_first, send_len, my_group, groups)
+    windows = send_windows(kv_rows, send_first, send_len, my_group, groups)
     received = [windows[0]] + [
         lax.ppermute(
             windows[shift], "dp", [(r, (r + shift) % groups) for r in range(groups)]
@@ -343,16 +344,11 @@
     ]
     place_shift = (my_group - place_slot) % groups
     cache = place_slots(received, place_shift, place_start, place_len, group_rows)
-    keys = keys_group.reshape(group_rows, heads_here, HD).transpose(1, 0, 2)
-    values = values_group.reshape(group_rows, heads_here, HD).transpose(1, 0, 2)
     mixed, log_total = attention_forward(queries, keys, values, block_start, block_end)
-    att_group = jnp.where(
-        src_live[:, None],
-        mixed.transpose(1, 0, 2).reshape(group_rows, width_here),
-        jnp.zeros((), jnp.bfloat16),
-    )
-    att_rows = lax.all_to_all(att_group, "mp", split_axis=0, concat_axis=1, tiled=True)
-    branch = jnp.dot(att_rows, out_all, preferred_element_type=jnp.float32)
+    att_group = jnp.where(src_live[None, :, None], mixed, jnp.zeros((), jnp.bfloat16))
+    att_heads = lax.all_to_all(att_group, "mp", split_axis=1, concat_axis=0, tiled=True)
+    out_heads = out_all.reshape(NH, HD, D)
+    branch = jnp.einsum("hie,hed->id", att_heads, out_heads, preferred_element_type=jnp.float32)
     first_sum = inputs + branch
     inv_two = lax.rsqrt(jnp.mean(first_sum * first_sum, axis=1, keepdims=True) + epsilon)
     normed_two = (first_sum * inv_two * gain_second).astype(jnp.bfloat16)
@@ -373,15 +369,11 @@
         - first_sum * inv_two**3 * jnp.mean(scaled_two * first_sum, axis=1, keepdims=True)
     )
     branch_grad = first_grad.astype(jnp.bfloat16)
-    att_rows_grad = jnp.einsum(
-        "rd,ud->ru", branch_grad, out_all, preferred_element_type=jnp.float32
+    att_heads_grad = jnp.einsum(
+        "id,hed->hie", branch_grad, out_heads, preferred_element_type=jnp.float32
     ).astype(jnp.bfloat16)
-    grad_group = lax.all_to_all(att_rows_grad, "mp", split_axis=1, concat_axis=0, tiled=True)
-    grad_heads = (
-        jnp.where(src_live[:, None], grad_group, jnp.zeros((), jnp.bfloat16))
-        .reshape(group_rows, heads_here, HD)
-        .transpose(1, 0, 2)
-    )
+    grad_group = lax.all_to_all(att_heads_grad, "mp", split_axis=0, concat_axis=1, tiled=True)
+    grad_heads = jnp.where(src_live[None, :, None], grad_group, jnp.zeros((), jnp.bfloat16))
     query_scaled_grad, key_grad, value_grad = attention_backward(
         queries, keys, values, grad_heads, log_total, block_start, block_end
     )
@@ -402,7 +394,6 @@
             jnp.where(live_heads, value_grad, jnp.zeros((), jnp.bfloat16)),
         ]
     )
-    weight_heads = attention_in.reshape(heads_here, HD, 3, D)
     qkv_part = jnp.einsum(
         "chre,rd->hecd", proj_grad, normed_group, preferred_element_type=jnp.float32
     ).reshape(width_here, 3, D)
@@ -432,7 +423,9 @@
     gain_one_grad = small[0, :shard_width]
     gain_two_grad = small[0, shard_width : 2 * shard_width]
     query_scale_grad = small[0, 2 * shard_width :]
-    out_part = jnp.einsum("ru,rd->ud", att_rows, branch_grad, preferred_element_type=jnp.float32)
+    out_part = jnp.einsum(
+        "hie,id->hed", att_heads, branch_grad, preferred_element_type=jnp.float32
+    ).reshape(D, D)
     in_part = jnp.einsum("ru,rd->ud", preact_grad, normed_two, preferred_element_type=jnp.float32)
     down_part = jnp.einsum("ru,rd->ud", hidden, feed_grad, preferred_element_type=jnp.float32)
     row_terms = jnp.stack([out_part, in_part, down_part], axis=1)

time: 826 us -> 805 us (0.975)
  waiting for transfers between devices: 355 us -> 327 us
  blocking collectives: 65.8 us -> 92.8 us
  local copies, waits for them, and re-layouts: 79.9 us -> 69.2 us
    ppermute x7, waiting for transfers between devices: 142 us -> 106 us  [per_device(): lax.ppermute(windows[shift], 'dp', [(r, (r + shift) % groups) for r in ra...]
    psum x1, blocking collectives: 50.9 us -> 77.8 us  [per_device(): lax.psum(lax.psum_scatter(small, 'mp', scatter_dimension=0, tiled=True),...]
    convert_element_type x3 -> x0, local copies, waits for them, and re-layouts: 10 us -> none  [the longest x1 3.73 us: per_device(): keys_group = projected[1].astype(jnp.bfloat16)]
    all_to_all x2, waiting for transfers between devices: 53.8 us -> 63.7 us  [the longest x1 39 us: per_device(): lax.all_to_all(att_group, 'mp', split_axis=1, concat_axis=0, tiled=True)]
    select_n x1, local copies, waits for them, and re-layouts: 1.3 us -> 10.7 us  [per_device(): jnp.where(src_live[None, :, None], mixed, jnp.zeros((), jnp.bfloat16))]
    unnamed x87 -> x77, local copies, waits for them, and re-layouts: 21.3 us -> 20.1 us
  transfers between devices with their start and end apart: 16 -> 16, of which waited for: 8 -> 8; matrix products, arithmetic and copies ran while one was open for 20% -> 22% of each run, Pallas kernels for 9% -> 9%
where the time goes in v4:
time: 805 us; the launch traced here: 800 us
  waiting for transfers between devices  327 us (41%)
  blocking collectives  92.8 us (12%)
  other arithmetic  78.4 us (10%)
  Pallas kernels  72.7 us (9%)
  local copies, waits for them, and re-layouts  69.2 us (9%)
  matrix products  64.8 us (8%)
  starting transfers between devices  55.5 us (7%)
  between operations  39.4 us (5%)
    ppermute x7, waiting for transfers between devices, per_device(): lax.ppermute(windows[shift], 'dp', [(r, (r + shift) % groups) for r in ra...  106 us
    psum x1, blocking collectives, per_device(): lax.psum(lax.psum_scatter(small, 'mp', scatter_dimension=0, tiled=True),...  77.8 us
    psum x1, waiting for transfers between devices, per_device(): lax.psum(jnp.concatenate([qkv_part.astype(jnp.bfloat16), shares], axis=1)...  67.6 us
    all_gather x1, waiting for transfers between devices, per_device(): lax.all_gather(jnp.concatenate([tokens, gain_rows]), 'mp', axis=0, tiled=...  61.3 us
    ppermute x7, starting transfers between devices, per_device(): lax.ppermute(windows[shift], 'dp', [(r, (r + shift) % groups) for r in ra...  46.3 us
    pallas_call x1, Pallas kernels, attention_backward(): pl.pallas_call(attn_bwd_kernel, grid_spec=pltpu.PrefetchScalarGridSpec(nu...  41.8 us
    all_to_all x1, waiting for transfers between devices, per_device(): lax.all_to_all(att_group, 'mp', split_axis=1, concat_axis=0, tiled=True)  39 us
    pallas_call x1, Pallas kernels, attention_forward(): pl.pallas_call(attn_fwd_kernel, grid_spec=pltpu.PrefetchScalarGridSpec(nu...  30.9 us
  transfers between devices with their start and end apart: 16, of which 8 were waited for; matrix products, arithmetic and copies ran while one was open for 22% of the time, Pallas kernels for 9%

profile of v4, /device:TPU:0, one launch (start us, length us, event | category | flops | bytes accessed | tf_op | source)
XLA Modules:
  0.0 799.8 jit_solution(17310838975022238151)
XLA Ops:
  20.5 61.3 %all-gather.12.cloned.1.call-done = bf16[2080,1280]{1,0:T(8,128)(2,1)} async-done(((bf16[520,1280]{1,0:T(8,128)(2,1)}), bf16[2080,1280]{1,0:T(8,128)(2,1)}) %all-gather.12.cloned.1.call-update) | async-done | bytes 5324816 | tf_op jit(solution)/shard_map/all_gather | solution.py:319
  90.1 11.1 %convolution_bitcast_fusion = f32[3,4,2048,80]{3,2,1,0:T(8,128)} fusion(bf16[2048,1280,1,1]{1,0,2,3:T(8,128)(2,1)S(1)} %bitcast.182, bf16[4,80,3,1280]{3,1,0,2:T(8,128)(2,1)S(1)} %bitcast.167), kind=kOutput, calls=%fused_computation.21 | convolution fusion | flops 5033164800 | bytes 15564800 | tf_op jit(solution)/shard_map/rd,hecd->chre/dot_general | solution.py:328
  103.8 6.9 fusion.64
  110.7 30.9 %shard_map.186 = (bf16[4,2048,80]{2,1,0:T(8,128)(2,1)S(1)}, f32[4,2048,1]{2,1,0:T(8,128)}) custom-call(s32[16]{0:T(128)S(1)} %get-tuple-element.88.starts_ref, s32[16]{0:T(128)S(1)} %get-tuple-element.87.ends_ref, bf16[4,2048,80]{2,1,0:T(8,128)(2,1)S(1)} %multiply_convert_fusion.q_ref, bf16[4,2048,80]{2,1,0:T(8,128)(2,1)} %bitcast.180, ...), custom_call_target="tpu_custom_call" | custom-call | flops 2684354560 | bytes 5242880 | tf_op jit(solution)/shard_map/pallas_call | solution.py:233
  142.1 10.7 %copy.44 = bf16[4,2048,80]{2,0,1:T(4,128)(2,1)} copy(bf16[4,2048,80]{2,1,0:T(8,128)(2,1)S(1)} %broadcast_select_fusion.1) | data formatting | bytes 2621440 | tf_op jit(solution)/shard_map/jit(_where)/select_n | solution.py:348
  157.5 39.0 %all-to-all-done = bf16[4,2048,80]{2,0,1:T(4,128)(2,1)} async-done(((bf16[4,2048,80]{2,0,1:T(4,128)(2,1)}), bf16[4,2048,80]{2,0,1:T(4,128)(2,1)}, u32[]{:S(2)}, u32[]{:S(2)}) %all-to-all-start) | async-done | bytes 1310752 | tf_op jit(solution)/shard_map/all_to_all | solution.py:349
  200.8 6.2 multiply_reduce_fusion.2
  217.3 26.4 %all-gather.10.cloned.1.call-done = bf16[1280,1280]{1,0:T(8,128)(2,1)} async-done(((bf16[320,1280]{1,0:T(8,128)(2,1)}), bf16[1280,1280]{1,0:T(8,128)(2,1)}) %all-gather.10.cloned.1.call-update) | async-done | bytes 3276816 | tf_op jit(solution)/shard_map/all_gather | solution.py:298
  278.8 24.6 %all-to-all-done.1 = bf16[16,512,80]{1,2,0:T(8,128)(2,1)} async-done(((bf16[16,512,80]{1,2,0:T(8,128)(2,1)}), bf16[16,512,80]{1,2,0:T(8,128)(2,1)}, u32[]{:S(2)}, u32[]{:S(2)}) %all-to-all-start.1) | async-done | bytes 1310752 | tf_op jit(solution)/shard_map/all_to_all | solution.py:375
  310.2 41.8 %shard_map.187 = (bf16[4,2048,80]{2,1,0:T(8,128)(2,1)S(1)}, bf16[4,2048,80]{2,1,0:T(8,128)(2,1)S(1)}, bf16[4,2048,80]{2,1,0:T(8,128)(2,1)}) custom-call(s32[16]{0:T(128)S(1)} %get-tuple-element.88.starts_ref, s32[16]{0:T(128)S(1)} %get-tuple-element.87.ends_ref, bf16[4,2048,80]{2,1,0:T(8,128)(2,1)} %copy-done.2, bf16[4,2048,80]{2,1,0:T(8,128)(2,1)} %bitcast.181, ...), custom_call_target="tpu_custom_call" | custom-call | flops 6710886400 | bytes 9175040 | tf_op jit(solution)/shard_map/pallas_call | solution.py:260
  356.4 10.5 %bitcast_convert_fusion = (bf16[2048,1280]{1,0:T(8,128)(2,1)}, f32[2048,1280,1,1]{1,0,3,2:T(8,128)}) fusion(bf16[4,80,3,1280]{3,1,0,2:T(8,128)(2,1)S(1)} %bitcast.168, bf16[1,4,2048,80]{3,2,1,0:T(8,128)(2,1)S(1)} %get-tuple-element.84, bf16[1,4,2048,80]{3,2,1,0:T(8,128)(2,1)S(1)} %get-tuple-element.83, bf16[1,4,2048,80]{3,2,1,0:T(8,128)(2,1)S(1)} %get-tuple-element.78), kind=kOutput, calls=%fused_computation.12 | convolution fusion | flops 5039718400 | bytes 22118400 | tf_op jit(solution)/shard_map/chre,hecd->rd/dot_general | solution.py:400
  405.5 6.4 fusion.40
  411.9 6.8 collective-permute-start.1
  430.2 10.3 %collective-permute-done = bf16[2,1024,320]{1,2,0:T(8,128)(2,1)} collective-permute-done((bf16[2,1024,320]{1,2,0:T(8,128)(2,1)}, bf16[2,1024,320]{1,2,0:T(8,128)(2,1)}, u32[]{:S(2)}, u32[]{:S(2)}) %collective-permute-start) | collective-permute-done | bytes 1310752 | tf_op jit(solution)/shard_map/ppermute | solution.py:340
  440.5 10.1 %collective-permute-start.5 = (bf16[2,1024,320]{1,2,0:T(8,128)(2,1)S(1)}, bf16[2,1024,320]{1,2,0:T(8,128)(2,1)S(1)}, u32[]{:S(2)}, u32[]{:S(2)}) collective-permute-start(bf16[2,1024,320]{1,2,0:T(8,128)(2,1)S(1)} %copy-done.21), channel_id=1, source_target_pairs={{0,24},{4,28},{8,0},{12,4},{16,8},{20,12},{24,16},{28,20},{1,25},{... | collective-permute-start | bytes 3932168 | tf_op jit(solution)/shard_map/ppermute | solution.py:340
  453.1 25.2 %collective-permute-start.6 = (bf16[2,1024,320]{1,2,0:T(8,128)(2,1)S(1)}, bf16[2,1024,320]{1,2,0:T(8,128)(2,1)S(1)}, u32[]{:S(2)}, u32[]{:S(2)}) collective-permute-start(bf16[2,1024,320]{1,2,0:T(8,128)(2,1)S(1)} %copy-done.20), channel_id=1, source_target_pairs={{0,28},{4,0},{8,4},{12,8},{16,12},{20,16},{24,20},{28,24},{1,29},{... | collective-permute-start | bytes 3932168 | tf_op jit(solution)/shard_map/ppermute | solution.py:340
  480.8 76.5 %collective-permute-done.2 = bf16[2,1024,320]{1,2,0:T(8,128)(2,1)} collective-permute-done((bf16[2,1024,320]{1,2,0:T(8,128)(2,1)}, bf16[2,1024,320]{1,2,0:T(8,128)(2,1)}, u32[]{:S(2)}, u32[]{:S(2)}) %collective-permute-start.2) | collective-permute-done | bytes 1310752 | tf_op jit(solution)/shard_map/ppermute | solution.py:340
  566.1 19.0 %collective-permute-done.6 = bf16[2,1024,320]{1,2,0:T(8,128)(2,1)S(1)} collective-permute-done((bf16[2,1024,320]{1,2,0:T(8,128)(2,1)S(1)}, bf16[2,1024,320]{1,2,0:T(8,128)(2,1)S(1)}, u32[]{:S(2)}, u32[]{:S(2)}) %collective-permute-start.6) | collective-permute-done | bytes 1310752 | tf_op jit(solution)/shard_map/ppermute | solution.py:340
  589.5 6.7 fusion.6
  596.3 7.3 fusion.14
  608.7 5.8 fusion.25
  614.6 15.0 %all-reduce.4 = f32[4,720]{1,0:T(4,128)S(1)} all-reduce(f32[4,720]{1,0:T(4,128)S(1)} %maximum_maximum_fusion), channel_id=4, replica_groups=mesh['dp'=8,'mp'=4] {'mp'}, use_global_device_ids=true, to_apply=%region_22.23.clone | all-reduce | flops 2880 | bytes 23040
  630.3 77.8 %psum.14 = f32[1,720]{1,0:T(1,128)S(1)} all-reduce(f32[1,720]{1,0:T(1,128)S(1)} %constant_dynamic-slice_fusion), channel_id=1, replica_groups=mesh['dp'=8,'mp'=4] {'dp'}, use_global_device_ids=true, to_apply=%region_23.24 | all-reduce | flops 720 | bytes 5760 | tf_op jit(solution)/shard_map/psum | solution.py:422
  715.0 67.6 %all-reduce.7.cloned.1.call-done = bf16[320,6,1280]{2,0,1:T(8,128)(2,1)} async-done(((bf16[320,6,1280]{2,0,1:T(8,128)(2,1)}), bf16[320,6,1280]{2,0,1:T(8,128)(2,1)}) %all-reduce.7.cloned.1.call-update) | async-done | bytes 4915216 | tf_op jit(solution)/shard_map/psum | solution.py:435
  (206 shorter events, 156.3 us)
Async XLA Ops:
  7.2 82.9 %copy-start = (bf16[320,3,1280]{2,0,1:T(8,128)(2,1)S(1)}, bf16[320,3,1280]{2,0,1:T(8,128)(2,1)}, u32[]{:S(2)}) copy-start(bf16[320,3,1280]{2,0,1:T(8,128)(2,1)} %param.21) | copy-start | bytes 7372804
  7.2 74.6 %all-gather.12.cloned.1.call-start = ((), (), s32[]{:S(2)}) async-start(), calls=%async_computation.10 | async-start | bytes 6656000 | tf_op jit(solution)/shard_map/all_gather | solution.py:319
  16.9 183.9 %all-gather.6.cloned.1.call-start = ((), (), s32[]{:S(2)}) async-start(), calls=%async_computation.4 | async-start | bytes 4096000 | tf_op jit(solution)/shard_map/all_gather | solution.py:296
  17.7 189.3 %all-gather.8.cloned.1.call-start = ((), (), s32[]{:S(2)}) async-start(), calls=%async_computation.5 | async-start | bytes 4096000 | tf_op jit(solution)/shard_map/all_gather | solution.py:297
  18.4 225.3 %all-gather.10.cloned.1.call-start = ((), (), s32[]{:S(2)}) async-start(), calls=%async_computation.6 | async-start | bytes 4096000 | tf_op jit(solution)/shard_map/all_gather | solution.py:298
  152.8 43.7 %all-to-all-start = ((bf16[4,2048,80]{2,0,1:T(4,128)(2,1)}), bf16[4,2048,80]{2,0,1:T(4,128)(2,1)}, u32[]{:S(2)}, u32[]{:S(2)}) async-start(bf16[4,2048,80]{2,0,1:T(4,128)(2,1)} %copy.44), calls=%async_computation | async-start | bytes 4194304 | tf_op jit(solution)/shard_map/all_to_all | solution.py:349
  157.3 446.3 %reduce-scatter.5.cloned.1.call-start = ((), (), s32[]{:S(2)}) async-start(), calls=%async_computation.8 | async-start | bytes 12288000 | tf_op jit(solution)/shard_map/reduce_scatter | solution.py:432
  267.6 35.8 %all-to-all-start.1 = ((bf16[16,512,80]{1,2,0:T(8,128)(2,1)}), bf16[16,512,80]{1,2,0:T(8,128)(2,1)}, u32[]{:S(2)}, u32[]{:S(2)}) async-start(bf16[16,512,80]{1,2,0:T(8,128)(2,1)} %fusion.30), calls=%async_computation.1 | async-start | bytes 2621440 | tf_op jit(solution)/shard_map/all_to_all | solution.py:375
  271.9 437.4 %reduce-scatter.3.cloned.1.call-start = ((), (), s32[]{:S(2)}) async-start(), calls=%async_computation.7 | async-start | bytes 6553600 | tf_op jit(solution)/shard_map/reduce_scatter | solution.py:403
  366.9 14.7 %copy-start.29 = (u32[32]{0:T(128)S(1)}, u32[32]{0:T(128)}, u32[]{:S(2)}) copy-start(u32[32]{0:T(128)} %constant.234) | copy-start | bytes 388
  366.9 29.1 %copy-start.7 = (bf16[1,4,2048,80]{3,2,1,0:T(8,128)(2,1)S(1)}, bf16[1,4,2048,80]{3,2,1,0:T(8,128)(2,1)}, u32[]{:S(2)}) copy-start(bf16[1,4,2048,80]{3,2,1,0:T(8,128)(2,1)} %get-tuple-element.62) | copy-start | bytes 3932164
  366.9 415.6 %all-reduce.7.cloned.1.call-start = ((), (), s32[]{:S(2)}) async-start(), calls=%async_computation.9 | async-start | bytes 9830400 | tf_op jit(solution)/shard_map/psum | solution.py:435
  405.5 20.8 %copy-start.31 = (f32[512,1280]{1,0:T(8,128)S(1)}, f32[512,1280]{1,0:T(8,128)}, u32[]{:S(2)}) copy-start(f32[512,1280]{1,0:T(8,128)} %copy-done.30) | copy-start | bytes 7864324
  411.9 28.6 %collective-permute-start = (bf16[2,1024,320]{1,2,0:T(8,128)(2,1)}, bf16[2,1024,320]{1,2,0:T(8,128)(2,1)}, u32[]{:S(2)}, u32[]{:S(2)}) collective-permute-start(bf16[2,1024,320]{1,2,0:T(8,128)(2,1)} %get-tuple-element.72), channel_id=1, source_target_pairs={{0,4},{4,8},{8,12},{12,16},{16,20},{20,24},{24,28},{28,0},{1,5},{5... | collective-permute-start | bytes 3932168 | tf_op jit(solution)/shard_map/ppermute | solution.py:340
  411.9 41.2 %collective-permute-start.1 = (bf16[2,1024,320]{1,2,0:T(8,128)(2,1)}, bf16[2,1024,320]{1,2,0:T(8,128)(2,1)}, u32[]{:S(2)}, u32[]{:S(2)}) collective-permute-start(bf16[2,1024,320]{1,2,0:T(8,128)(2,1)} %get-tuple-element.73), channel_id=1, source_target_pairs={{0,8},{4,12},{8,16},{12,20},{16,24},{20,28},{24,0},{28,4},{1,9},{5... | collective-permute-start | bytes 3932168 | tf_op jit(solution)/shard_map/ppermute | solution.py:340
  418.7 138.7 %collective-permute-start.2 = (bf16[2,1024,320]{1,2,0:T(8,128)(2,1)}, bf16[2,1024,320]{1,2,0:T(8,128)(2,1)}, u32[]{:S(2)}, u32[]{:S(2)}) collective-permute-start(bf16[2,1024,320]{1,2,0:T(8,128)(2,1)} %get-tuple-element.74), channel_id=1, source_target_pairs={{0,12},{4,16},{8,20},{12,24},{16,28},{20,0},{24,4},{28,8},{1,13},{... | collective-permute-start | bytes 3932168 | tf_op jit(solution)/shard_map/ppermute | solution.py:340
  420.4 139.6 %collective-permute-start.3 = (bf16[2,1024,320]{1,2,0:T(8,128)(2,1)}, bf16[2,1024,320]{1,2,0:T(8,128)(2,1)}, u32[]{:S(2)}, u32[]{:S(2)}) collective-permute-start(bf16[2,1024,320]{1,2,0:T(8,128)(2,1)} %get-tuple-element.75), channel_id=1, source_target_pairs={{0,16},{4,20},{8,24},{12,28},{16,0},{20,4},{24,8},{28,12},{1,17},{... | collective-permute-start | bytes 3932168 | tf_op jit(solution)/shard_map/ppermute | solution.py:340
  420.4 142.0 %collective-permute-start.4 = (bf16[2,1024,320]{1,2,0:T(8,128)(2,1)}, bf16[2,1024,320]{1,2,0:T(8,128)(2,1)}, u32[]{:S(2)}, u32[]{:S(2)}) collective-permute-start(bf16[2,1024,320]{1,2,0:T(8,128)(2,1)} %get-tuple-element.76), channel_id=1, source_target_pairs={{0,20},{4,24},{8,28},{12,0},{16,4},{20,8},{24,12},{28,16},{1,21},{... | collective-permute-start | bytes 3932168 | tf_op jit(solution)/shard_map/ppermute | solution.py:340
  430.1 23.0 %copy-start.20 = (bf16[2,1024,320]{1,2,0:T(8,128)(2,1)S(1)}, bf16[2,1024,320]{1,2,0:T(8,128)(2,1)}, u32[]{:S(2)}) copy-start(bf16[2,1024,320]{1,2,0:T(8,128)(2,1)} %get-tuple-element.71) | copy-start | bytes 3932164
  440.5 124.5 %collective-permute-start.5 = (bf16[2,1024,320]{1,2,0:T(8,128)(2,1)S(1)}, bf16[2,1024,320]{1,2,0:T(8,128)(2,1)S(1)}, u32[]{:S(2)}, u32[]{:S(2)}) collective-permute-start(bf16[2,1024,320]{1,2,0:T(8,128)(2,1)S(1)} %copy-done.21), channel_id=1, source_target_pairs={{0,24},{4,28},{8,0},{12,4},{16,8},{20,12},{24,16},{28,20},{1,25},{... | collective-permute-start | bytes 3932168 | tf_op jit(solution)/shard_map/ppermute | solution.py:340
  453.1 132.1 %collective-permute-start.6 = (bf16[2,1024,320]{1,2,0:T(8,128)(2,1)S(1)}, bf16[2,1024,320]{1,2,0:T(8,128)(2,1)S(1)}, u32[]{:S(2)}, u32[]{:S(2)}) collective-permute-start(bf16[2,1024,320]{1,2,0:T(8,128)(2,1)S(1)} %copy-done.20), channel_id=1, source_target_pairs={{0,28},{4,0},{8,4},{12,8},{16,12},{20,16},{24,20},{28,24},{1,29},{... | collective-permute-start | bytes 3932168 | tf_op jit(solution)/shard_map/ppermute | solution.py:340
  557.4 32.1 %slice-start = ((s8[5324800]{0:T(1024)(128)(4,1)}), s8[4194304]{0:T(1024)(128)(4,1)S(1)}, s32[]{:S(2)}) async-start(s8[5324800]{0:T(1024)(128)(4,1)} %bitcast.172), calls=%async_computation.11 | async-start | bytes 8388608
  565.0 24.5 %slice-start.1 = ((s8[5324800]{0:T(1024)(128)(4,1)}), s8[1130496]{0:T(1024)(128)(4,1)S(1)}, s32[]{:S(2)}) async-start(s8[5324800]{0:T(1024)(128)(4,1)} %bitcast.172), calls=%async_computation.12 | async-start | bytes 2260992
  608.7 100.6 %copy-start.4 = (bf16[512,1280]{1,0:T(8,128)(2,1)S(1)}, bf16[512,1280]{1,0:T(8,128)(2,1)}, u32[]{:S(2)}) copy-start(bf16[512,1280]{1,0:T(8,128)(2,1)} %param.15) | copy-start | bytes 3932164
  (26 other events, 130.9 us)
Sparse Core Ops, SparseCore 0:
  17.0 64.6 all-gather.11
  83.6 44.9 all-gather.5
  130.5 66.1 all-gather.7
  198.3 45.3 all-gather.9
  261.8 112.1 reduce-scatter.4
  376.8 61.3 reduce-scatter.2
  608.8 173.7 all-reduce.6

commit v5 on v4

--- a/solution.py
+++ b/solution.py
@@ -333,7 +333,9 @@
     queries = (query_raw * dim_scale).astype(jnp.bfloat16)
     keys = projected[1].astype(jnp.bfloat16)
     values = projected[2].astype(jnp.bfloat16)
-    kv_rows = jnp.stack([keys, values]).transpose(0, 2, 1, 3).reshape(2, group_rows, width_here)
+    mixed, log_total = attention_forward(queries, keys, values, block_start, block_end)
+    kv_heads, mixed = lax.optimization_barrier((jnp.stack([keys, values]), mixed))
+    kv_rows = kv_heads.transpose(0, 2, 1, 3).reshape(2, group_rows, width_here)
     groups = lax.axis_size("dp")
     windows = send_windows(kv_rows, send_first, send_len, my_group, groups)
     received = [windows[0]] + [
@@ -344,7 +346,6 @@
     ]
     place_shift = (my_group - place_slot) % groups
     cache = place_slots(received, place_shift, place_start, place_len, group_rows)
-    mixed, log_total = attention_forward(queries, keys, values, block_start, block_end)
     att_group = jnp.where(src_live[None, :, None], mixed, jnp.zeros((), jnp.bfloat16))
     att_heads = lax.all_to_all(att_group, "mp", split_axis=1, concat_axis=0, tiled=True)
     out_heads = out_all.reshape(NH, HD, D)
@@ -387,18 +388,21 @@
         * jax.nn.sigmoid(query_scale)
     )
     query_grad = (query_scaled_grad * dim_scale).astype(jnp.bfloat16)
-    proj_grad = jnp.stack(
+    proj_grad = (
+        query_grad,
+        jnp.where(live_heads, key_grad, jnp.zeros((), jnp.bfloat16)),
+        jnp.where(live_heads, value_grad, jnp.zeros((), jnp.bfloat16)),
+    )
+    qkv_part = jnp.stack(
         [
-            query_grad,
-            jnp.where(live_heads, key_grad, jnp.zeros((), jnp.bfloat16)),
-            jnp.where(live_heads, value_grad, jnp.zeros((), jnp.bfloat16)),
-        ]
-    )
-    qkv_part = jnp.einsum(
-        "chre,rd->hecd", proj_grad, normed_group, preferred_element_type=jnp.float32
+            jnp.einsum("hre,rd->hed", g, normed_group, preferred_element_type=jnp.float32)
+            for g in proj_grad
+        ],
+        axis=2,
     ).reshape(width_here, 3, D)
-    normed_one_part = jnp.einsum(
-        "chre,hecd->rd", proj_grad, weight_heads, preferred_element_type=jnp.float32
+    normed_one_part = sum(
+        jnp.einsum("hre,hed->rd", g, weight_heads[:, :, c], preferred_element_type=jnp.float32)
+        for c, g in enumerate(proj_grad)
     )
     normed_one_grad = lax.psum_scatter(
         normed_one_part.astype(jnp.bfloat16), "mp", scatter_dimension=0, tiled=True

time: 805 us -> 842 us (1.046)
  matrix products: 64.8 us -> 84.3 us
  local copies, waits for them, and re-layouts: 69.2 us -> 78.3 us
    dot_general x2 -> x6, matrix products: 17.8 us -> 40.9 us  [the longest x3 26.9 us: per_device(): jnp.einsum('hre,hed->rd', g, weight_heads[:, :, c], preferred_element_typ...]
    dot_general x0 -> x3, local copies, waits for them, and re-layouts: none -> 10 us  [per_device(): jnp.einsum('hre,rd->hed', g, normed_group, preferred_element_type=jnp.flo...]
    unnamed x77 -> x91, local copies, waits for them, and re-layouts: 20.1 us -> 24.1 us
  transfers between devices with their start and end apart: 16 -> 16, of which waited for: 8 -> 8; matrix products, arithmetic and copies ran while one was open for 22% -> 24% of each run, Pallas kernels for 9% -> 9%
where the time goes in v5:
time: 842 us; the launch traced here: 831 us
  waiting for transfers between devices  329 us (39%)
  blocking collectives  93.6 us (11%)
  matrix products  84.3 us (10%)
  other arithmetic  79.6 us (9%)
  local copies, waits for them, and re-layouts  78.3 us (9%)
  Pallas kernels  73.8 us (9%)
  starting transfers between devices  53.2 us (6%)
  between operations  39.7 us (5%)
    ppermute x7, waiting for transfers between devices, per_device(): lax.ppermute(windows[shift], 'dp', [(r, (r + shift) % groups) for r in ra...  107 us
    psum x1, blocking collectives, per_device(): lax.psum(lax.psum_scatter(small, 'mp', scatter_dimension=0, tiled=True),...  78.6 us
    psum x1, waiting for transfers between devices, per_device(): lax.psum(jnp.concatenate([qkv_part.astype(jnp.bfloat16), shares], axis=1)...  66.2 us
    all_gather x1, waiting for transfers between devices, per_device(): lax.all_gather(jnp.concatenate([tokens, gain_rows]), 'mp', axis=0, tiled=...  61.3 us
    ppermute x7, starting transfers between devices, per_device(): lax.ppermute(windows[shift], 'dp', [(r, (r + shift) % groups) for r in ra...  45.8 us
    pallas_call x1, Pallas kernels, attention_backward(): pl.pallas_call(attn_bwd_kernel, grid_spec=pltpu.PrefetchScalarGridSpec(nu...  42 us
    all_to_all x1, waiting for transfers between devices, per_device(): lax.all_to_all(att_group, 'mp', split_axis=1, concat_axis=0, tiled=True)  39 us
    pallas_call x1, Pallas kernels, attention_forward(): pl.pallas_call(attn_fwd_kernel, grid_spec=pltpu.PrefetchScalarGridSpec(nu...  31.8 us
  transfers between devices with their start and end apart: 16, of which 8 were waited for; matrix products, arithmetic and copies ran while one was open for 24% of the time, Pallas kernels for 9%

profile of v5, /device:TPU:0, one launch (start us, length us, event | category | flops | bytes accessed | tf_op | source)
XLA Modules:
  0.0 831.4 jit_solution(3170532117127114211)
XLA Ops:
  20.3 61.3 %all-gather.12.cloned.1.call-done = bf16[2080,1280]{1,0:T(8,128)(2,1)} async-done(((bf16[520,1280]{1,0:T(8,128)(2,1)}), bf16[2080,1280]{1,0:T(8,128)(2,1)}) %all-gather.12.cloned.1.call-update) | async-done | bytes 5324816 | tf_op jit(solution)/shard_map/all_gather | solution.py:319
  90.1 8.4 %convolution_bitcast_fusion = f32[3,4,2048,80]{3,2,1,0:T(8,128)S(1)} fusion(bf16[2048,1280,1,1]{1,0,2,3:T(8,128)(2,1)S(1)} %bitcast.192, bf16[4,80,3,1280]{3,1,0,2:T(8,128)(2,1)S(1)} %bitcast.204), kind=kOutput, calls=%fused_computation.15 | convolution fusion | flops 5033164800 | bytes 15564800 | tf_op jit(solution)/shard_map/rd,hecd->chre/dot_general | solution.py:328
  104.3 31.8 %shard_map.186 = (bf16[4,2048,80]{2,1,0:T(8,128)(2,1)S(1)}, f32[4,2048,1]{2,1,0:T(8,128)}) custom-call(s32[16]{0:T(128)S(1)} %get-tuple-element.92.starts_ref, s32[16]{0:T(128)S(1)} %get-tuple-element.91.ends_ref, bf16[4,2048,80]{2,1,0:T(8,128)(2,1)S(1)} %multiply_convert_fusion.1.q_ref, bf16[4,2048,80]{2,1,0:T(8,128)(2,1)} %bitcast.188, ...), custom_call_target="tpu_custom_call" | custom-call | flops 2684354560 | bytes 5242880 | tf_op jit(solution)/shard_map/pallas_call | solution.py:233
  139.5 10.7 %copy.53 = bf16[4,2048,80]{2,0,1:T(4,128)(2,1)} copy(bf16[4,2048,80]{2,1,0:T(8,128)(2,1)S(1)} %broadcast_select_fusion.3) | data formatting | bytes 2621440 | tf_op jit(solution)/shard_map/jit(_where)/select_n | solution.py:349
  154.1 39.0 %all-to-all-done = bf16[4,2048,80]{2,0,1:T(4,128)(2,1)S(1)} async-done(((bf16[4,2048,80]{2,0,1:T(4,128)(2,1)}), bf16[4,2048,80]{2,0,1:T(4,128)(2,1)S(1)}, u32[]{:S(2)}, u32[]{:S(2)}) %all-to-all-start) | async-done | bytes 1310752 | tf_op jit(solution)/shard_map/all_to_all | solution.py:350
  195.8 5.8 multiply_reduce_fusion.3
  212.1 29.8 %all-gather.10.cloned.1.call-done = bf16[1280,1280]{1,0:T(8,128)(2,1)} async-done(((bf16[320,1280]{1,0:T(8,128)(2,1)}), bf16[1280,1280]{1,0:T(8,128)(2,1)}) %all-gather.10.cloned.1.call-update) | async-done | bytes 3276816 | tf_op jit(solution)/shard_map/all_gather | solution.py:298
  268.6 7.3 slice_convert_fusion
  275.9 24.1 %all-to-all-done.1 = bf16[16,512,80]{1,2,0:T(8,128)(2,1)S(1)} async-done(((bf16[16,512,80]{1,2,0:T(8,128)(2,1)}), bf16[16,512,80]{1,2,0:T(8,128)(2,1)S(1)}, u32[]{:S(2)}, u32[]{:S(2)}) %all-to-all-start.1) | async-done | bytes 1310752 | tf_op jit(solution)/shard_map/all_to_all | solution.py:376
  305.6 42.0 %shard_map.187 = (bf16[4,2048,80]{2,1,0:T(8,128)(2,1)S(1)}, bf16[4,2048,80]{2,1,0:T(8,128)(2,1)S(1)}, bf16[4,2048,80]{2,1,0:T(8,128)(2,1)}) custom-call(s32[16]{0:T(128)S(1)} %get-tuple-element.92.starts_ref, s32[16]{0:T(128)S(1)} %get-tuple-element.91.ends_ref, bf16[4,2048,80]{2,1,0:T(8,128)(2,1)} %copy-done.2, bf16[4,2048,80]{2,1,0:T(8,128)(2,1)} %bitcast.189, ...), custom_call_target="tpu_custom_call" | custom-call | flops 6710886400 | bytes 9175040 | tf_op jit(solution)/shard_map/pallas_call | solution.py:260
  347.6 6.1 fusion.37
  353.7 6.1 fusion.22
  359.7 14.8 %fusion.1 = (f32[1280]{0:T(1024)S(1)}, bf16[2048,1280]{1,0:T(8,128)(2,1)}) fusion(f32[4,512,1280]{2,1,0:T(8,128)} %slice_convert_fusion, f32[2048]{0:T(1024)S(1)} %bitcast.208, bf16[4,80,3,1280]{3,1,0,2:T(8,128)(2,1)S(1)} %bitcast.207, bf16[4,2048,80]{2,1,0:T(8,128)(2,1)S(1)} %copy-done.12, pred[2048]{0:T(1024)(128)(4,1)S(1)} %fusion.44, ...), kind=kOutput, calls=%fused_computation.3 | convolution fusion | flops 1694104320 | bytes 39631872 | tf_op jit(solution)/shard_map/hre,hed->rd/dot_general | solution.py:404
  410.5 6.1 copy.62
  416.6 9.2 %fusion.34 = (bf16[2,1024,320]{1,2,0:T(8,128)(2,1)}, bf16[2,1024,320]{1,2,0:T(8,128)(2,1)}, bf16[2,1024,320]{1,2,0:T(8,128)(2,1)}, bf16[2,1024,320]{1,2,0:T(8,12...) fusion(s32[]{:T(128)S(6)} %select_n.308, bf16[2,2048,320]{1,2,0:T(8,128)(2,1)} %bitcast.183, ...), kind=kLoop, calls=%fused_computation.92 | loop fusion | flops 3932160 | bytes 10491928 | tf_op jit(solution)/shard_map/jit(_where)/select_n | solution.py:100
  425.8 7.4 collective-permute-start.1
  444.0 10.5 %collective-permute-done = bf16[2,1024,320]{1,2,0:T(8,128)(2,1)} collective-permute-done((bf16[2,1024,320]{1,2,0:T(8,128)(2,1)}, bf16[2,1024,320]{1,2,0:T(8,128)(2,1)}, u32[]{:S(2)}, u32[]{:S(2)}) %collective-permute-start) | collective-permute-done | bytes 1310752 | tf_op jit(solution)/shard_map/ppermute | solution.py:342
  454.5 9.8 %collective-permute-start.5 = (bf16[2,1024,320]{1,2,0:T(8,128)(2,1)}, bf16[2,1024,320]{1,2,0:T(8,128)(2,1)S(1)}, u32[]{:S(2)}, u32[]{:S(2)}) collective-permute-start(bf16[2,1024,320]{1,2,0:T(8,128)(2,1)} %fusion.33), channel_id=1, source_target_pairs={{0,24},{4,28},{8,0},{12,4},{16,8},{20,12},{24,16},{28,20},{1,25},{... | collective-permute-start | bytes 3932168 | tf_op jit(solution)/shard_map/ppermute | solution.py:342
  466.9 25.0 %collective-permute-start.6 = (bf16[2,1024,320]{1,2,0:T(8,128)(2,1)S(1)}, bf16[2,1024,320]{1,2,0:T(8,128)(2,1)S(1)}, u32[]{:S(2)}, u32[]{:S(2)}) collective-permute-start(bf16[2,1024,320]{1,2,0:T(8,128)(2,1)S(1)} %copy-done.20), channel_id=1, source_target_pairs={{0,28},{4,0},{8,4},{12,8},{16,12},{20,16},{24,20},{28,24},{1,29},{... | collective-permute-start | bytes 3932168 | tf_op jit(solution)/shard_map/ppermute | solution.py:342
  494.4 76.9 %collective-permute-done.2 = bf16[2,1024,320]{1,2,0:T(8,128)(2,1)} collective-permute-done((bf16[2,1024,320]{1,2,0:T(8,128)(2,1)}, bf16[2,1024,320]{1,2,0:T(8,128)(2,1)}, u32[]{:S(2)}, u32[]{:S(2)}) %collective-permute-start.2) | collective-permute-done | bytes 1310752 | tf_op jit(solution)/shard_map/ppermute | solution.py:342
  580.0 19.2 %collective-permute-done.6 = bf16[2,1024,320]{1,2,0:T(8,128)(2,1)S(1)} collective-permute-done((bf16[2,1024,320]{1,2,0:T(8,128)(2,1)S(1)}, bf16[2,1024,320]{1,2,0:T(8,128)(2,1)S(1)}, u32[]{:S(2)}, u32[]{:S(2)}) %collective-permute-start.6) | collective-permute-done | bytes 1310752 | tf_op jit(solution)/shard_map/ppermute | solution.py:342
  646.6 15.0 %all-reduce.4 = f32[4,720]{1,0:T(4,128)S(1)} all-reduce(f32[4,720]{1,0:T(4,128)S(1)} %maximum_maximum_fusion), channel_id=4, replica_groups=mesh['dp'=8,'mp'=4] {'mp'}, use_global_device_ids=true, to_apply=%region_22.23.clone | all-reduce | flops 2880 | bytes 23040
  662.3 78.6 %psum.14 = f32[1,720]{1,0:T(1,128)S(1)} all-reduce(f32[1,720]{1,0:T(1,128)S(1)} %constant_dynamic-slice_fusion), channel_id=1, replica_groups=mesh['dp'=8,'mp'=4] {'dp'}, use_global_device_ids=true, to_apply=%region_23.24 | all-reduce | flops 720 | bytes 5760 | tf_op jit(solution)/shard_map/psum | solution.py:426
  747.8 66.2 %all-reduce.7.cloned.1.call-done = bf16[320,6,1280]{2,0,1:T(8,128)(2,1)} async-done(((bf16[320,6,1280]{2,0,1:T(8,128)(2,1)}), bf16[320,6,1280]{2,0,1:T(8,128)(2,1)}) %all-reduce.7.cloned.1.call-update) | async-done | bytes 4915216 | tf_op jit(solution)/shard_map/psum | solution.py:439
  (227 shorter events, 180.7 us)
Async XLA Ops:
  7.2 74.4 %all-gather.12.cloned.1.call-start = ((), (), s32[]{:S(2)}) async-start(), calls=%async_computation.10 | async-start | bytes 6656000 | tf_op jit(solution)/shard_map/all_gather | solution.py:319
  16.8 179.0 %all-gather.6.cloned.1.call-start = ((), (), s32[]{:S(2)}) async-start(), calls=%async_computation.4 | async-start | bytes 4096000 | tf_op jit(solution)/shard_map/all_gather | solution.py:296
  17.5 184.2 %all-gather.8.cloned.1.call-start = ((), (), s32[]{:S(2)}) async-start(), calls=%async_computation.5 | async-start | bytes 4096000 | tf_op jit(solution)/shard_map/all_gather | solution.py:297
  18.2 223.6 %all-gather.10.cloned.1.call-start = ((), (), s32[]{:S(2)}) async-start(), calls=%async_computation.6 | async-start | bytes 4096000 | tf_op jit(solution)/shard_map/all_gather | solution.py:298
  101.9 34.3 %copy-start.2 = (bf16[4,2048,80]{2,1,0:T(8,128)(2,1)}, bf16[4,2048,80]{2,1,0:T(8,128)(2,1)S(1)}, u32[]{:S(2)}) copy-start(bf16[4,2048,80]{2,1,0:T(8,128)(2,1)S(1)} %multiply_convert_fusion.1.q_ref) | copy-start | bytes 3932164
  104.3 31.8 %copy-start.10 = (bf16[1,4,2048,80]{3,2,1,0:T(8,128)(2,1)S(1)}, bf16[1,4,2048,80]{3,2,1,0:T(8,128)(2,1)}, u32[]{:S(2)}) copy-start(bf16[1,4,2048,80]{3,2,1,0:T(8,128)(2,1)} %get-tuple-element.66) | copy-start | bytes 3932164
  104.3 31.8 %copy-start.11 = (bf16[1,4,2048,80]{3,2,1,0:T(8,128)(2,1)S(1)}, bf16[1,4,2048,80]{3,2,1,0:T(8,128)(2,1)}, u32[]{:S(2)}) copy-start(bf16[1,4,2048,80]{3,2,1,0:T(8,128)(2,1)} %get-tuple-element.67) | copy-start | bytes 3932164
  150.2 42.8 %all-to-all-start = ((bf16[4,2048,80]{2,0,1:T(4,128)(2,1)}), bf16[4,2048,80]{2,0,1:T(4,128)(2,1)S(1)}, u32[]{:S(2)}, u32[]{:S(2)}) async-start(bf16[4,2048,80]{2,0,1:T(4,128)(2,1)} %copy.53), calls=%async_computation | async-start | bytes 4194304 | tf_op jit(solution)/shard_map/all_to_all | solution.py:350
  153.8 42.0 %copy-start.6 = (bf16[512,1280]{1,0:T(8,128)(2,1)S(1)}, bf16[512,1280]{1,0:T(8,128)(2,1)}, u32[]{:S(2)}) copy-start(bf16[512,1280]{1,0:T(8,128)(2,1)} %param.15) | copy-start | bytes 3932164
  153.8 481.7 %reduce-scatter.5.cloned.1.call-start = ((), (), s32[]{:S(2)}) async-start(), calls=%async_computation.8 | async-start | bytes 12288000 | tf_op jit(solution)/shard_map/reduce_scatter | solution.py:436
  265.0 35.0 %all-to-all-start.1 = ((bf16[16,512,80]{1,2,0:T(8,128)(2,1)}), bf16[16,512,80]{1,2,0:T(8,128)(2,1)S(1)}, u32[]{:S(2)}, u32[]{:S(2)}) async-start(bf16[16,512,80]{1,2,0:T(8,128)(2,1)} %fusion.24), calls=%async_computation.1 | async-start | bytes 2621440 | tf_op jit(solution)/shard_map/all_to_all | solution.py:376
  268.6 473.5 %reduce-scatter.3.cloned.1.call-start = ((), (), s32[]{:S(2)}) async-start(), calls=%async_computation.7 | async-start | bytes 6553600 | tf_op jit(solution)/shard_map/reduce_scatter | solution.py:407
  305.6 42.0 %copy-start.27 = (bf16[320,3,1280]{2,0,1:T(8,128)(2,1)S(1)}, bf16[320,3,1280]{2,0,1:T(8,128)(2,1)}, u32[]{:S(2)}) copy-start(bf16[320,3,1280]{2,0,1:T(8,128)(2,1)} %param.21) | copy-start | bytes 7372804
  374.6 439.4 %all-reduce.7.cloned.1.call-start = ((), (), s32[]{:S(2)}) async-start(), calls=%async_computation.9 | async-start | bytes 9830400 | tf_op jit(solution)/shard_map/psum | solution.py:439
  416.6 23.5 %copy-start.38 = (f32[512,1280]{1,0:T(8,128)S(1)}, f32[512,1280]{1,0:T(8,128)}, u32[]{:S(2)}) copy-start(f32[512,1280]{1,0:T(8,128)} %copy-done.37) | copy-start | bytes 7864324
  425.8 28.8 %collective-permute-start = (bf16[2,1024,320]{1,2,0:T(8,128)(2,1)}, bf16[2,1024,320]{1,2,0:T(8,128)(2,1)}, u32[]{:S(2)}, u32[]{:S(2)}) collective-permute-start(bf16[2,1024,320]{1,2,0:T(8,128)(2,1)} %get-tuple-element.76), channel_id=1, source_target_pairs={{0,4},{4,8},{8,12},{12,16},{16,20},{20,24},{24,28},{28,0},{1,5},{5... | collective-permute-start | bytes 3932168 | tf_op jit(solution)/shard_map/ppermute | solution.py:342
  425.8 41.0 %collective-permute-start.1 = (bf16[2,1024,320]{1,2,0:T(8,128)(2,1)}, bf16[2,1024,320]{1,2,0:T(8,128)(2,1)}, u32[]{:S(2)}, u32[]{:S(2)}) collective-permute-start(bf16[2,1024,320]{1,2,0:T(8,128)(2,1)} %get-tuple-element.77), channel_id=1, source_target_pairs={{0,8},{4,12},{8,16},{12,20},{16,24},{20,28},{24,0},{28,4},{1,9},{5... | collective-permute-start | bytes 3932168 | tf_op jit(solution)/shard_map/ppermute | solution.py:342
  433.3 138.0 %collective-permute-start.2 = (bf16[2,1024,320]{1,2,0:T(8,128)(2,1)}, bf16[2,1024,320]{1,2,0:T(8,128)(2,1)}, u32[]{:S(2)}, u32[]{:S(2)}) collective-permute-start(bf16[2,1024,320]{1,2,0:T(8,128)(2,1)} %get-tuple-element.78), channel_id=1, source_target_pairs={{0,12},{4,16},{8,20},{12,24},{16,28},{20,0},{24,4},{28,8},{1,13},{... | collective-permute-start | bytes 3932168 | tf_op jit(solution)/shard_map/ppermute | solution.py:342
  434.2 139.6 %collective-permute-start.3 = (bf16[2,1024,320]{1,2,0:T(8,128)(2,1)}, bf16[2,1024,320]{1,2,0:T(8,128)(2,1)}, u32[]{:S(2)}, u32[]{:S(2)}) collective-permute-start(bf16[2,1024,320]{1,2,0:T(8,128)(2,1)} %get-tuple-element.79), channel_id=1, source_target_pairs={{0,16},{4,20},{8,24},{12,28},{16,0},{20,4},{24,8},{28,12},{1,17},{... | collective-permute-start | bytes 3932168 | tf_op jit(solution)/shard_map/ppermute | solution.py:342
  434.3 142.0 %collective-permute-start.4 = (bf16[2,1024,320]{1,2,0:T(8,128)(2,1)}, bf16[2,1024,320]{1,2,0:T(8,128)(2,1)}, u32[]{:S(2)}, u32[]{:S(2)}) collective-permute-start(bf16[2,1024,320]{1,2,0:T(8,128)(2,1)} %get-tuple-element.80), channel_id=1, source_target_pairs={{0,20},{4,24},{8,28},{12,0},{16,4},{20,8},{24,12},{28,16},{1,21},{... | collective-permute-start | bytes 3932168 | tf_op jit(solution)/shard_map/ppermute | solution.py:342
  444.0 22.8 %copy-start.20 = (bf16[2,1024,320]{1,2,0:T(8,128)(2,1)S(1)}, bf16[2,1024,320]{1,2,0:T(8,128)(2,1)}, u32[]{:S(2)}) copy-start(bf16[2,1024,320]{1,2,0:T(8,128)(2,1)} %get-tuple-element.75) | copy-start | bytes 3932164
  454.5 124.2 %collective-permute-start.5 = (bf16[2,1024,320]{1,2,0:T(8,128)(2,1)}, bf16[2,1024,320]{1,2,0:T(8,128)(2,1)S(1)}, u32[]{:S(2)}, u32[]{:S(2)}) collective-permute-start(bf16[2,1024,320]{1,2,0:T(8,128)(2,1)} %fusion.33), channel_id=1, source_target_pairs={{0,24},{4,28},{8,0},{12,4},{16,8},{20,12},{24,16},{28,20},{1,25},{... | collective-permute-start | bytes 3932168 | tf_op jit(solution)/shard_map/ppermute | solution.py:342
  466.9 132.3 %collective-permute-start.6 = (bf16[2,1024,320]{1,2,0:T(8,128)(2,1)S(1)}, bf16[2,1024,320]{1,2,0:T(8,128)(2,1)S(1)}, u32[]{:S(2)}, u32[]{:S(2)}) collective-permute-start(bf16[2,1024,320]{1,2,0:T(8,128)(2,1)S(1)} %copy-done.20), channel_id=1, source_target_pairs={{0,28},{4,0},{8,4},{12,8},{16,12},{20,16},{24,20},{28,24},{1,29},{... | collective-permute-start | bytes 3932168 | tf_op jit(solution)/shard_map/ppermute | solution.py:342
  640.8 101.3 %copy-start.29 = (f32[1280]{0:T(1024)S(1)}, f32[1280]{0:T(1024)}, u32[]{:S(2)}) copy-start(f32[1280]{0:T(1024)} %copy-done.28) | copy-start | bytes 15364
  (33 other events, 172.8 us)
Sparse Core Ops, SparseCore 0:
  16.9 64.6 all-gather.11
  83.5 44.9 all-gather.5
  130.3 62.9 all-gather.7
  195.0 46.8 all-gather.9
  259.5 112.1 reduce-scatter.4
  374.7 65.5 reduce-scatter.2
  639.6 174.3 all-reduce.6

commit v6 on v4

--- a/solution.py
+++ b/solution.py
@@ -138,81 +138,99 @@
     return block_start.astype(jnp.int32), block_end.astype(jnp.int32), live_row
 
 
-def _window(i, rows):
+def _window(i, rows, width):
     qs = i * TQ
-    ws = jnp.minimum(jnp.maximum(qs - (LMAX - TQ), 0), rows - LMAX)
+    ws = jnp.minimum(jnp.maximum(qs - (width - TQ), 0), rows - width)
     return qs, pl.multiple_of(ws, TQ)
 
 
-def _allowed(qs, ws, s0, e0):
-    a = qs + lax.broadcasted_iota(jnp.int32, (TQ, LMAX), 0)
-    b = ws + lax.broadcasted_iota(jnp.int32, (TQ, LMAX), 1)
+def _allowed(qs, ws, s0, e0, width):
+    a = qs + lax.broadcasted_iota(jnp.int32, (TQ, width), 0)
+    b = ws + lax.broadcasted_iota(jnp.int32, (TQ, width), 1)
     return (b >= s0) & (b <= a) & (b < e0)
+
+
+def _fwd_block(i, s0, e0, q_ref, k_ref, v_ref, o_ref, lse_ref, width):
+    heads, rows = k_ref.shape[0], k_ref.shape[1]
+    qs, ws = _window(i, rows, width)
+    allowed = _allowed(qs, ws, s0, e0, width)
+    for h in range(heads):
+        q = q_ref[h]
+        k = k_ref[h, pl.ds(ws, width), :]
+        v = v_ref[h, pl.ds(ws, width), :]
+        s = lax.dot_general(q, k, (((1,), (1,)), ((), ())), preferred_element_type=jnp.float32)
+        s = jnp.where(allowed, s, masked_score)
+        m = jnp.max(s, axis=1, keepdims=True)
+        p = jnp.exp(s - m)
+        l = jnp.sum(p, axis=1, keepdims=True)
+        probs = (p / l).astype(jnp.bfloat16)
+        o = jnp.dot(probs, v, preferred_element_type=jnp.float32)
+        o_ref[h] = o.astype(o_ref.dtype)
+        lse_ref[h] = m + jnp.log(l)
 
 
 def attn_fwd_kernel(starts_ref, ends_ref, q_ref, k_ref, v_ref, o_ref, lse_ref):
     i = pl.program_id(0)
-    heads, rows = k_ref.shape[0], k_ref.shape[1]
-    qs, ws = _window(i, rows)
     s0 = starts_ref[i]
     e0 = ends_ref[i]
-
-    @pl.when(s0 < e0)
-    def _():
-        allowed = _allowed(qs, ws, s0, e0)
-        for h in range(heads):
-            q = q_ref[h]
-            k = k_ref[h, pl.ds(ws, LMAX), :]
-            v = v_ref[h, pl.ds(ws, LMAX), :]
-            s = lax.dot_general(q, k, (((1,), (1,)), ((), ())), preferred_element_type=jnp.float32)
-            s = jnp.where(allowed, s, masked_score)
-            m = jnp.max(s, axis=1, keepdims=True)
-            p = jnp.exp(s - m)
-            l = jnp.sum(p, axis=1, keepdims=True)
-            probs = (p / l).astype(jnp.bfloat16)
-            o = jnp.dot(probs, v, preferred_element_type=jnp.float32)
-            o_ref[h] = o.astype(o_ref.dtype)
-            lse_ref[h] = m + jnp.log(l)
+    short = i * TQ + TQ - s0 <= LMAX // 2
+
+    @pl.when((s0 < e0) & short)
+    def _():
+        _fwd_block(i, s0, e0, q_ref, k_ref, v_ref, o_ref, lse_ref, LMAX // 2)
+
+    @pl.when((s0 < e0) & jnp.logical_not(short))
+    def _():
+        _fwd_block(i, s0, e0, q_ref, k_ref, v_ref, o_ref, lse_ref, LMAX)
 
     @pl.when(s0 >= e0)
     def _():
         o_ref[...] = jnp.zeros(o_ref.shape, o_ref.dtype)
         lse_ref[...] = jnp.zeros(lse_ref.shape, lse_ref.dtype)
+
+
+def _bwd_block(i, s0, e0, q_ref, k_ref, v_ref, do_ref, lse_ref, dq_ref, dk_acc, dv_acc, width):
+    heads, rows = k_ref.shape[0], k_ref.shape[1]
+    qs, ws = _window(i, rows, width)
+    allowed = _allowed(qs, ws, s0, e0, width)
+    for h in range(heads):
+        q = q_ref[h]
+        k = k_ref[h, pl.ds(ws, width), :]
+        v = v_ref[h, pl.ds(ws, width), :]
+        do = do_ref[h]
+        s = lax.dot_general(q, k, (((1,), (1,)), ((), ())), preferred_element_type=jnp.float32)
+        s = jnp.where(allowed, s, masked_score)
+        probs = jnp.exp(s - lse_ref[h])
+        dp = lax.dot_general(do, v, (((1,), (1,)), ((), ())), preferred_element_type=jnp.float32)
+        row_dot = jnp.sum(probs * dp, axis=1, keepdims=True)
+        ds = (probs * (dp - row_dot)).astype(jnp.bfloat16)
+        dq = jnp.dot(ds, k, preferred_element_type=jnp.float32)
+        dq_ref[h] = dq.astype(dq_ref.dtype)
+        dk_acc[h, pl.ds(ws, width), :] += jnp.dot(ds.T, q, preferred_element_type=jnp.float32)
+        dv_acc[h, pl.ds(ws, width), :] += jnp.dot(
+            probs.astype(jnp.bfloat16).T, do, preferred_element_type=jnp.float32
+        )
 
 
 def attn_bwd_kernel(starts_ref, ends_ref, q_ref, k_ref, v_ref, do_ref, lse_ref,
                     dq_ref, dk_ref, dv_ref, dk_acc, dv_acc):
     i = pl.program_id(0)
-    heads, rows = k_ref.shape[0], k_ref.shape[1]
-    qs, ws = _window(i, rows)
     s0 = starts_ref[i]
     e0 = ends_ref[i]
+    short = i * TQ + TQ - s0 <= LMAX // 2
 
     @pl.when(i == 0)
     def _():
         dk_acc[...] = jnp.zeros(dk_acc.shape, dk_acc.dtype)
         dv_acc[...] = jnp.zeros(dv_acc.shape, dv_acc.dtype)
 
-    @pl.when(s0 < e0)
-    def _():
-        allowed = _allowed(qs, ws, s0, e0)
-        for h in range(heads):
-            q = q_ref[h]
-            k = k_ref[h, pl.ds(ws, LMAX), :]
-            v = v_ref[h, pl.ds(ws, LMAX), :]
-            do = do_ref[h]
-            s = lax.dot_general(q, k, (((1,), (1,)), ((), ())), preferred_element_type=jnp.float32)
-            s = jnp.where(allowed, s, masked_score)
-            probs = jnp.exp(s - lse_ref[h])
-            dp = lax.dot_general(do, v, (((1,), (1,)), ((), ())), preferred_element_type=jnp.float32)
-            row_dot = jnp.sum(probs * dp, axis=1, keepdims=True)
-            ds = (probs * (dp - row_dot)).astype(jnp.bfloat16)
-            dq = jnp.dot(ds, k, preferred_element_type=jnp.float32)
-            dq_ref[h] = dq.astype(dq_ref.dtype)
-            dk_acc[h, pl.ds(ws, LMAX), :] += jnp.dot(ds.T, q, preferred_element_type=jnp.float32)
-            dv_acc[h, pl.ds(ws, LMAX), :] += jnp.dot(
-                probs.astype(jnp.bfloat16).T, do, preferred_element_type=jnp.float32
-            )
+    @pl.when((s0 < e0) & short)
+    def _():
+        _bwd_block(i, s0, e0, q_ref, k_ref, v_ref, do_ref, lse_ref, dq_ref, dk_acc, dv_acc, LMAX // 2)
+
+    @pl.when((s0 < e0) & jnp.logical_not(short))
+    def _():
+        _bwd_block(i, s0, e0, q_ref, k_ref, v_ref, do_ref, lse_ref, dq_ref, dk_acc, dv_acc, LMAX)
 
     @pl.when(s0 >= e0)
     def _():

time: 805 us -> 796 us (0.989)
  Pallas kernels: 72.7 us -> 62.5 us
  transfers between devices with their start and end apart: 16 -> 16, of which waited for: 8 -> 8; matrix products, arithmetic and copies ran while one was open for 22% -> 22% of each run, Pallas kernels for 9% -> 8%
where the time goes in v6:
time: 796 us; the launch traced here: 791 us
  waiting for transfers between devices  329 us (41%)
  blocking collectives  92.8 us (12%)
  other arithmetic  78.5 us (10%)
  local copies, waits for them, and re-layouts  69.9 us (9%)
  matrix products  64.9 us (8%)
  Pallas kernels  62.5 us (8%)
  starting transfers between devices  54.7 us (7%)
  between operations  39.7 us (5%)
    ppermute x7, waiting for transfers between devices, per_device(): lax.ppermute(windows[shift], 'dp', [(r, (r + shift) % groups) for r in ra...  106 us
    psum x1, blocking collectives, per_device(): lax.psum(lax.psum_scatter(small, 'mp', scatter_dimension=0, tiled=True),...  77.8 us
    psum x1, waiting for transfers between devices, per_device(): lax.psum(jnp.concatenate([qkv_part.astype(jnp.bfloat16), shares], axis=1)...  67.6 us
    all_gather x1, waiting for transfers between devices, per_device(): lax.all_gather(jnp.concatenate([tokens, gain_rows]), 'mp', axis=0, tiled=...  61.3 us
    ppermute x7, starting transfers between devices, per_device(): lax.ppermute(windows[shift], 'dp', [(r, (r + shift) % groups) for r in ra...  45.7 us
    all_to_all x1, waiting for transfers between devices, per_device(): lax.all_to_all(att_group, 'mp', split_axis=1, concat_axis=0, tiled=True)  39.5 us
    pallas_call x1, Pallas kernels, attention_backward(): pl.pallas_call(attn_bwd_kernel, grid_spec=pltpu.PrefetchScalarGridSpec(nu...  35.1 us
    pallas_call x1, Pallas kernels, attention_forward(): pl.pallas_call(attn_fwd_kernel, grid_spec=pltpu.PrefetchScalarGridSpec(nu...  27.4 us
  transfers between devices with their start and end apart: 16, of which 8 were waited for; matrix products, arithmetic and copies ran while one was open for 22% of the time, Pallas kernels for 8%

profile of v6, /device:TPU:0, one launch (start us, length us, event | category | flops | bytes accessed | tf_op | source)
XLA Modules:
  0.0 791.4 jit_solution(7545120460733291274)
XLA Ops:
  20.5 61.3 %all-gather.12.cloned.1.call-done = bf16[2080,1280]{1,0:T(8,128)(2,1)} async-done(((bf16[520,1280]{1,0:T(8,128)(2,1)}), bf16[2080,1280]{1,0:T(8,128)(2,1)}) %all-gather.12.cloned.1.call-update) | async-done | bytes 5324816 | tf_op jit(solution)/shard_map/all_gather | solution.py:337
  90.1 11.2 %convolution_bitcast_fusion = f32[3,4,2048,80]{3,2,1,0:T(8,128)} fusion(bf16[2048,1280,1,1]{1,0,2,3:T(8,128)(2,1)S(1)} %bitcast.182, bf16[4,80,3,1280]{3,1,0,2:T(8,128)(2,1)S(1)} %bitcast.167), kind=kOutput, calls=%fused_computation.21 | convolution fusion | flops 5033164800 | bytes 15564800 | tf_op jit(solution)/shard_map/rd,hecd->chre/dot_general | solution.py:346
  103.8 6.9 fusion.64
  110.8 27.4 %shard_map.186 = (bf16[4,2048,80]{2,1,0:T(8,128)(2,1)S(1)}, f32[4,2048,1]{2,1,0:T(8,128)}) custom-call(s32[16]{0:T(128)S(1)} %get-tuple-element.88.starts_ref, s32[16]{0:T(128)S(1)} %get-tuple-element.87.ends_ref, bf16[4,2048,80]{2,1,0:T(8,128)(2,1)S(1)} %multiply_convert_fusion.q_ref, bf16[4,2048,80]{2,1,0:T(8,128)(2,1)} %bitcast.180, ...), custom_call_target="tpu_custom_call" | custom-call | flops 2684354560 | bytes 5242880 | tf_op jit(solution)/shard_map/pallas_call | solution.py:251
  138.6 10.7 %copy.44 = bf16[4,2048,80]{2,0,1:T(4,128)(2,1)} copy(bf16[4,2048,80]{2,1,0:T(8,128)(2,1)S(1)} %broadcast_select_fusion.1) | data formatting | bytes 2621440 | tf_op jit(solution)/shard_map/jit(_where)/select_n | solution.py:366
  153.9 39.5 %all-to-all-done = bf16[4,2048,80]{2,0,1:T(4,128)(2,1)} async-done(((bf16[4,2048,80]{2,0,1:T(4,128)(2,1)}), bf16[4,2048,80]{2,0,1:T(4,128)(2,1)}, u32[]{:S(2)}, u32[]{:S(2)}) %all-to-all-start) | async-done | bytes 1310752 | tf_op jit(solution)/shard_map/all_to_all | solution.py:367
  198.0 6.2 multiply_reduce_fusion.2
  214.7 27.1 %all-gather.10.cloned.1.call-done = bf16[1280,1280]{1,0:T(8,128)(2,1)} async-done(((bf16[320,1280]{1,0:T(8,128)(2,1)}), bf16[1280,1280]{1,0:T(8,128)(2,1)}) %all-gather.10.cloned.1.call-update) | async-done | bytes 3276816 | tf_op jit(solution)/shard_map/all_gather | solution.py:316
  276.9 24.6 %all-to-all-done.1 = bf16[16,512,80]{1,2,0:T(8,128)(2,1)} async-done(((bf16[16,512,80]{1,2,0:T(8,128)(2,1)}), bf16[16,512,80]{1,2,0:T(8,128)(2,1)}, u32[]{:S(2)}, u32[]{:S(2)}) %all-to-all-start.1) | async-done | bytes 1310752 | tf_op jit(solution)/shard_map/all_to_all | solution.py:393
  308.3 35.1 %shard_map.187 = (bf16[4,2048,80]{2,1,0:T(8,128)(2,1)S(1)}, bf16[4,2048,80]{2,1,0:T(8,128)(2,1)S(1)}, bf16[4,2048,80]{2,1,0:T(8,128)(2,1)}) custom-call(s32[16]{0:T(128)S(1)} %get-tuple-element.88.starts_ref, s32[16]{0:T(128)S(1)} %get-tuple-element.87.ends_ref, bf16[4,2048,80]{2,1,0:T(8,128)(2,1)} %copy-done.2, bf16[4,2048,80]{2,1,0:T(8,128)(2,1)} %bitcast.181, ...), custom_call_target="tpu_custom_call" | custom-call | flops 6710886400 | bytes 9175040 | tf_op jit(solution)/shard_map/pallas_call | solution.py:278
  347.8 10.6 %bitcast_convert_fusion = (bf16[2048,1280]{1,0:T(8,128)(2,1)}, f32[2048,1280,1,1]{1,0,3,2:T(8,128)}) fusion(bf16[4,80,3,1280]{3,1,0,2:T(8,128)(2,1)S(1)} %bitcast.168, bf16[1,4,2048,80]{3,2,1,0:T(8,128)(2,1)S(1)} %get-tuple-element.84, bf16[1,4,2048,80]{3,2,1,0:T(8,128)(2,1)S(1)} %get-tuple-element.83, bf16[1,4,2048,80]{3,2,1,0:T(8,128)(2,1)S(1)} %get-tuple-element.78), kind=kOutput, calls=%fused_computation.12 | convolution fusion | flops 5039718400 | bytes 22118400 | tf_op jit(solution)/shard_map/chre,hecd->rd/dot_general | solution.py:418
  397.0 6.4 fusion.40
  403.4 6.6 collective-permute-start.1
  421.6 10.6 %collective-permute-done = bf16[2,1024,320]{1,2,0:T(8,128)(2,1)} collective-permute-done((bf16[2,1024,320]{1,2,0:T(8,128)(2,1)}, bf16[2,1024,320]{1,2,0:T(8,128)(2,1)}, u32[]{:S(2)}, u32[]{:S(2)}) %collective-permute-start) | collective-permute-done | bytes 1310752 | tf_op jit(solution)/shard_map/ppermute | solution.py:358
  432.1 9.8 %collective-permute-start.5 = (bf16[2,1024,320]{1,2,0:T(8,128)(2,1)S(1)}, bf16[2,1024,320]{1,2,0:T(8,128)(2,1)S(1)}, u32[]{:S(2)}, u32[]{:S(2)}) collective-permute-start(bf16[2,1024,320]{1,2,0:T(8,128)(2,1)S(1)} %copy-done.21), channel_id=1, source_target_pairs={{0,24},{4,28},{8,0},{12,4},{16,8},{20,12},{24,16},{28,20},{1,25},{... | collective-permute-start | bytes 3932168 | tf_op jit(solution)/shard_map/ppermute | solution.py:358
  444.4 25.0 %collective-permute-start.6 = (bf16[2,1024,320]{1,2,0:T(8,128)(2,1)S(1)}, bf16[2,1024,320]{1,2,0:T(8,128)(2,1)S(1)}, u32[]{:S(2)}, u32[]{:S(2)}) collective-permute-start(bf16[2,1024,320]{1,2,0:T(8,128)(2,1)S(1)} %copy-done.20), channel_id=1, source_target_pairs={{0,28},{4,0},{8,4},{12,8},{16,12},{20,16},{24,20},{28,24},{1,29},{... | collective-permute-start | bytes 3932168 | tf_op jit(solution)/shard_map/ppermute | solution.py:358
  472.0 76.9 %collective-permute-done.2 = bf16[2,1024,320]{1,2,0:T(8,128)(2,1)} collective-permute-done((bf16[2,1024,320]{1,2,0:T(8,128)(2,1)}, bf16[2,1024,320]{1,2,0:T(8,128)(2,1)}, u32[]{:S(2)}, u32[]{:S(2)}) %collective-permute-start.2) | collective-permute-done | bytes 1310752 | tf_op jit(solution)/shard_map/ppermute | solution.py:358
  557.7 18.9 %collective-permute-done.6 = bf16[2,1024,320]{1,2,0:T(8,128)(2,1)S(1)} collective-permute-done((bf16[2,1024,320]{1,2,0:T(8,128)(2,1)S(1)}, bf16[2,1024,320]{1,2,0:T(8,128)(2,1)S(1)}, u32[]{:S(2)}, u32[]{:S(2)}) %collective-permute-start.6) | collective-permute-done | bytes 1310752 | tf_op jit(solution)/shard_map/ppermute | solution.py:358
  580.9 6.8 fusion.6
  587.7 7.3 fusion.14
  600.2 5.8 fusion.25
  606.1 15.0 %all-reduce.4 = f32[4,720]{1,0:T(4,128)S(1)} all-reduce(f32[4,720]{1,0:T(4,128)S(1)} %maximum_maximum_fusion), channel_id=4, replica_groups=mesh['dp'=8,'mp'=4] {'mp'}, use_global_device_ids=true, to_apply=%region_22.23.clone | all-reduce | flops 2880 | bytes 23040
  621.8 77.8 %psum.14 = f32[1,720]{1,0:T(1,128)S(1)} all-reduce(f32[1,720]{1,0:T(1,128)S(1)} %constant_dynamic-slice_fusion), channel_id=1, replica_groups=mesh['dp'=8,'mp'=4] {'dp'}, use_global_device_ids=true, to_apply=%region_23.24 | all-reduce | flops 720 | bytes 5760 | tf_op jit(solution)/shard_map/psum | solution.py:440
  706.4 67.6 %all-reduce.7.cloned.1.call-done = bf16[320,6,1280]{2,0,1:T(8,128)(2,1)} async-done(((bf16[320,6,1280]{2,0,1:T(8,128)(2,1)}), bf16[320,6,1280]{2,0,1:T(8,128)(2,1)}) %all-reduce.7.cloned.1.call-update) | async-done | bytes 4915216 | tf_op jit(solution)/shard_map/psum | solution.py:453
  (206 shorter events, 156.7 us)
Async XLA Ops:
  7.2 82.9 %copy-start = (bf16[320,3,1280]{2,0,1:T(8,128)(2,1)S(1)}, bf16[320,3,1280]{2,0,1:T(8,128)(2,1)}, u32[]{:S(2)}) copy-start(bf16[320,3,1280]{2,0,1:T(8,128)(2,1)} %param.21) | copy-start | bytes 7372804
  7.2 74.6 %all-gather.12.cloned.1.call-start = ((), (), s32[]{:S(2)}) async-start(), calls=%async_computation.10 | async-start | bytes 6656000 | tf_op jit(solution)/shard_map/all_gather | solution.py:337
  16.9 181.1 %all-gather.6.cloned.1.call-start = ((), (), s32[]{:S(2)}) async-start(), calls=%async_computation.4 | async-start | bytes 4096000 | tf_op jit(solution)/shard_map/all_gather | solution.py:314
  17.7 186.5 %all-gather.8.cloned.1.call-start = ((), (), s32[]{:S(2)}) async-start(), calls=%async_computation.5 | async-start | bytes 4096000 | tf_op jit(solution)/shard_map/all_gather | solution.py:315
  18.4 223.4 %all-gather.10.cloned.1.call-start = ((), (), s32[]{:S(2)}) async-start(), calls=%async_computation.6 | async-start | bytes 4096000 | tf_op jit(solution)/shard_map/all_gather | solution.py:316
  149.3 44.2 %all-to-all-start = ((bf16[4,2048,80]{2,0,1:T(4,128)(2,1)}), bf16[4,2048,80]{2,0,1:T(4,128)(2,1)}, u32[]{:S(2)}, u32[]{:S(2)}) async-start(bf16[4,2048,80]{2,0,1:T(4,128)(2,1)} %copy.44), calls=%async_computation | async-start | bytes 4194304 | tf_op jit(solution)/shard_map/all_to_all | solution.py:367
  153.7 441.3 %reduce-scatter.5.cloned.1.call-start = ((), (), s32[]{:S(2)}) async-start(), calls=%async_computation.8 | async-start | bytes 12288000 | tf_op jit(solution)/shard_map/reduce_scatter | solution.py:450
  265.7 35.8 %all-to-all-start.1 = ((bf16[16,512,80]{1,2,0:T(8,128)(2,1)}), bf16[16,512,80]{1,2,0:T(8,128)(2,1)}, u32[]{:S(2)}, u32[]{:S(2)}) async-start(bf16[16,512,80]{1,2,0:T(8,128)(2,1)} %fusion.30), calls=%async_computation.1 | async-start | bytes 2621440 | tf_op jit(solution)/shard_map/all_to_all | solution.py:393
  270.0 430.7 %reduce-scatter.3.cloned.1.call-start = ((), (), s32[]{:S(2)}) async-start(), calls=%async_computation.7 | async-start | bytes 6553600 | tf_op jit(solution)/shard_map/reduce_scatter | solution.py:421
  358.4 14.6 %copy-start.29 = (u32[32]{0:T(128)S(1)}, u32[32]{0:T(128)}, u32[]{:S(2)}) copy-start(u32[32]{0:T(128)} %constant.234) | copy-start | bytes 388
  358.4 28.9 %copy-start.7 = (bf16[1,4,2048,80]{3,2,1,0:T(8,128)(2,1)S(1)}, bf16[1,4,2048,80]{3,2,1,0:T(8,128)(2,1)}, u32[]{:S(2)}) copy-start(bf16[1,4,2048,80]{3,2,1,0:T(8,128)(2,1)} %get-tuple-element.62) | copy-start | bytes 3932164
  358.4 415.6 %all-reduce.7.cloned.1.call-start = ((), (), s32[]{:S(2)}) async-start(), calls=%async_computation.9 | async-start | bytes 9830400 | tf_op jit(solution)/shard_map/psum | solution.py:453
  397.0 20.6 %copy-start.31 = (f32[512,1280]{1,0:T(8,128)S(1)}, f32[512,1280]{1,0:T(8,128)}, u32[]{:S(2)}) copy-start(f32[512,1280]{1,0:T(8,128)} %copy-done.30) | copy-start | bytes 7864324
  403.4 28.8 %collective-permute-start = (bf16[2,1024,320]{1,2,0:T(8,128)(2,1)}, bf16[2,1024,320]{1,2,0:T(8,128)(2,1)}, u32[]{:S(2)}, u32[]{:S(2)}) collective-permute-start(bf16[2,1024,320]{1,2,0:T(8,128)(2,1)} %get-tuple-element.72), channel_id=1, source_target_pairs={{0,4},{4,8},{8,12},{12,16},{16,20},{20,24},{24,28},{28,0},{1,5},{5... | collective-permute-start | bytes 3932168 | tf_op jit(solution)/shard_map/ppermute | solution.py:358
  403.4 41.0 %collective-permute-start.1 = (bf16[2,1024,320]{1,2,0:T(8,128)(2,1)}, bf16[2,1024,320]{1,2,0:T(8,128)(2,1)}, u32[]{:S(2)}, u32[]{:S(2)}) collective-permute-start(bf16[2,1024,320]{1,2,0:T(8,128)(2,1)} %get-tuple-element.73), channel_id=1, source_target_pairs={{0,8},{4,12},{8,16},{12,20},{16,24},{20,28},{24,0},{28,4},{1,9},{5... | collective-permute-start | bytes 3932168 | tf_op jit(solution)/shard_map/ppermute | solution.py:358
  410.0 138.8 %collective-permute-start.2 = (bf16[2,1024,320]{1,2,0:T(8,128)(2,1)}, bf16[2,1024,320]{1,2,0:T(8,128)(2,1)}, u32[]{:S(2)}, u32[]{:S(2)}) collective-permute-start(bf16[2,1024,320]{1,2,0:T(8,128)(2,1)} %get-tuple-element.74), channel_id=1, source_target_pairs={{0,12},{4,16},{8,20},{12,24},{16,28},{20,0},{24,4},{28,8},{1,13},{... | collective-permute-start | bytes 3932168 | tf_op jit(solution)/shard_map/ppermute | solution.py:358
  411.8 139.7 %collective-permute-start.3 = (bf16[2,1024,320]{1,2,0:T(8,128)(2,1)}, bf16[2,1024,320]{1,2,0:T(8,128)(2,1)}, u32[]{:S(2)}, u32[]{:S(2)}) collective-permute-start(bf16[2,1024,320]{1,2,0:T(8,128)(2,1)} %get-tuple-element.75), channel_id=1, source_target_pairs={{0,16},{4,20},{8,24},{12,28},{16,0},{20,4},{24,8},{28,12},{1,17},{... | collective-permute-start | bytes 3932168 | tf_op jit(solution)/shard_map/ppermute | solution.py:358
  411.8 142.1 %collective-permute-start.4 = (bf16[2,1024,320]{1,2,0:T(8,128)(2,1)}, bf16[2,1024,320]{1,2,0:T(8,128)(2,1)}, u32[]{:S(2)}, u32[]{:S(2)}) collective-permute-start(bf16[2,1024,320]{1,2,0:T(8,128)(2,1)} %get-tuple-element.76), channel_id=1, source_target_pairs={{0,20},{4,24},{8,28},{12,0},{16,4},{20,8},{24,12},{28,16},{1,21},{... | collective-permute-start | bytes 3932168 | tf_op jit(solution)/shard_map/ppermute | solution.py:358
  421.5 23.0 %copy-start.20 = (bf16[2,1024,320]{1,2,0:T(8,128)(2,1)S(1)}, bf16[2,1024,320]{1,2,0:T(8,128)(2,1)}, u32[]{:S(2)}) copy-start(bf16[2,1024,320]{1,2,0:T(8,128)(2,1)} %get-tuple-element.71) | copy-start | bytes 3932164
  432.1 124.4 %collective-permute-start.5 = (bf16[2,1024,320]{1,2,0:T(8,128)(2,1)S(1)}, bf16[2,1024,320]{1,2,0:T(8,128)(2,1)S(1)}, u32[]{:S(2)}, u32[]{:S(2)}) collective-permute-start(bf16[2,1024,320]{1,2,0:T(8,128)(2,1)S(1)} %copy-done.21), channel_id=1, source_target_pairs={{0,24},{4,28},{8,0},{12,4},{16,8},{20,12},{24,16},{28,20},{1,25},{... | collective-permute-start | bytes 3932168 | tf_op jit(solution)/shard_map/ppermute | solution.py:358
  444.4 132.1 %collective-permute-start.6 = (bf16[2,1024,320]{1,2,0:T(8,128)(2,1)S(1)}, bf16[2,1024,320]{1,2,0:T(8,128)(2,1)S(1)}, u32[]{:S(2)}, u32[]{:S(2)}) collective-permute-start(bf16[2,1024,320]{1,2,0:T(8,128)(2,1)S(1)} %copy-done.20), channel_id=1, source_target_pairs={{0,28},{4,0},{8,4},{12,8},{16,12},{20,16},{24,20},{28,24},{1,29},{... | collective-permute-start | bytes 3932168 | tf_op jit(solution)/shard_map/ppermute | solution.py:358
  548.9 32.0 %slice-start = ((s8[5324800]{0:T(1024)(128)(4,1)}), s8[4194304]{0:T(1024)(128)(4,1)S(1)}, s32[]{:S(2)}) async-start(s8[5324800]{0:T(1024)(128)(4,1)} %bitcast.172), calls=%async_computation.11 | async-start | bytes 8388608
  556.5 24.4 %slice-start.1 = ((s8[5324800]{0:T(1024)(128)(4,1)}), s8[1130496]{0:T(1024)(128)(4,1)S(1)}, s32[]{:S(2)}) async-start(s8[5324800]{0:T(1024)(128)(4,1)} %bitcast.172), calls=%async_computation.12 | async-start | bytes 2260992
  600.1 100.6 %copy-start.4 = (bf16[512,1280]{1,0:T(8,128)(2,1)S(1)}, bf16[512,1280]{1,0:T(8,128)(2,1)}, u32[]{:S(2)}) copy-start(bf16[512,1280]{1,0:T(8,128)(2,1)} %param.15) | copy-start | bytes 3932164
  (26 other events, 131.6 us)
Sparse Core Ops, SparseCore 0:
  17.0 64.6 all-gather.11
  83.6 44.9 all-gather.5
  130.4 63.0 all-gather.7
  195.3 46.4 all-gather.9
  259.8 112.1 reduce-scatter.4
  374.9 61.3 reduce-scatter.2
  600.3 173.7 all-reduce.6

commit v7 on v6

--- a/solution.py
+++ b/solution.py
@@ -113,6 +113,21 @@
         inside = (rows >= place_start[q]) & (rows < place_start[q] + place_len[q])
         placed = jnp.where(inside, shifted, placed)
     return placed
+
+
+def pair_then_line_sum(values, axis, count):
+    me = lax.axis_index(axis)
+    half = values.shape[0] // 2
+    pairs = [(r, r ^ 1) for r in range(count)]
+    mine = lax.dynamic_slice_in_dim(values, (me % 2) * half, half, 0)
+    other = lax.dynamic_slice_in_dim(values, (1 - me % 2) * half, half, 0)
+    got = lax.ppermute(other, axis, pairs)
+    part = (mine.astype(jnp.float32) + got.astype(jnp.float32)).astype(values.dtype)
+    lines = [list(range(c, count, 2)) for c in range(2)]
+    summed = lax.psum(part, axis, axis_index_groups=lines)
+    back = lax.ppermute(summed, axis, pairs)
+    even = me % 2 == 0
+    return jnp.concatenate([jnp.where(even, summed, back), jnp.where(even, back, summed)], 0)
 
 
 def dealt_places(lengths, dealing, series_grp, my_group):
@@ -450,8 +465,8 @@
     shares = lax.psum_scatter(
         row_terms.astype(jnp.bfloat16), "mp", scatter_dimension=0, tiled=True
     )
-    totals = lax.psum(
-        jnp.concatenate([qkv_part.astype(jnp.bfloat16), shares], axis=1), "dp"
+    totals = pair_then_line_sum(
+        jnp.concatenate([qkv_part.astype(jnp.bfloat16), shares], axis=1), "dp", lax.axis_size("dp")
     ).astype(jnp.float32)
     return (
         layer_out,

time: 796 us -> 777 us (0.976)
  waiting for transfers between devices: 329 us -> 314 us
  blocking collectives: 92.8 us -> 81 us
  starting transfers between devices: 54.7 us -> 65.8 us
    psum x1, waiting for transfers between devices: 67.6 us -> 0.01 us  [pair_then_line_sum(): summed = lax.psum(part, axis, axis_index_groups=lines)]
    ppermute x7, waiting for transfers between devices: 106 us -> 142 us  [per_device(): lax.ppermute(windows[shift], 'dp', [(r, (r + shift) % groups) for r in ra...]
    psum x1, blocking collectives: 77.8 us -> 65.8 us  [per_device(): lax.psum(lax.psum_scatter(small, 'mp', scatter_dimension=0, tiled=True),...]
    ppermute x0 -> x2, starting transfers between devices: none -> 9.56 us  [the longest x1 9.56 us: pair_then_line_sum(): back = lax.ppermute(summed, axis, pairs)]
    unnamed x77 -> x91, local copies, waits for them, and re-layouts: 20.3 us -> 18.7 us
  transfers between devices with their start and end apart: 16 -> 18, of which waited for: 8 -> 9; matrix products, arithmetic and copies ran while one was open for 22% -> 21% of each run, Pallas kernels for 8% -> 8%
where the time goes in v7:
time: 777 us; the launch traced here: 772 us
  waiting for transfers between devices  314 us (40%)
  blocking collectives  81 us (10%)
  other arithmetic  80 us (10%)
  starting transfers between devices  65.8 us (8%)
  local copies, waits for them, and re-layouts  65.2 us (8%)
  matrix products  63.1 us (8%)
  Pallas kernels  62.3 us (8%)
  between operations  39.9 us (5%)
    ppermute x7, waiting for transfers between devices, per_device(): lax.ppermute(windows[shift], 'dp', [(r, (r + shift) % groups) for r in ra...  142 us
    psum x1, blocking collectives, per_device(): lax.psum(lax.psum_scatter(small, 'mp', scatter_dimension=0, tiled=True),...  65.8 us
    all_gather x1, waiting for transfers between devices, per_device(): lax.all_gather(jnp.concatenate([tokens, gain_rows]), 'mp', axis=0, tiled=...  60.8 us
    ppermute x7, starting transfers between devices, per_device(): lax.ppermute(windows[shift], 'dp', [(r, (r + shift) % groups) for r in ra...  47.2 us
    all_to_all x1, waiting for transfers between devices, per_device(): lax.all_to_all(att_group, 'mp', split_axis=1, concat_axis=0, tiled=True)  39.5 us
    pallas_call x1, Pallas kernels, attention_backward(): pl.pallas_call(attn_bwd_kernel, grid_spec=pltpu.PrefetchScalarGridSpec(nu...  34.9 us
    all_to_all x1, waiting for transfers between devices, per_device(): lax.all_to_all(att_heads_grad, 'mp', split_axis=0, concat_axis=1, tiled=T...  31.4 us
    pallas_call x1, Pallas kernels, attention_forward(): pl.pallas_call(attn_fwd_kernel, grid_spec=pltpu.PrefetchScalarGridSpec(nu...  27.4 us
  transfers between devices with their start and end apart: 18, of which 9 were waited for; matrix products, arithmetic and copies ran while one was open for 21% of the time, Pallas kernels for 8%

profile of v7, /device:TPU:0, one launch (start us, length us, event | category | flops | bytes accessed | tf_op | source)
XLA Modules:
  0.0 771.7 jit_solution(15048948520265405283)
XLA Ops:
  21.0 60.8 %all-gather.12.cloned.1.call-done = bf16[2080,1280]{1,0:T(8,128)(2,1)} async-done(((bf16[520,1280]{1,0:T(8,128)(2,1)}), bf16[2080,1280]{1,0:T(8,128)(2,1)}) %all-gather.12.cloned.1.call-update) | async-done | bytes 5324816 | tf_op jit(solution)/shard_map/all_gather | solution.py:352
  90.1 11.1 %convolution_bitcast_fusion = f32[3,4,2048,80]{3,2,1,0:T(8,128)} fusion(bf16[2048,1280,1,1]{1,0,2,3:T(8,128)(2,1)S(1)} %bitcast.184, bf16[4,80,3,1280]{3,1,0,2:T(8,128)(2,1)S(1)} %bitcast.167), kind=kOutput, calls=%fused_computation.25 | convolution fusion | flops 5033164800 | bytes 15564800 | tf_op jit(solution)/shard_map/rd,hecd->chre/dot_general | solution.py:361
  103.8 6.9 fusion.66
  110.7 27.4 %shard_map.186 = (bf16[4,2048,80]{2,1,0:T(8,128)(2,1)S(1)}, f32[4,2048,1]{2,1,0:T(8,128)}) custom-call(s32[16]{0:T(128)S(1)} %get-tuple-element.90.starts_ref, s32[16]{0:T(128)S(1)} %get-tuple-element.89.ends_ref, bf16[4,2048,80]{2,1,0:T(8,128)(2,1)S(1)} %multiply_convert_fusion.q_ref, bf16[4,2048,80]{2,1,0:T(8,128)(2,1)} %bitcast.182, ...), custom_call_target="tpu_custom_call" | custom-call | flops 2684354560 | bytes 5242880 | tf_op jit(solution)/shard_map/pallas_call | solution.py:266
  138.5 10.7 %copy.44 = bf16[4,2048,80]{2,0,1:T(4,128)(2,1)} copy(bf16[4,2048,80]{2,1,0:T(8,128)(2,1)S(1)} %broadcast_select_fusion.3) | data formatting | bytes 2621440 | tf_op jit(solution)/shard_map/jit(_where)/select_n | solution.py:381
  153.8 39.5 %all-to-all-done = bf16[4,2048,80]{2,0,1:T(4,128)(2,1)} async-done(((bf16[4,2048,80]{2,0,1:T(4,128)(2,1)}), bf16[4,2048,80]{2,0,1:T(4,128)(2,1)}, u32[]{:S(2)}, u32[]{:S(2)}) %all-to-all-start) | async-done | bytes 1310752 | tf_op jit(solution)/shard_map/all_to_all | solution.py:382
  197.9 6.2 multiply_reduce_fusion.2
  214.5 27.3 %all-gather.10.cloned.1.call-done = bf16[1280,1280]{1,0:T(8,128)(2,1)} async-done(((bf16[320,1280]{1,0:T(8,128)(2,1)}), bf16[1280,1280]{1,0:T(8,128)(2,1)}) %all-gather.10.cloned.1.call-update) | async-done | bytes 3276816 | tf_op jit(solution)/shard_map/all_gather | solution.py:331
  260.5 5.7 fusion.32
  270.6 31.4 %all-to-all-done.1 = bf16[16,512,80]{1,2,0:T(8,128)(2,1)} async-done(((bf16[16,512,80]{1,2,0:T(8,128)(2,1)}), bf16[16,512,80]{1,2,0:T(8,128)(2,1)}, u32[]{:S(2)}, u32[]{:S(2)}) %all-to-all-start.1) | async-done | bytes 1310752 | tf_op jit(solution)/shard_map/all_to_all | solution.py:408
  308.9 34.9 %shard_map.187 = (bf16[4,2048,80]{2,1,0:T(8,128)(2,1)S(1)}, bf16[4,2048,80]{2,1,0:T(8,128)(2,1)S(1)}, bf16[4,2048,80]{2,1,0:T(8,128)(2,1)}) custom-call(s32[16]{0:T(128)S(1)} %get-tuple-element.90.starts_ref, s32[16]{0:T(128)S(1)} %get-tuple-element.89.ends_ref, bf16[4,2048,80]{2,1,0:T(8,128)(2,1)} %copy-done.2, bf16[4,2048,80]{2,1,0:T(8,128)(2,1)} %bitcast.183, ...), custom_call_target="tpu_custom_call" | custom-call | flops 6710886400 | bytes 9175040 | tf_op jit(solution)/shard_map/pallas_call | solution.py:293
  347.5 8.8 %bitcast_convert_fusion = (bf16[2048,1280]{1,0:T(8,128)(2,1)}, f32[2048,1280,1,1]{1,0,3,2:T(8,128)S(1)}) fusion(bf16[4,80,3,1280]{3,1,0,2:T(8,128)(2,1)S(1)} %bitcast.168, bf16[1,4,2048,80]{3,2,1,0:T(8,128)(2,1)S(1)} %get-tuple-element.86, bf16[1,4,2048,80]{3,2,1,0:T(8,128)(2,1)S(1)} %get-tuple-element.85, bf16[1,4,2048,80]{3,2,1,0:T(8,128)(2,1)S(1)} %get-tuple-element.80), kind=kOutput, calls=%fused_computation.12 | convolution fusion | flops 5039718400 | bytes 22118400 | tf_op jit(solution)/shard_map/chre,hecd->rd/dot_general | solution.py:433
  359.6 7.3 fusion.14
  366.9 5.9 reduce-scatter.5.cloned.1.call-done
  431.3 6.4 fusion.42
  451.9 44.0 %collective-permute-done = bf16[2,1024,320]{1,2,0:T(8,128)(2,1)} collective-permute-done((bf16[2,1024,320]{1,2,0:T(8,128)(2,1)}, bf16[2,1024,320]{1,2,0:T(8,128)(2,1)}, u32[]{:S(2)}, u32[]{:S(2)}) %collective-permute-start) | collective-permute-done | bytes 1310752 | tf_op jit(solution)/shard_map/ppermute | solution.py:373
  495.9 15.3 %collective-permute-start.5 = (bf16[2,1024,320]{1,2,0:T(8,128)(2,1)S(1)}, bf16[2,1024,320]{1,2,0:T(8,128)(2,1)S(1)}, u32[]{:S(2)}, u32[]{:S(2)}) collective-permute-start(bf16[2,1024,320]{1,2,0:T(8,128)(2,1)S(1)} %copy-done.20), channel_id=1, source_target_pairs={{0,24},{4,28},{8,0},{12,4},{16,8},{20,12},{24,16},{28,20},{1,25},{... | collective-permute-start | bytes 3932168 | tf_op jit(solution)/shard_map/ppermute | solution.py:373
  513.7 25.2 %collective-permute-start.6 = (bf16[2,1024,320]{1,2,0:T(8,128)(2,1)S(1)}, bf16[2,1024,320]{1,2,0:T(8,128)(2,1)S(1)}, u32[]{:S(2)}, u32[]{:S(2)}) collective-permute-start(bf16[2,1024,320]{1,2,0:T(8,128)(2,1)S(1)} %copy-done.19), channel_id=1, source_target_pairs={{0,28},{4,0},{8,4},{12,8},{16,12},{20,16},{24,20},{28,24},{1,29},{... | collective-permute-start | bytes 3932168 | tf_op jit(solution)/shard_map/ppermute | solution.py:373
  541.4 81.4 %collective-permute-done.2 = bf16[2,1024,320]{1,2,0:T(8,128)(2,1)} collective-permute-done((bf16[2,1024,320]{1,2,0:T(8,128)(2,1)}, bf16[2,1024,320]{1,2,0:T(8,128)(2,1)}, u32[]{:S(2)}, u32[]{:S(2)}) %collective-permute-start.2) | collective-permute-done | bytes 1310752 | tf_op jit(solution)/shard_map/ppermute | solution.py:373
  631.5 16.5 %collective-permute-done.6 = bf16[2,1024,320]{1,2,0:T(8,128)(2,1)S(1)} collective-permute-done((bf16[2,1024,320]{1,2,0:T(8,128)(2,1)S(1)}, bf16[2,1024,320]{1,2,0:T(8,128)(2,1)S(1)}, u32[]{:S(2)}, u32[]{:S(2)}) %collective-permute-start.6) | collective-permute-done | bytes 1310752 | tf_op jit(solution)/shard_map/ppermute | solution.py:373
  652.4 9.6 %collective-permute-start.8 = (bf16[160,6,1280]{2,0,1:T(8,128)(2,1)}, bf16[160,6,1280]{2,0,1:T(8,128)(2,1)}, u32[]{:S(2)}, u32[]{:S(2)}) collective-permute-start(bf16[160,6,1280]{2,0,1:T(8,128)(2,1)} %all-reduce.7.cloned.1.call-done), channel_id=1, source_target_pairs={{0,4},{4,0},{8,12},{12,8},{16,20},{20,16},{24,28},{28,24},{1,5},{5... | collective-permute-start | bytes 7372808 | tf_op jit(solution)/shard_map/ppermute | solution.py:128
  662.0 5.7 fusion.25
  667.9 15.2 %all-reduce.4 = f32[4,720]{1,0:T(4,128)S(1)} all-reduce(f32[4,720]{1,0:T(4,128)S(1)} %maximum_maximum_fusion), channel_id=4, replica_groups=mesh['dp'=8,'mp'=4] {'mp'}, use_global_device_ids=true, to_apply=%region_22.23.clone | all-reduce | flops 2880 | bytes 23040
  683.8 65.8 %psum.14 = f32[1,720]{1,0:T(1,128)S(1)} all-reduce(f32[1,720]{1,0:T(1,128)S(1)} %constant_dynamic-slice_fusion), channel_id=1, replica_groups=mesh['dp'=8,'mp'=4] {'dp'}, use_global_device_ids=true, to_apply=%region_23.24 | all-reduce | flops 720 | bytes 5760 | tf_op jit(solution)/shard_map/psum | solution.py:455
  (226 shorter events, 162.9 us)
Async XLA Ops:
  7.2 83.0 %copy-start = (bf16[320,3,1280]{2,0,1:T(8,128)(2,1)S(1)}, bf16[320,3,1280]{2,0,1:T(8,128)(2,1)}, u32[]{:S(2)}) copy-start(bf16[320,3,1280]{2,0,1:T(8,128)(2,1)} %param.21) | copy-start | bytes 7372804
  7.2 74.6 %all-gather.12.cloned.1.call-start = ((), (), s32[]{:S(2)}) async-start(), calls=%async_computation.10 | async-start | bytes 6656000 | tf_op jit(solution)/shard_map/all_gather | solution.py:352
  16.9 181.0 %all-gather.6.cloned.1.call-start = ((), (), s32[]{:S(2)}) async-start(), calls=%async_computation.4 | async-start | bytes 4096000 | tf_op jit(solution)/shard_map/all_gather | solution.py:329
  17.7 186.4 %all-gather.8.cloned.1.call-start = ((), (), s32[]{:S(2)}) async-start(), calls=%async_computation.5 | async-start | bytes 4096000 | tf_op jit(solution)/shard_map/all_gather | solution.py:330
  18.4 223.4 %all-gather.10.cloned.1.call-start = ((), (), s32[]{:S(2)}) async-start(), calls=%async_computation.6 | async-start | bytes 4096000 | tf_op jit(solution)/shard_map/all_gather | solution.py:331
  19.9 65.4 %copy-start.24 = (s32[2]{0:T(128)}, s32[2]{0:T(128)S(1)}, u32[]{:S(2)}) copy-start(s32[2]{0:T(128)S(1)} %multiply_subtract_fusion.1) | copy-start | bytes 28
  149.2 44.2 %all-to-all-start = ((bf16[4,2048,80]{2,0,1:T(4,128)(2,1)}), bf16[4,2048,80]{2,0,1:T(4,128)(2,1)}, u32[]{:S(2)}, u32[]{:S(2)}) async-start(bf16[4,2048,80]{2,0,1:T(4,128)(2,1)} %copy.44), calls=%async_computation | async-start | bytes 4194304 | tf_op jit(solution)/shard_map/all_to_all | solution.py:382
  153.6 219.2 %reduce-scatter.5.cloned.1.call-start = ((), (), s32[]{:S(2)}) async-start(), calls=%async_computation.8 | async-start | bytes 12288000 | tf_op jit(solution)/shard_map/reduce_scatter | solution.py:465
  266.2 35.8 %all-to-all-start.1 = ((bf16[16,512,80]{1,2,0:T(8,128)(2,1)}), bf16[16,512,80]{1,2,0:T(8,128)(2,1)}, u32[]{:S(2)}, u32[]{:S(2)}) async-start(bf16[16,512,80]{1,2,0:T(8,128)(2,1)} %fusion.32), calls=%async_computation.1 | async-start | bytes 2621440 | tf_op jit(solution)/shard_map/all_to_all | solution.py:408
  270.5 381.9 %all-reduce.7.cloned.1.call-start = ((), (), s32[]{:S(2)}) async-start(), calls=%async_computation.9 | async-start | bytes 4915200 | tf_op jit(solution)/shard_map/psum | solution.py:127
  376.2 5.0 collective-permute-start.7
  385.3 365.5 %reduce-scatter.3.cloned.1.call-start = ((), (), s32[]{:S(2)}) async-start(), calls=%async_computation.7 | async-start | bytes 6553600 | tf_op jit(solution)/shard_map/reduce_scatter | solution.py:436
  385.4 36.7 %copy-start.7 = (bf16[1,4,2048,80]{3,2,1,0:T(8,128)(2,1)S(1)}, bf16[1,4,2048,80]{3,2,1,0:T(8,128)(2,1)}, u32[]{:S(2)}) copy-start(bf16[1,4,2048,80]{3,2,1,0:T(8,128)(2,1)} %get-tuple-element.62) | copy-start | bytes 3932164
  437.7 58.2 %collective-permute-start = (bf16[2,1024,320]{1,2,0:T(8,128)(2,1)}, bf16[2,1024,320]{1,2,0:T(8,128)(2,1)}, u32[]{:S(2)}, u32[]{:S(2)}) collective-permute-start(bf16[2,1024,320]{1,2,0:T(8,128)(2,1)} %get-tuple-element.74), channel_id=1, source_target_pairs={{0,4},{4,8},{8,12},{12,16},{16,20},{20,24},{24,28},{28,0},{1,5},{5... | collective-permute-start | bytes 3932168 | tf_op jit(solution)/shard_map/ppermute | solution.py:373
  437.9 75.8 %collective-permute-start.1 = (bf16[2,1024,320]{1,2,0:T(8,128)(2,1)}, bf16[2,1024,320]{1,2,0:T(8,128)(2,1)}, u32[]{:S(2)}, u32[]{:S(2)}) collective-permute-start(bf16[2,1024,320]{1,2,0:T(8,128)(2,1)} %get-tuple-element.75), channel_id=1, source_target_pairs={{0,8},{4,12},{8,16},{12,20},{16,24},{20,28},{24,0},{28,4},{1,9},{5... | collective-permute-start | bytes 3932168 | tf_op jit(solution)/shard_map/ppermute | solution.py:373
  439.4 183.4 %collective-permute-start.2 = (bf16[2,1024,320]{1,2,0:T(8,128)(2,1)}, bf16[2,1024,320]{1,2,0:T(8,128)(2,1)}, u32[]{:S(2)}, u32[]{:S(2)}) collective-permute-start(bf16[2,1024,320]{1,2,0:T(8,128)(2,1)} %get-tuple-element.76), channel_id=1, source_target_pairs={{0,12},{4,16},{8,20},{12,24},{16,28},{20,0},{24,4},{28,8},{1,13},{... | collective-permute-start | bytes 3932168 | tf_op jit(solution)/shard_map/ppermute | solution.py:373
  441.7 183.6 %collective-permute-start.3 = (bf16[2,1024,320]{1,2,0:T(8,128)(2,1)}, bf16[2,1024,320]{1,2,0:T(8,128)(2,1)}, u32[]{:S(2)}, u32[]{:S(2)}) collective-permute-start(bf16[2,1024,320]{1,2,0:T(8,128)(2,1)} %get-tuple-element.77), channel_id=1, source_target_pairs={{0,16},{4,20},{8,24},{12,28},{16,0},{20,4},{24,8},{28,12},{1,17},{... | collective-permute-start | bytes 3932168 | tf_op jit(solution)/shard_map/ppermute | solution.py:373
  443.1 184.7 %collective-permute-start.4 = (bf16[2,1024,320]{1,2,0:T(8,128)(2,1)}, bf16[2,1024,320]{1,2,0:T(8,128)(2,1)}, u32[]{:S(2)}, u32[]{:S(2)}) collective-permute-start(bf16[2,1024,320]{1,2,0:T(8,128)(2,1)} %get-tuple-element.78), channel_id=1, source_target_pairs={{0,20},{4,24},{8,28},{12,0},{16,4},{20,8},{24,12},{28,16},{1,21},{... | collective-permute-start | bytes 3932168 | tf_op jit(solution)/shard_map/ppermute | solution.py:373
  448.6 47.4 %copy-start.20 = (bf16[2,1024,320]{1,2,0:T(8,128)(2,1)S(1)}, bf16[2,1024,320]{1,2,0:T(8,128)(2,1)}, u32[]{:S(2)}) copy-start(bf16[2,1024,320]{1,2,0:T(8,128)(2,1)} %fusion.41) | copy-start | bytes 3932164
  451.9 61.9 %copy-start.19 = (bf16[2,1024,320]{1,2,0:T(8,128)(2,1)S(1)}, bf16[2,1024,320]{1,2,0:T(8,128)(2,1)}, u32[]{:S(2)}) copy-start(bf16[2,1024,320]{1,2,0:T(8,128)(2,1)} %get-tuple-element.73) | copy-start | bytes 3932164
  495.9 134.4 %collective-permute-start.5 = (bf16[2,1024,320]{1,2,0:T(8,128)(2,1)S(1)}, bf16[2,1024,320]{1,2,0:T(8,128)(2,1)S(1)}, u32[]{:S(2)}, u32[]{:S(2)}) collective-permute-start(bf16[2,1024,320]{1,2,0:T(8,128)(2,1)S(1)} %copy-done.20), channel_id=1, source_target_pairs={{0,24},{4,28},{8,0},{12,4},{16,8},{20,12},{24,16},{28,20},{1,25},{... | collective-permute-start | bytes 3932168 | tf_op jit(solution)/shard_map/ppermute | solution.py:373
  513.7 134.3 %collective-permute-start.6 = (bf16[2,1024,320]{1,2,0:T(8,128)(2,1)S(1)}, bf16[2,1024,320]{1,2,0:T(8,128)(2,1)S(1)}, u32[]{:S(2)}, u32[]{:S(2)}) collective-permute-start(bf16[2,1024,320]{1,2,0:T(8,128)(2,1)S(1)} %copy-done.19), channel_id=1, source_target_pairs={{0,28},{4,0},{8,4},{12,8},{16,12},{20,16},{24,20},{28,24},{1,29},{... | collective-permute-start | bytes 3932168 | tf_op jit(solution)/shard_map/ppermute | solution.py:373
  652.4 104.2 %collective-permute-start.8 = (bf16[160,6,1280]{2,0,1:T(8,128)(2,1)}, bf16[160,6,1280]{2,0,1:T(8,128)(2,1)}, u32[]{:S(2)}, u32[]{:S(2)}) collective-permute-start(bf16[160,6,1280]{2,0,1:T(8,128)(2,1)} %all-reduce.7.cloned.1.call-done), channel_id=1, source_target_pairs={{0,4},{4,0},{8,12},{12,8},{16,20},{20,16},{24,28},{28,24},{1,5},{5... | collective-permute-start | bytes 7372808 | tf_op jit(solution)/shard_map/ppermute | solution.py:128
  662.0 88.8 %copy-start.3 = (bf16[512,1280]{1,0:T(8,128)(2,1)S(1)}, bf16[512,1280]{1,0:T(8,128)(2,1)}, u32[]{:S(2)}) copy-start(bf16[512,1280]{1,0:T(8,128)(2,1)} %param.15) | copy-start | bytes 3932164
  (35 other events, 189.3 us)
Sparse Core Ops, SparseCore 0:
  17.0 64.6 all-gather.11
  83.6 44.9 all-gather.5
  130.4 62.9 all-gather.7
  195.2 46.5 all-gather.9
  260.6 112.1 reduce-scatter.4
  385.4 229.2 all-reduce.6
  617.7 58.7 reduce-scatter.2

commit v8 on v6

--- a/solution.py
+++ b/solution.py
@@ -113,6 +113,17 @@
         inside = (rows >= place_start[q]) & (rows < place_start[q] + place_len[q])
         placed = jnp.where(inside, shifted, placed)
     return placed
+
+
+def scatter_sum(partial, axis, count, me):
+    size = partial.shape[0] // count
+    total = lax.dynamic_slice_in_dim(partial, me * size, size, 0).astype(jnp.float32)
+    for shift in range(1, count):
+        piece = lax.dynamic_slice_in_dim(partial, ((me + shift) % count) * size, size, 0)
+        total = total + lax.ppermute(
+            piece, axis, [(r, (r + shift) % count) for r in range(count)]
+        ).astype(jnp.float32)
+    return total
 
 
 def dealt_places(lengths, dealing, series_grp, my_group):
@@ -447,8 +458,8 @@
     in_part = jnp.einsum("ru,rd->ud", preact_grad, normed_two, preferred_element_type=jnp.float32)
     down_part = jnp.einsum("ru,rd->ud", hidden, feed_grad, preferred_element_type=jnp.float32)
     row_terms = jnp.stack([out_part, in_part, down_part], axis=1)
-    shares = lax.psum_scatter(
-        row_terms.astype(jnp.bfloat16), "mp", scatter_dimension=0, tiled=True
+    shares = scatter_sum(row_terms.astype(jnp.bfloat16), "mp", mp_count, my_part).astype(
+        jnp.bfloat16
     )
     totals = lax.psum(
         jnp.concatenate([qkv_part.astype(jnp.bfloat16), shares], axis=1), "dp"

time: 796 us -> 789 us (level)
  waiting for transfers between devices: 329 us -> 320 us
    psum x1, waiting for transfers between devices: 67.6 us -> 0.01 us  [per_device(): lax.psum(jnp.concatenate([qkv_part.astype(jnp.bfloat16), shares], axis=1)...]
    ppermute x7, waiting for transfers between devices: 106 us -> 148 us  [per_device(): lax.ppermute(windows[shift], 'dp', [(r, (r + shift) % groups) for r in ra...]
    ppermute x0 -> x3, waiting for transfers between devices: none -> 40.4 us  [scatter_sum(): lax.ppermute(piece, axis, [(r, (r + shift) % count) for r in range(count)])]
    all_to_all x1, waiting for transfers between devices: 24.6 us -> 1.67 us  [per_device(): lax.all_to_all(att_heads_grad, 'mp', split_axis=0, concat_axis=1, tiled=T...]
    unnamed x77 -> x95, local copies, waits for them, and re-layouts: 20.3 us -> 21.7 us
  transfers between devices with their start and end apart: 16 -> 18, of which waited for: 8 -> 9; matrix products, arithmetic and copies ran while one was open for 22% -> 21% of each run, Pallas kernels for 8% -> 8%
where the time goes in v8:
time: 789 us; the launch traced here: 784 us
  waiting for transfers between devices  320 us (41%)
  blocking collectives  91.4 us (12%)
  local copies, waits for them, and re-layouts  74.6 us (9%)
  other arithmetic  71.7 us (9%)
  matrix products  63.3 us (8%)
  Pallas kernels  62.1 us (8%)
  starting transfers between devices  61.1 us (8%)
  between operations  39.7 us (5%)
    ppermute x7, waiting for transfers between devices, per_device(): lax.ppermute(windows[shift], 'dp', [(r, (r + shift) % groups) for r in ra...  148 us
    psum x1, blocking collectives, per_device(): lax.psum(lax.psum_scatter(small, 'mp', scatter_dimension=0, tiled=True),...  76.1 us
    all_gather x1, waiting for transfers between devices, per_device(): lax.all_gather(jnp.concatenate([tokens, gain_rows]), 'mp', axis=0, tiled=...  60.8 us
    ppermute x7, starting transfers between devices, per_device(): lax.ppermute(windows[shift], 'dp', [(r, (r + shift) % groups) for r in ra...  47.3 us
    ppermute x3, waiting for transfers between devices, scatter_sum(): lax.ppermute(piece, axis, [(r, (r + shift) % count) for r in range(count)])  40.4 us
    all_to_all x1, waiting for transfers between devices, per_device(): lax.all_to_all(att_group, 'mp', split_axis=1, concat_axis=0, tiled=True)  39.5 us
    pallas_call x1, Pallas kernels, attention_backward(): pl.pallas_call(attn_bwd_kernel, grid_spec=pltpu.PrefetchScalarGridSpec(nu...  34.8 us
    pallas_call x1, Pallas kernels, attention_forward(): pl.pallas_call(attn_fwd_kernel, grid_spec=pltpu.PrefetchScalarGridSpec(nu...  27.4 us
  transfers between devices with their start and end apart: 18, of which 9 were waited for; matrix products, arithmetic and copies ran while one was open for 21% of the time, Pallas kernels for 8%

profile of v8, /device:TPU:0, one launch (start us, length us, event | category | flops | bytes accessed | tf_op | source)
XLA Modules:
  0.0 784.3 jit_solution(5671730285030805053)
XLA Ops:
  21.0 60.8 %all-gather.12.cloned.1.call-done = bf16[2080,1280]{1,0:T(8,128)(2,1)} async-done(((bf16[520,1280]{1,0:T(8,128)(2,1)}), bf16[2080,1280]{1,0:T(8,128)(2,1)}) %all-gather.12.cloned.1.call-update) | async-done | bytes 5324816 | tf_op jit(solution)/shard_map/all_gather | solution.py:348
  90.1 11.1 %convolution_bitcast_fusion = f32[3,4,2048,80]{3,2,1,0:T(8,128)} fusion(bf16[2048,1280,1,1]{1,0,2,3:T(8,128)(2,1)S(1)} %bitcast.182, bf16[4,80,3,1280]{3,1,0,2:T(8,128)(2,1)S(1)} %bitcast.167), kind=kOutput, calls=%fused_computation.21 | convolution fusion | flops 5033164800 | bytes 15564800 | tf_op jit(solution)/shard_map/rd,hecd->chre/dot_general | solution.py:357
  103.8 6.9 fusion.64
  110.7 27.4 %shard_map.186 = (bf16[4,2048,80]{2,1,0:T(8,128)(2,1)S(1)}, f32[4,2048,1]{2,1,0:T(8,128)}) custom-call(s32[16]{0:T(128)S(1)} %get-tuple-element.91.starts_ref, s32[16]{0:T(128)S(1)} %get-tuple-element.90.ends_ref, bf16[4,2048,80]{2,1,0:T(8,128)(2,1)S(1)} %multiply_convert_fusion.q_ref, bf16[4,2048,80]{2,1,0:T(8,128)(2,1)} %bitcast.180, ...), custom_call_target="tpu_custom_call" | custom-call | flops 2684354560 | bytes 5242880 | tf_op jit(solution)/shard_map/pallas_call | solution.py:262
  138.5 10.7 %copy.44 = bf16[4,2048,80]{2,0,1:T(4,128)(2,1)} copy(bf16[4,2048,80]{2,1,0:T(8,128)(2,1)S(1)} %broadcast_select_fusion.1) | data formatting | bytes 2621440 | tf_op jit(solution)/shard_map/jit(_where)/select_n | solution.py:377
  153.9 39.5 %all-to-all-done = bf16[4,2048,80]{2,0,1:T(4,128)(2,1)} async-done(((bf16[4,2048,80]{2,0,1:T(4,128)(2,1)}), bf16[4,2048,80]{2,0,1:T(4,128)(2,1)}, u32[]{:S(2)}, u32[]{:S(2)}) %all-to-all-start) | async-done | bytes 1310752 | tf_op jit(solution)/shard_map/all_to_all | solution.py:378
  193.4 4.5 copy.45
  198.0 6.2 multiply_reduce_fusion.2
  204.2 5.1 fusion.63
  214.5 27.3 %all-gather.10.cloned.1.call-done = bf16[1280,1280]{1,0:T(8,128)(2,1)} async-done(((bf16[320,1280]{1,0:T(8,128)(2,1)}), bf16[1280,1280]{1,0:T(8,128)(2,1)}) %all-gather.10.cloned.1.call-update) | async-done | bytes 3276816 | tf_op jit(solution)/shard_map/all_gather | solution.py:327
  241.8 5.5 fusion.20
  287.9 34.8 %shard_map.187 = (bf16[4,2048,80]{2,1,0:T(8,128)(2,1)S(1)}, bf16[4,2048,80]{2,1,0:T(8,128)(2,1)S(1)}, bf16[4,2048,80]{2,1,0:T(8,128)(2,1)}) custom-call(s32[16]{0:T(128)S(1)} %get-tuple-element.91.starts_ref, s32[16]{0:T(128)S(1)} %get-tuple-element.90.ends_ref, bf16[4,2048,80]{2,1,0:T(8,128)(2,1)} %copy-done.2, bf16[4,2048,80]{2,1,0:T(8,128)(2,1)} %bitcast.181, ...), custom_call_target="tpu_custom_call" | custom-call | flops 6710886400 | bytes 9175040 | tf_op jit(solution)/shard_map/pallas_call | solution.py:289
  326.3 8.8 %bitcast_convert_fusion = (bf16[2048,1280]{1,0:T(8,128)(2,1)}, f32[2048,1280,1,1]{1,0,3,2:T(8,128)S(1)}) fusion(bf16[4,80,3,1280]{3,1,0,2:T(8,128)(2,1)S(1)} %bitcast.168, bf16[1,4,2048,80]{3,2,1,0:T(8,128)(2,1)S(1)} %get-tuple-element.87, bf16[1,4,2048,80]{3,2,1,0:T(8,128)(2,1)S(1)} %get-tuple-element.86, bf16[1,4,2048,80]{3,2,1,0:T(8,128)(2,1)S(1)} %get-tuple-element.81), kind=kOutput, calls=%fused_computation.12 | convolution fusion | flops 5039718400 | bytes 22118400 | tf_op jit(solution)/shard_map/chre,hecd->rd/dot_general | solution.py:429
  338.4 6.3 fusion.14
  344.7 40.4 %collective-permute-done.9 = bf16[320,3,1280]{2,0,1:T(8,128)(2,1)} collective-permute-done((bf16[320,3,1280]{2,0,1:T(8,128)(2,1)}, bf16[320,3,1280]{2,0,1:T(8,128)(2,1)}, u32[]{:S(2)}, u32[]{:S(2)}) %collective-permute-start.9) | collective-permute-done | bytes 2457632 | tf_op jit(solution)/shard_map/ppermute | solution.py:123
  385.2 5.1 add_convert_fusion
  433.8 4.7 copy.51
  438.6 6.4 fusion.40
  459.2 37.1 %collective-permute-done = bf16[2,1024,320]{1,2,0:T(8,128)(2,1)} collective-permute-done((bf16[2,1024,320]{1,2,0:T(8,128)(2,1)}, bf16[2,1024,320]{1,2,0:T(8,128)(2,1)}, u32[]{:S(2)}, u32[]{:S(2)}) %collective-permute-start) | collective-permute-done | bytes 1310752 | tf_op jit(solution)/shard_map/ppermute | solution.py:369
  501.2 38.3 %collective-permute-start.6 = (bf16[2,1024,320]{1,2,0:T(8,128)(2,1)S(1)}, bf16[2,1024,320]{1,2,0:T(8,128)(2,1)S(1)}, u32[]{:S(2)}, u32[]{:S(2)}) collective-permute-start(bf16[2,1024,320]{1,2,0:T(8,128)(2,1)S(1)} %copy-done.21), channel_id=1, source_target_pairs={{0,28},{4,0},{8,4},{12,8},{16,12},{20,16},{24,20},{28,24},{1,29},{... | collective-permute-start | bytes 3932168 | tf_op jit(solution)/shard_map/ppermute | solution.py:369
  542.0 76.3 %collective-permute-done.2 = bf16[2,1024,320]{1,2,0:T(8,128)(2,1)} collective-permute-done((bf16[2,1024,320]{1,2,0:T(8,128)(2,1)}, bf16[2,1024,320]{1,2,0:T(8,128)(2,1)}, u32[]{:S(2)}, u32[]{:S(2)}) %collective-permute-start.2) | collective-permute-done | bytes 1310752 | tf_op jit(solution)/shard_map/ppermute | solution.py:369
  627.3 34.6 %collective-permute-done.6 = bf16[2,1024,320]{1,2,0:T(8,128)(2,1)S(1)} collective-permute-done((bf16[2,1024,320]{1,2,0:T(8,128)(2,1)S(1)}, bf16[2,1024,320]{1,2,0:T(8,128)(2,1)S(1)}, u32[]{:S(2)}, u32[]{:S(2)}) %collective-permute-start.6) | collective-permute-done | bytes 1310752 | tf_op jit(solution)/shard_map/ppermute | solution.py:369
  669.7 15.3 %all-reduce.4 = f32[4,720]{1,0:T(4,128)S(1)} all-reduce(f32[4,720]{1,0:T(4,128)S(1)} %maximum_maximum_fusion), channel_id=4, replica_groups=mesh['dp'=8,'mp'=4] {'mp'}, use_global_device_ids=true, to_apply=%region_22.23.clone | all-reduce | flops 2880 | bytes 23040
  685.6 76.1 %psum.14 = f32[1,720]{1,0:T(1,128)S(1)} all-reduce(f32[1,720]{1,0:T(1,128)S(1)} %constant_dynamic-slice_fusion.3), channel_id=1, replica_groups=mesh['dp'=8,'mp'=4] {'dp'}, use_global_device_ids=true, to_apply=%region_23.24 | all-reduce | flops 720 | bytes 5760 | tf_op jit(solution)/shard_map/psum | solution.py:451
  (229 shorter events, 155.3 us)
Async XLA Ops:
  7.2 83.0 %copy-start = (bf16[320,3,1280]{2,0,1:T(8,128)(2,1)S(1)}, bf16[320,3,1280]{2,0,1:T(8,128)(2,1)}, u32[]{:S(2)}) copy-start(bf16[320,3,1280]{2,0,1:T(8,128)(2,1)} %param.21) | copy-start | bytes 7372804
  7.2 74.6 %all-gather.12.cloned.1.call-start = ((), (), s32[]{:S(2)}) async-start(), calls=%async_computation.8 | async-start | bytes 6656000 | tf_op jit(solution)/shard_map/all_gather | solution.py:348
  16.9 181.0 %all-gather.6.cloned.1.call-start = ((), (), s32[]{:S(2)}) async-start(), calls=%async_computation.3 | async-start | bytes 4096000 | tf_op jit(solution)/shard_map/all_gather | solution.py:325
  17.7 186.5 %all-gather.8.cloned.1.call-start = ((), (), s32[]{:S(2)}) async-start(), calls=%async_computation.4 | async-start | bytes 4096000 | tf_op jit(solution)/shard_map/all_gather | solution.py:326
  18.4 223.4 %all-gather.10.cloned.1.call-start = ((), (), s32[]{:S(2)}) async-start(), calls=%async_computation.5 | async-start | bytes 4096000 | tf_op jit(solution)/shard_map/all_gather | solution.py:327
  19.9 65.4 %copy-start.25 = (s32[2]{0:T(128)}, s32[2]{0:T(128)S(1)}, u32[]{:S(2)}) copy-start(s32[2]{0:T(128)S(1)} %multiply_subtract_fusion.1) | copy-start | bytes 28
  149.2 44.2 %all-to-all-start = ((bf16[4,2048,80]{2,0,1:T(4,128)(2,1)}), bf16[4,2048,80]{2,0,1:T(4,128)(2,1)}, u32[]{:S(2)}, u32[]{:S(2)}) async-start(bf16[4,2048,80]{2,0,1:T(4,128)(2,1)} %copy.44), calls=%async_computation | async-start | bytes 4194304 | tf_op jit(solution)/shard_map/all_to_all | solution.py:378
  258.9 22.2 %all-to-all-start.1 = ((bf16[16,512,80]{1,2,0:T(8,128)(2,1)}), bf16[16,512,80]{1,2,0:T(8,128)(2,1)}, u32[]{:S(2)}, u32[]{:S(2)}) async-start(bf16[16,512,80]{1,2,0:T(8,128)(2,1)} %fusion.30), calls=%async_computation.1 | async-start | bytes 2621440 | tf_op jit(solution)/shard_map/all_to_all | solution.py:404
  263.2 499.7 %all-reduce.7.cloned.1.call-start = ((), (), s32[]{:S(2)}) async-start(), calls=%async_computation.7 | async-start | bytes 9830400 | tf_op jit(solution)/shard_map/psum | solution.py:464
  274.5 70.2 %collective-permute-start.7 = (bf16[320,3,1280]{2,0,1:T(8,128)(2,1)}, bf16[320,3,1280]{2,0,1:T(8,128)(2,1)}, u32[]{:S(2)}, u32[]{:S(2)}) collective-permute-start(bf16[320,3,1280]{2,0,1:T(8,128)(2,1)} %get-tuple-element.69), channel_id=1, source_target_pairs={{0,1},{1,2},{2,3},{3,0},{4,5},{5,6},{6,7},{7,4},{8,9},{9,10},{10,1... | collective-permute-start | bytes 7372808 | tf_op jit(solution)/shard_map/ppermute | solution.py:123
  276.4 108.7 %collective-permute-start.9 = (bf16[320,3,1280]{2,0,1:T(8,128)(2,1)}, bf16[320,3,1280]{2,0,1:T(8,128)(2,1)}, u32[]{:S(2)}, u32[]{:S(2)}) collective-permute-start(bf16[320,3,1280]{2,0,1:T(8,128)(2,1)} %get-tuple-element.70), channel_id=1, source_target_pairs={{0,3},{1,0},{2,1},{3,2},{4,7},{5,4},{6,5},{7,6},{8,11},{9,8},{10,9... | collective-permute-start | bytes 7372808 | tf_op jit(solution)/shard_map/ppermute | solution.py:123
  277.4 107.7 %collective-permute-start.8 = (bf16[320,3,1280]{2,0,1:T(8,128)(2,1)}, bf16[320,3,1280]{2,0,1:T(8,128)(2,1)}, u32[]{:S(2)}, u32[]{:S(2)}) collective-permute-start(bf16[320,3,1280]{2,0,1:T(8,128)(2,1)} %get-tuple-element.71), channel_id=1, source_target_pairs={{0,2},{1,3},{2,0},{3,1},{4,6},{5,7},{6,4},{7,5},{8,10},{9,11},{10,... | collective-permute-start | bytes 7372808 | tf_op jit(solution)/shard_map/ppermute | solution.py:123
  392.9 377.7 %reduce-scatter.2.cloned.1.call-start = ((), (), s32[]{:S(2)}) async-start(), calls=%async_computation.6 | async-start | bytes 6553600 | tf_op jit(solution)/shard_map/reduce_scatter | solution.py:432
  393.1 22.1 %copy-start.38 = (u32[32]{0:T(128)S(1)}, u32[32]{0:T(128)}, u32[]{:S(2)}) copy-start(u32[32]{0:T(128)} %constant.252) | copy-start | bytes 388
  393.1 36.2 %copy-start.8 = (bf16[1,4,2048,80]{3,2,1,0:T(8,128)(2,1)S(1)}, bf16[1,4,2048,80]{3,2,1,0:T(8,128)(2,1)}, u32[]{:S(2)}) copy-start(bf16[1,4,2048,80]{3,2,1,0:T(8,128)(2,1)} %get-tuple-element.62) | copy-start | bytes 3932164
  445.0 51.3 %collective-permute-start = (bf16[2,1024,320]{1,2,0:T(8,128)(2,1)}, bf16[2,1024,320]{1,2,0:T(8,128)(2,1)}, u32[]{:S(2)}, u32[]{:S(2)}) collective-permute-start(bf16[2,1024,320]{1,2,0:T(8,128)(2,1)} %get-tuple-element.75), channel_id=1, source_target_pairs={{0,4},{4,8},{8,12},{12,16},{16,20},{20,24},{24,28},{28,0},{1,5},{5... | collective-permute-start | bytes 3932168 | tf_op jit(solution)/shard_map/ppermute | solution.py:369
  445.0 56.3 %collective-permute-start.1 = (bf16[2,1024,320]{1,2,0:T(8,128)(2,1)}, bf16[2,1024,320]{1,2,0:T(8,128)(2,1)}, u32[]{:S(2)}, u32[]{:S(2)}) collective-permute-start(bf16[2,1024,320]{1,2,0:T(8,128)(2,1)} %get-tuple-element.76), channel_id=1, source_target_pairs={{0,8},{4,12},{8,16},{12,20},{16,24},{20,28},{24,0},{28,4},{1,9},{5... | collective-permute-start | bytes 3932168 | tf_op jit(solution)/shard_map/ppermute | solution.py:369
  446.6 171.8 %collective-permute-start.2 = (bf16[2,1024,320]{1,2,0:T(8,128)(2,1)}, bf16[2,1024,320]{1,2,0:T(8,128)(2,1)}, u32[]{:S(2)}, u32[]{:S(2)}) collective-permute-start(bf16[2,1024,320]{1,2,0:T(8,128)(2,1)} %get-tuple-element.77), channel_id=1, source_target_pairs={{0,12},{4,16},{8,20},{12,24},{16,28},{20,0},{24,4},{28,8},{1,13},{... | collective-permute-start | bytes 3932168 | tf_op jit(solution)/shard_map/ppermute | solution.py:369
  448.9 171.9 %collective-permute-start.3 = (bf16[2,1024,320]{1,2,0:T(8,128)(2,1)}, bf16[2,1024,320]{1,2,0:T(8,128)(2,1)}, u32[]{:S(2)}, u32[]{:S(2)}) collective-permute-start(bf16[2,1024,320]{1,2,0:T(8,128)(2,1)} %get-tuple-element.78), channel_id=1, source_target_pairs={{0,16},{4,20},{8,24},{12,28},{16,0},{20,4},{24,8},{28,12},{1,17},{... | collective-permute-start | bytes 3932168 | tf_op jit(solution)/shard_map/ppermute | solution.py:369
  450.3 173.0 %collective-permute-start.4 = (bf16[2,1024,320]{1,2,0:T(8,128)(2,1)}, bf16[2,1024,320]{1,2,0:T(8,128)(2,1)}, u32[]{:S(2)}, u32[]{:S(2)}) collective-permute-start(bf16[2,1024,320]{1,2,0:T(8,128)(2,1)} %get-tuple-element.79), channel_id=1, source_target_pairs={{0,20},{4,24},{8,28},{12,0},{16,4},{20,8},{24,12},{28,16},{1,21},{... | collective-permute-start | bytes 3932168 | tf_op jit(solution)/shard_map/ppermute | solution.py:369
  455.8 40.5 %copy-start.22 = (bf16[2,1024,320]{1,2,0:T(8,128)(2,1)S(1)}, bf16[2,1024,320]{1,2,0:T(8,128)(2,1)}, u32[]{:S(2)}) copy-start(bf16[2,1024,320]{1,2,0:T(8,128)(2,1)} %fusion.39) | copy-start | bytes 3932164
  459.1 42.1 %copy-start.21 = (bf16[2,1024,320]{1,2,0:T(8,128)(2,1)S(1)}, bf16[2,1024,320]{1,2,0:T(8,128)(2,1)}, u32[]{:S(2)}) copy-start(bf16[2,1024,320]{1,2,0:T(8,128)(2,1)} %get-tuple-element.74) | copy-start | bytes 3932164
  496.3 129.8 %collective-permute-start.5 = (bf16[2,1024,320]{1,2,0:T(8,128)(2,1)S(1)}, bf16[2,1024,320]{1,2,0:T(8,128)(2,1)S(1)}, u32[]{:S(2)}, u32[]{:S(2)}) collective-permute-start(bf16[2,1024,320]{1,2,0:T(8,128)(2,1)S(1)} %copy-done.22), channel_id=1, source_target_pairs={{0,24},{4,28},{8,0},{12,4},{16,8},{20,12},{24,16},{28,20},{1,25},{... | collective-permute-start | bytes 3932168 | tf_op jit(solution)/shard_map/ppermute | solution.py:369
  501.2 160.7 %collective-permute-start.6 = (bf16[2,1024,320]{1,2,0:T(8,128)(2,1)S(1)}, bf16[2,1024,320]{1,2,0:T(8,128)(2,1)S(1)}, u32[]{:S(2)}, u32[]{:S(2)}) collective-permute-start(bf16[2,1024,320]{1,2,0:T(8,128)(2,1)S(1)} %copy-done.21), channel_id=1, source_target_pairs={{0,28},{4,0},{8,4},{12,8},{16,12},{20,16},{24,20},{28,24},{1,29},{... | collective-permute-start | bytes 3932168 | tf_op jit(solution)/shard_map/ppermute | solution.py:369
  (37 other events, 176.3 us)
Sparse Core Ops, SparseCore 0:
  17.0 64.6 all-gather.11
  83.6 44.9 all-gather.5
  130.4 63.0 all-gather.7
  195.3 46.5 all-gather.9
  393.1 271.9 all-reduce.6
  667.9 86.5 reduce-scatter.1

commit v9 on v6

--- a/solution.py
+++ b/solution.py
@@ -310,11 +310,10 @@
     hidden_in,
     hidden_out,
 ):
-    out_all, in_all, down_all = (
-        lax.all_gather(attention_out, "mp", axis=0, tiled=True),
-        lax.all_gather(hidden_in, "mp", axis=0, tiled=True),
-        lax.all_gather(hidden_out, "mp", axis=0, tiled=True),
-    )
+    weights_all = lax.all_gather(
+        jnp.stack([attention_out, hidden_in, hidden_out]), "mp", axis=1, tiled=True
+    )
+    out_all, in_all, down_all = weights_all[0], weights_all[1], weights_all[2]
     row_count = tokens.shape[0]
     mp_count = lax.axis_size("mp")
     my_group = lax.axis_index("dp")

time: 796 us -> 753 us (0.946)
  waiting for transfers between devices: 329 us -> 307 us
  matrix products: 64.9 us -> 52.4 us
    all_gather x3 -> x1, waiting for transfers between devices: 27.2 us -> 0.79 us  [per_device(): lax.all_gather(jnp.stack([attention_out, hidden_in, hidden_out]), 'mp', a...]
  transfers between devices with their start and end apart: 16 -> 14, of which waited for: 8 -> 10; matrix products, arithmetic and copies ran while one was open for 22% -> 19% of each run, Pallas kernels for 8% -> 8%
where the time goes in v9:
time: 753 us; the launch traced here: 742 us
  waiting for transfers between devices  307 us (41%)
  blocking collectives  89.8 us (12%)
  other arithmetic  78.4 us (10%)
  local copies, waits for them, and re-layouts  63.8 us (8%)
  Pallas kernels  62.5 us (8%)
  matrix products  52.4 us (7%)
  starting transfers between devices  48.8 us (6%)
  between operations  39.6 us (5%)
    ppermute x7, waiting for transfers between devices, per_device(): lax.ppermute(windows[shift], 'dp', [(r, (r + shift) % groups) for r in ra...  110 us
    psum x1, blocking collectives, per_device(): lax.psum(lax.psum_scatter(small, 'mp', scatter_dimension=0, tiled=True),...  74.8 us
    psum x1, waiting for transfers between devices, per_device(): lax.psum(jnp.concatenate([qkv_part.astype(jnp.bfloat16), shares], axis=1)...  66.4 us
    all_gather x1, waiting for transfers between devices, per_device(): lax.all_gather(jnp.concatenate([tokens, gain_rows]), 'mp', axis=0, tiled=...  60.2 us
    all_to_all x1, waiting for transfers between devices, per_device(): lax.all_to_all(att_group, 'mp', split_axis=1, concat_axis=0, tiled=True)  47.2 us
    ppermute x7, starting transfers between devices, per_device(): lax.ppermute(windows[shift], 'dp', [(r, (r + shift) % groups) for r in ra...  39.7 us
    pallas_call x1, Pallas kernels, attention_backward(): pl.pallas_call(attn_bwd_kernel, grid_spec=pltpu.PrefetchScalarGridSpec(nu...  35 us
    pallas_call x1, Pallas kernels, attention_forward(): pl.pallas_call(attn_fwd_kernel, grid_spec=pltpu.PrefetchScalarGridSpec(nu...  27.6 us
  transfers between devices with their start and end apart: 14, of which 10 were waited for; matrix products, arithmetic and copies ran while one was open for 19% of the time, Pallas kernels for 8%

profile of v9, /device:TPU:0, one launch (start us, length us, event | category | flops | bytes accessed | tf_op | source)
XLA Modules:
  0.0 742.4 jit_solution(14213804048111268516)
XLA Ops:
  21.6 60.2 %all-gather.6.cloned.1.call-done = bf16[2080,1280]{1,0:T(8,128)(2,1)} async-done(((bf16[520,1280]{1,0:T(8,128)(2,1)}), bf16[2080,1280]{1,0:T(8,128)(2,1)}) %all-gather.6.cloned.1.call-update) | async-done | bytes 5324816 | tf_op jit(solution)/shard_map/all_gather | solution.py:336
  90.1 8.4 %convolution_bitcast_fusion = f32[3,4,2048,80]{3,2,1,0:T(8,128)S(1)} fusion(bf16[2048,1280,1,1]{1,0,2,3:T(8,128)(2,1)S(1)} %bitcast.193, bf16[4,80,3,1280]{3,1,0,2:T(8,128)(2,1)S(1)} %bitcast.176), kind=kOutput, calls=%fused_computation.21 | convolution fusion | flops 5033164800 | bytes 15564800 | tf_op jit(solution)/shard_map/rd,hecd->chre/dot_general | solution.py:345
  103.5 6.8 fusion.65
  110.3 27.6 %shard_map.186 = (bf16[4,2048,80]{2,1,0:T(8,128)(2,1)S(1)}, f32[4,2048,1]{2,1,0:T(8,128)}) custom-call(s32[16]{0:T(128)S(1)} %get-tuple-element.88.starts_ref, s32[16]{0:T(128)S(1)} %get-tuple-element.87.ends_ref, bf16[4,2048,80]{2,1,0:T(8,128)(2,1)S(1)} %multiply_convert_fusion.q_ref, bf16[4,2048,80]{2,1,0:T(8,128)(2,1)} %bitcast.191, ...), custom_call_target="tpu_custom_call" | custom-call | flops 2684354560 | bytes 5242880 | tf_op jit(solution)/shard_map/pallas_call | solution.py:251
  138.3 10.7 %copy.44 = bf16[4,2048,80]{2,0,1:T(4,128)(2,1)} copy(bf16[4,2048,80]{2,1,0:T(8,128)(2,1)S(1)} %broadcast_select_fusion.1) | data formatting | bytes 2621440 | tf_op jit(solution)/shard_map/jit(_where)/select_n | solution.py:365
  153.7 47.2 %all-to-all-done = bf16[4,2048,80]{2,0,1:T(4,128)(2,1)} async-done(((bf16[4,2048,80]{2,0,1:T(4,128)(2,1)}), bf16[4,2048,80]{2,0,1:T(4,128)(2,1)}, u32[]{:S(2)}, u32[]{:S(2)}) %all-to-all-start) | async-done | bytes 1310752 | tf_op jit(solution)/shard_map/all_to_all | solution.py:366
  227.9 4.6 pad_maximum_fusion
  232.5 5.7 fusion.32
  251.7 22.3 %all-to-all-done.1 = bf16[16,512,80]{1,2,0:T(8,128)(2,1)} async-done(((bf16[16,512,80]{1,2,0:T(8,128)(2,1)}), bf16[16,512,80]{1,2,0:T(8,128)(2,1)}, u32[]{:S(2)}, u32[]{:S(2)}) %all-to-all-start.1) | async-done | bytes 1310752 | tf_op jit(solution)/shard_map/all_to_all | solution.py:392
  281.0 35.0 %shard_map.187 = (bf16[4,2048,80]{2,1,0:T(8,128)(2,1)S(1)}, bf16[4,2048,80]{2,1,0:T(8,128)(2,1)S(1)}, bf16[4,2048,80]{2,1,0:T(8,128)(2,1)}) custom-call(s32[16]{0:T(128)S(1)} %get-tuple-element.88.starts_ref, s32[16]{0:T(128)S(1)} %get-tuple-element.87.ends_ref, bf16[4,2048,80]{2,1,0:T(8,128)(2,1)} %copy-done.2, bf16[4,2048,80]{2,1,0:T(8,128)(2,1)} %bitcast.192, ...), custom_call_target="tpu_custom_call" | custom-call | flops 6710886400 | bytes 9175040 | tf_op jit(solution)/shard_map/pallas_call | solution.py:278
  321.0 10.6 %bitcast_convert_fusion = (bf16[2048,1280]{1,0:T(8,128)(2,1)}, f32[2048,1280,1,1]{1,0,3,2:T(8,128)}) fusion(bf16[4,80,3,1280]{3,1,0,2:T(8,128)(2,1)S(1)} %bitcast.177, bf16[1,4,2048,80]{3,2,1,0:T(8,128)(2,1)S(1)} %get-tuple-element.84, bf16[1,4,2048,80]{3,2,1,0:T(8,128)(2,1)S(1)} %get-tuple-element.83, bf16[1,4,2048,80]{3,2,1,0:T(8,128)(2,1)S(1)} %get-tuple-element.78), kind=kOutput, calls=%fused_computation.12 | convolution fusion | flops 5039718400 | bytes 22118400 | tf_op jit(solution)/shard_map/chre,hecd->rd/dot_general | solution.py:417
  340.7 4.5 maximum_bitcast_fusion
  345.3 6.1 copy.51
  351.3 9.1 %fusion.42 = (bf16[2,1024,320]{1,2,0:T(8,128)(2,1)S(1)}, bf16[2,1024,320]{1,2,0:T(8,128)(2,1)}, bf16[2,1024,320]{1,2,0:T(8,128)(2,1)}, bf16[2,1024,320]{1,2,0:T(...) fusion(s32[]{:T(128)S(6)} %select_n.308, bf16[2,2048,320]{1,2,0:T(8,128)(2,1)} %bitcast.184, ...), kind=kLoop, calls=%fused_computation.99 | loop fusion | flops 3932160 | bytes 10491928 | tf_op jit(solution)/shard_map/jit(_where)/select_n | solution.py:100
  361.7 10.8 %collective-permute-start.1 = (bf16[2,1024,320]{1,2,0:T(8,128)(2,1)}, bf16[2,1024,320]{1,2,0:T(8,128)(2,1)}, u32[]{:S(2)}, u32[]{:S(2)}) collective-permute-start(bf16[2,1024,320]{1,2,0:T(8,128)(2,1)} %get-tuple-element.73), channel_id=1, source_target_pairs={{0,8},{4,12},{8,16},{12,20},{16,24},{20,28},{24,0},{28,4},{1,9},{5... | collective-permute-start | bytes 3932168 | tf_op jit(solution)/shard_map/ppermute | solution.py:357
  402.0 23.7 %collective-permute-start.6 = (bf16[2,1024,320]{1,2,0:T(8,128)(2,1)S(1)}, bf16[2,1024,320]{1,2,0:T(8,128)(2,1)S(1)}, u32[]{:S(2)}, u32[]{:S(2)}) collective-permute-start(bf16[2,1024,320]{1,2,0:T(8,128)(2,1)S(1)} %get-tuple-element.71), channel_id=1, source_target_pairs={{0,28},{4,0},{8,4},{12,8},{16,12},{20,16},{24,20},{28,24},{1,29},{... | collective-permute-start | bytes 3932168 | tf_op jit(solution)/shard_map/ppermute | solution.py:357
  427.1 78.7 %collective-permute-done.2 = bf16[2,1024,320]{1,2,0:T(8,128)(2,1)S(1)} collective-permute-done((bf16[2,1024,320]{1,2,0:T(8,128)(2,1)}, bf16[2,1024,320]{1,2,0:T(8,128)(2,1)S(1)}, u32[]{:S(2)}, u32[]{:S(2)}) %collective-permute-start.2) | collective-permute-done | bytes 1310752 | tf_op jit(solution)/shard_map/ppermute | solution.py:357
  506.3 8.0 %collective-permute-done.5 = bf16[2,1024,320]{1,2,0:T(8,128)(2,1)S(1)} collective-permute-done((bf16[2,1024,320]{1,2,0:T(8,128)(2,1)S(1)}, bf16[2,1024,320]{1,2,0:T(8,128)(2,1)S(1)}, u32[]{:S(2)}, u32[]{:S(2)}) %collective-permute-start.5) | collective-permute-done | bytes 1310752 | tf_op jit(solution)/shard_map/ppermute | solution.py:357
  514.4 21.0 %collective-permute-done.6 = bf16[2,1024,320]{1,2,0:T(8,128)(2,1)S(1)} collective-permute-done((bf16[2,1024,320]{1,2,0:T(8,128)(2,1)S(1)}, bf16[2,1024,320]{1,2,0:T(8,128)(2,1)S(1)}, u32[]{:S(2)}, u32[]{:S(2)}) %collective-permute-start.6) | collective-permute-done | bytes 1310752 | tf_op jit(solution)/shard_map/ppermute | solution.py:357
  543.9 6.1 fusion.14
  554.4 6.9 fusion.19
  561.5 15.0 %all-reduce.4 = f32[4,720]{1,0:T(4,128)S(1)} all-reduce(f32[4,720]{1,0:T(4,128)S(1)} %maximum_maximum_fusion), channel_id=4, replica_groups=mesh['dp'=8,'mp'=4] {'mp'}, use_global_device_ids=true, to_apply=%region_22.23.clone | all-reduce | flops 2880 | bytes 23040
  577.2 74.8 %psum.14 = f32[1,720]{1,0:T(1,128)S(1)} all-reduce(f32[1,720]{1,0:T(1,128)S(1)} %constant_dynamic-slice_fusion), channel_id=1, replica_groups=mesh['dp'=8,'mp'=4] {'dp'}, use_global_device_ids=true, to_apply=%region_23.24 | all-reduce | flops 720 | bytes 5760 | tf_op jit(solution)/shard_map/psum | solution.py:439
  658.9 66.4 %all-reduce.7.cloned.1.call-done = bf16[320,6,1280]{2,0,1:T(8,128)(2,1)} async-done(((bf16[320,6,1280]{2,0,1:T(8,128)(2,1)}), bf16[320,6,1280]{2,0,1:T(8,128)(2,1)}) %all-reduce.7.cloned.1.call-update) | async-done | bytes 4915216 | tf_op jit(solution)/shard_map/psum | solution.py:452
  (203 shorter events, 132.6 us)
Async XLA Ops:
  7.2 83.0 %copy-start = (bf16[320,3,1280]{2,0,1:T(8,128)(2,1)S(1)}, bf16[320,3,1280]{2,0,1:T(8,128)(2,1)}, u32[]{:S(2)}) copy-start(bf16[320,3,1280]{2,0,1:T(8,128)(2,1)} %param.21) | copy-start | bytes 7372804
  7.2 9.8 %copy-start.22 = (bf16[320,1280]{1,0:T(8,128)(2,1)S(1)}, bf16[320,1280]{1,0:T(8,128)(2,1)}, u32[]{:S(2)}) copy-start(bf16[320,1280]{1,0:T(8,128)(2,1)} %param.25) | copy-start | bytes 2457604
  7.2 74.6 %all-gather.6.cloned.1.call-start = ((), (), s32[]{:S(2)}) async-start(), calls=%async_computation.8 | async-start | bytes 6656000 | tf_op jit(solution)/shard_map/all_gather | solution.py:336
  16.9 189.3 %all-gather.4.cloned.1.call-start = ((), (), s32[]{:S(2)}) async-start(), calls=%async_computation.4 | async-start | bytes 12288000 | tf_op jit(solution)/shard_map/all_gather | solution.py:313
  149.1 51.9 %all-to-all-start = ((bf16[4,2048,80]{2,0,1:T(4,128)(2,1)}), bf16[4,2048,80]{2,0,1:T(4,128)(2,1)}, u32[]{:S(2)}, u32[]{:S(2)}) async-start(bf16[4,2048,80]{2,0,1:T(4,128)(2,1)} %copy.44), calls=%async_computation | async-start | bytes 4194304 | tf_op jit(solution)/shard_map/all_to_all | solution.py:366
  153.5 396.5 %reduce-scatter.5.cloned.1.call-start = ((), (), s32[]{:S(2)}) async-start(), calls=%async_computation.6 | async-start | bytes 12288000 | tf_op jit(solution)/shard_map/reduce_scatter | solution.py:449
  211.1 14.0 %copy-start.11 = (f32[512,1280]{1,0:T(8,128)}, f32[512,1280]{1,0:T(8,128)S(1)}, u32[]{:S(2)}) copy-start(f32[512,1280]{1,0:T(8,128)S(1)} %get-tuple-element.114) | copy-start | bytes 7864324
  238.2 35.9 %all-to-all-start.1 = ((bf16[16,512,80]{1,2,0:T(8,128)(2,1)}), bf16[16,512,80]{1,2,0:T(8,128)(2,1)}, u32[]{:S(2)}, u32[]{:S(2)}) async-start(bf16[16,512,80]{1,2,0:T(8,128)(2,1)} %fusion.32), calls=%async_computation.1 | async-start | bytes 2621440 | tf_op jit(solution)/shard_map/all_to_all | solution.py:392
  242.5 410.6 %reduce-scatter.3.cloned.1.call-start = ((), (), s32[]{:S(2)}) async-start(), calls=%async_computation.5 | async-start | bytes 6553600 | tf_op jit(solution)/shard_map/reduce_scatter | solution.py:420
  320.3 11.3 %copy-start.14 = (bf16[1,4,2048,80]{3,2,1,0:T(8,128)(2,1)}, bf16[1,4,2048,80]{3,2,1,0:T(8,128)(2,1)S(1)}, u32[]{:S(2)}) copy-start(bf16[1,4,2048,80]{3,2,1,0:T(8,128)(2,1)S(1)} %get-tuple-element.83) | copy-start | bytes 3932164
  320.3 11.3 %copy-start.16 = (bf16[1,4,2048,80]{3,2,1,0:T(8,128)(2,1)}, bf16[1,4,2048,80]{3,2,1,0:T(8,128)(2,1)S(1)}, u32[]{:S(2)}) copy-start(bf16[1,4,2048,80]{3,2,1,0:T(8,128)(2,1)S(1)} %get-tuple-element.84) | copy-start | bytes 3932164
  331.6 393.7 %all-reduce.7.cloned.1.call-start = ((), (), s32[]{:S(2)}) async-start(), calls=%async_computation.7 | async-start | bytes 9830400 | tf_op jit(solution)/shard_map/psum | solution.py:452
  351.3 31.9 %copy-start.27 = (u32[32]{0:T(128)S(1)}, u32[32]{0:T(128)}, u32[]{:S(2)}) copy-start(u32[32]{0:T(128)} %constant.234) | copy-start | bytes 388
  360.4 35.4 %collective-permute-start = (bf16[2,1024,320]{1,2,0:T(8,128)(2,1)}, bf16[2,1024,320]{1,2,0:T(8,128)(2,1)}, u32[]{:S(2)}, u32[]{:S(2)}) collective-permute-start(bf16[2,1024,320]{1,2,0:T(8,128)(2,1)} %get-tuple-element.72), channel_id=1, source_target_pairs={{0,4},{4,8},{8,12},{12,16},{16,20},{20,24},{24,28},{28,0},{1,5},{5... | collective-permute-start | bytes 3932168 | tf_op jit(solution)/shard_map/ppermute | solution.py:357
  361.7 40.3 %collective-permute-start.1 = (bf16[2,1024,320]{1,2,0:T(8,128)(2,1)}, bf16[2,1024,320]{1,2,0:T(8,128)(2,1)}, u32[]{:S(2)}, u32[]{:S(2)}) collective-permute-start(bf16[2,1024,320]{1,2,0:T(8,128)(2,1)} %get-tuple-element.73), channel_id=1, source_target_pairs={{0,8},{4,12},{8,16},{12,20},{16,24},{20,28},{24,0},{28,4},{1,9},{5... | collective-permute-start | bytes 3932168 | tf_op jit(solution)/shard_map/ppermute | solution.py:357
  387.7 118.2 %collective-permute-start.2 = (bf16[2,1024,320]{1,2,0:T(8,128)(2,1)}, bf16[2,1024,320]{1,2,0:T(8,128)(2,1)S(1)}, u32[]{:S(2)}, u32[]{:S(2)}) collective-permute-start(bf16[2,1024,320]{1,2,0:T(8,128)(2,1)} %get-tuple-element.74), channel_id=1, source_target_pairs={{0,12},{4,16},{8,20},{12,24},{16,28},{20,0},{24,4},{28,8},{1,13},{... | collective-permute-start | bytes 3932168 | tf_op jit(solution)/shard_map/ppermute | solution.py:357
  389.1 117.0 %collective-permute-start.3 = (bf16[2,1024,320]{1,2,0:T(8,128)(2,1)}, bf16[2,1024,320]{1,2,0:T(8,128)(2,1)S(1)}, u32[]{:S(2)}, u32[]{:S(2)}) collective-permute-start(bf16[2,1024,320]{1,2,0:T(8,128)(2,1)} %get-tuple-element.75), channel_id=1, source_target_pairs={{0,16},{4,20},{8,24},{12,28},{16,0},{20,4},{24,8},{28,12},{1,17},{... | collective-permute-start | bytes 3932168 | tf_op jit(solution)/shard_map/ppermute | solution.py:357
  389.1 117.0 %collective-permute-start.4 = (bf16[2,1024,320]{1,2,0:T(8,128)(2,1)}, bf16[2,1024,320]{1,2,0:T(8,128)(2,1)S(1)}, u32[]{:S(2)}, u32[]{:S(2)}) collective-permute-start(bf16[2,1024,320]{1,2,0:T(8,128)(2,1)} %get-tuple-element.76), channel_id=1, source_target_pairs={{0,20},{4,24},{8,28},{12,0},{16,4},{20,8},{24,12},{28,16},{1,21},{... | collective-permute-start | bytes 3932168 | tf_op jit(solution)/shard_map/ppermute | solution.py:357
  395.9 118.4 %collective-permute-start.5 = (bf16[2,1024,320]{1,2,0:T(8,128)(2,1)S(1)}, bf16[2,1024,320]{1,2,0:T(8,128)(2,1)S(1)}, u32[]{:S(2)}, u32[]{:S(2)}) collective-permute-start(bf16[2,1024,320]{1,2,0:T(8,128)(2,1)S(1)} %fusion.41), channel_id=1, source_target_pairs={{0,24},{4,28},{8,0},{12,4},{16,8},{20,12},{24,16},{28,20},{1,25},{... | collective-permute-start | bytes 3932168 | tf_op jit(solution)/shard_map/ppermute | solution.py:357
  398.2 142.1 %slice-start.2 = ((s8[10485760]{0:T(1024)(128)(4,1)}), s8[4194304]{0:T(1024)(128)(4,1)S(1)}, s32[]{:S(2)}) async-start(s8[10485760]{0:T(1024)(128)(4,1)} %bitcast.187), calls=%async_computation.11 | async-start | bytes 8388608
  402.0 133.4 %collective-permute-start.6 = (bf16[2,1024,320]{1,2,0:T(8,128)(2,1)S(1)}, bf16[2,1024,320]{1,2,0:T(8,128)(2,1)S(1)}, u32[]{:S(2)}, u32[]{:S(2)}) collective-permute-start(bf16[2,1024,320]{1,2,0:T(8,128)(2,1)S(1)} %get-tuple-element.71), channel_id=1, source_target_pairs={{0,28},{4,0},{8,4},{12,8},{16,12},{20,16},{24,20},{28,24},{1,29},{... | collective-permute-start | bytes 3932168 | tf_op jit(solution)/shard_map/ppermute | solution.py:357
  506.0 34.3 %slice-start.3 = ((s8[10485760]{0:T(1024)(128)(4,1)}), s8[4194304]{0:T(1024)(128)(4,1)S(1)}, s32[]{:S(2)}) async-start(s8[10485760]{0:T(1024)(128)(4,1)} %bitcast.187), calls=%async_computation.12 | async-start | bytes 8388608
  514.3 26.0 %slice-start = ((s8[5324800]{0:T(1024)(128)(4,1)}), s8[4194304]{0:T(1024)(128)(4,1)S(1)}, s32[]{:S(2)}) async-start(s8[5324800]{0:T(1024)(128)(4,1)} %bitcast.181), calls=%async_computation.9 | async-start | bytes 8388608
  554.4 98.7 %copy-start.6 = (bf16[512,1280]{1,0:T(8,128)(2,1)S(1)}, bf16[512,1280]{1,0:T(8,128)(2,1)}, u32[]{:S(2)}) copy-start(bf16[512,1280]{1,0:T(8,128)(2,1)} %param.15) | copy-start | bytes 3932164
  (24 other events, 92.9 us)
Sparse Core Ops, SparseCore 0:
  17.1 64.6 all-gather.5
  84.2 121.9 all-gather.3
  232.6 114.1 reduce-scatter.4
  349.6 61.2 reduce-scatter.2
  554.5 170.7 all-reduce.6
